TPU v7x, 256 devices: a whole 4x4x8 slice. The times are simulated.
256 devices in a mesh: query: 2 (over core), list: 128 (over y, x, z).
Axes of the slice: x: 4, y: 4, z: 8, core: 2. Of those that a mesh axis runs over, the one named last changes fastest.
Arguments:
- queries: float32 [1024, 1024], P(('query', 'list')), may hold values from -0.24 to 0.24
- probes: int32 [1024, 32], P(('query', 'list')), may hold values from 0 to 127, all different within a row; in each aligned block of 4 rows (0 to 3, 4 to 7, ...) at most 2 rows name the same one
- centroids: float32 [128, 1024], replicated, may hold values from -0.15 to 0.15
- codebook: float32 [64, 16, 256], P('query'), may hold values from -0.15 to 0.15
- codes: int32 [128, 64, 512], P('list'), may hold values from 0 to 255
- cell_sizes: int32 [128], P('list'), may hold values from 64 to 512
Outputs:
- scores: float32 [1024, 32, 512], P(('query', 'list'))
Inputs may be any that keep to these rules, and one draw needn't show every extreme that they name: `probes`: each row names 32 different cells; among the rows of one device no cell is named by more than 2 rows.
All inputs are finite; a program needn't handle non-finite values.
Results may differ from a plain program's by a relative error of at most 0.0003.
Values sent between devices are 32-bit elements; how exact they have to be, the bound alone decides.
No kernel may reach another device: no remote copies, remote signals or barrier semaphores. Data moves between devices by JAX's collectives and lax.ppermute only.
A program may use at most 128 MiB of HBM per device.

v0:
```python
import jax
import jax.numpy as jnp
from jax import lax
from jax.sharding import PartitionSpec as P

sub_block = 4


def make_tables(residual, codebook_all, word_norm):
    cross_terms = jnp.einsum(
        "scmd,mdk->scmk", residual, codebook_all, precision=lax.Precision.HIGHEST
    )
    own_norm = jnp.sum(residual * residual, axis=-1)[..., None]
    return own_norm - 2.0 * cross_terms + word_norm[None, None]


def score_levels(level_tables, codes):
    cells_dev, subspaces, capacity = codes.shape
    codewords = level_tables[0].shape[3]
    word_ids = jnp.arange(codewords, dtype=jnp.int32)
    totals = [jnp.zeros(level.shape[:2] + (capacity,), jnp.float32) for level in level_tables]
    for block_index in range(subspaces // sub_block):
        first_sub = block_index * sub_block
        code_part = codes[:, first_sub : first_sub + sub_block, :]
        one_hot = (code_part[:, :, None, :] == word_ids[None, None, :, None]).astype(jnp.float32)
        for level in range(len(level_tables)):
            table_part = level_tables[level][:, :, first_sub : first_sub + sub_block, :]
            totals[level] = totals[level] + jnp.einsum(
                "scmk,cmkv->scv", table_part, one_hot, precision=lax.Precision.HIGHEST
            )
    return totals


def body(queries, probes, centroids, codebook, codes, cell_sizes):
    list_size = lax.axis_size("list")
    query_rows, probe_count = probes.shape
    cells_dev, subspaces, capacity = codes.shape
    cell_count = cells_dev * list_size
    slot_count = max(2, 2 * query_rows * probe_count // cell_count)
    codebook_all = lax.all_gather(codebook, "query", axis=0, tiled=True)
    sub_width = codebook_all.shape[1]
    word_norm = jnp.sum(codebook_all * codebook_all, axis=1)
    flat_cells = probes.reshape(-1)
    pair_count = flat_cells.shape[0]
    pair_order = jnp.arange(pair_count, dtype=jnp.int32)
    earlier_same = (flat_cells[:, None] == flat_cells[None, :]) & (
        pair_order[None, :] < pair_order[:, None]
    )
    slot_rank = jnp.sum(earlier_same.astype(jnp.int32), axis=1)
    owner_query = pair_order // probe_count
    cell_ids = jnp.arange(cell_count, dtype=jnp.int32)
    positions = jnp.arange(capacity, dtype=jnp.int32)
    valid_rows = positions[None, :] < cell_sizes[:, None]
    level_tables = []
    for slot_level in range(slot_count):
        chosen = (flat_cells[:, None] == cell_ids[None, :]) & (slot_rank[:, None] == slot_level)
        filled = jnp.any(chosen, axis=0)
        source = jnp.sum(jnp.where(chosen, owner_query[:, None], 0), axis=0)
        residual = jnp.where(
            filled[:, None], queries[source] - centroids, jnp.zeros_like(centroids)
        )
        tables_now = make_tables(
            residual.reshape(list_size, cells_dev, subspaces, sub_width), codebook_all, word_norm
        )
        arrived = lax.all_to_all(tables_now, "list", split_axis=0, concat_axis=0, tiled=True)
        level_tables.append(arrived)
    level_scores = score_levels(level_tables, codes)
    result = jnp.zeros((pair_count, capacity), jnp.float32)
    for slot_level in range(slot_count):
        scored = jnp.where(
            valid_rows[None], level_scores[slot_level], jnp.zeros_like(level_scores[slot_level])
        )
        returned = lax.all_to_all(scored, "list", split_axis=0, concat_axis=0, tiled=True).reshape(
            cell_count, capacity
        )
        taking = slot_rank == slot_level
        result = jnp.where(taking[:, None], returned[flat_cells], result)
    return result.reshape(query_rows, probe_count, capacity)


def solution(mesh):
    in_specs = (
        P(("query", "list"), None),
        P(("query", "list"), None),
        P(),
        P("query", None, None),
        P("list", None, None),
        P("list"),
    )
    out_specs = P(("query", "list"), None, None)
    return jax.shard_map(body, mesh=mesh, in_specs=in_specs, out_specs=out_specs, check_vma=False)
```

profile of v0, /device:TPU:32, one launch (start us, length us, event | category | flops | bytes accessed | tf_op | source)
XLA Modules:
  0.0 514.0 jit_solution(17842060241017689125)
XLA Ops:
  10.1 1.3 fusion.142
  11.9 14.2 %all-gather.2.cloned.1.call-done = f32[64,16,256]{2,1,0:T(8,128)} async-done(((f32[32,16,256]{2,1,0:T(8,128)}), f32[64,16,256]{2,1,0:T(8,128)}) %all-gather.2.cloned.1.call-update) | async-done | bytes 1048592 | tf_op jit(solution)/shard_map/all_gather | solution.py:40
  26.1 1.4 multiply_reduce_fusion
  27.6 9.3 %fusion.1 = f32[128,1,64,256]{3,0,2,1:T(8,128)S(1)} fusion(f32[64,256]{1,0:T(8,128)S(1)} %multiply_reduce_fusion, f32[128,64]{0,1:T(8,128)S(1)} %bitcast_reduce_fusion.1, f32[128,64,16]{0,2,1:T(8,128)S(1)} %bitcast.328, f32[64,16,256]{2,1,0:T(8,128)} %all-gather.2.cloned.1.call-done), kind=kOutput, calls=%fused_computation.7 | convolution fusion | flops 408944640 | bytes 10059776 | tf_op jit(solution)/shard_map/scmd,mdk->scmk/dot_general | solution.py:10
  36.9 8.3 %copy.59 = f32[128,1,64,256]{3,2,1,0:T(8,128)} copy(f32[128,1,64,256]{3,0,2,1:T(8,128)S(1)} %fusion.1) | data formatting | bytes 16777216 | tf_op jit(solution)/shard_map/add | solution.py:14
  45.1 14.1 %all-to-all-start = ((f32[128,1,64,256]{3,2,1,0:T(8,128)}), f32[128,1,64,256]{3,2,1,0:T(8,128)}, u32[]{:S(2)}, u32[]{:S(2)}) async-start(f32[128,1,64,256]{3,2,1,0:T(8,128)} %copy.59), calls=%async_computation | async-start | bytes 16777216 | tf_op jit(solution)/shard_map/all_to_all | solution.py:65
  60.5 8.1 %fusion = f32[128,1,64,256]{3,0,2,1:T(8,128)S(1)} fusion(f32[128,64]{0,1:T(8,128)S(1)} %bitcast_reduce_fusion, f32[64,256]{1,0:T(8,128)S(1)} %multiply_reduce_fusion, f32[128,64,16]{0,2,1:T(8,128)S(1)} %bitcast.329, f32[64,16,256]{2,1,0:T(8,128)S(1)} %copy-done.2), kind=kOutput, calls=%fused_computation.5 | convolution fusion | flops 408944640 | bytes 10059776 | tf_op jit(solution)/shard_map/scmd,mdk->scmk/dot_general | solution.py:10
  68.6 8.5 %copy.79 = f32[128,1,64,256]{3,2,1,0:T(8,128)} copy(f32[128,1,64,256]{3,0,2,1:T(8,128)S(1)} %fusion) | data formatting | bytes 16777216 | tf_op jit(solution)/shard_map/add | solution.py:14
  77.1 171.0 %all-to-all-done = f32[128,1,64,256]{3,2,1,0:T(8,128)} async-done(((f32[128,1,64,256]{3,2,1,0:T(8,128)}), f32[128,1,64,256]{3,2,1,0:T(8,128)}, u32[]{:S(2)}, u32[]{:S(2)}) %all-to-all-start) | async-done | bytes 8388640 | tf_op jit(solution)/shard_map/all_to_all | solution.py:65
  248.0 7.9 %all-to-all-start.2 = ((f32[128,1,64,256]{3,2,1,0:T(8,128)}), f32[128,1,64,256]{3,2,1,0:T(8,128)}, u32[]{:S(2)}, u32[]{:S(2)}) async-start(f32[128,1,64,256]{3,2,1,0:T(8,128)} %copy.79), calls=%async_computation.2 | async-start | bytes 16777216 | tf_op jit(solution)/shard_map/all_to_all | solution.py:65
  256.6 8.7 %fusion.145 = (f32[128,1,4,256]{3,2,1,0:T(4,128)S(1)}, f32[128,1,4,256]{3,2,1,0:T(4,128)S(1)}, f32[128,1,4,256]{3,2,1,0:T(4,128)S(1)}, f32[128,1,4,256]{3,2,1,0:...) fusion(f32[128,1,64,256]{3,2,1,0:T(8,128)} %all-to-all-done), kind=kLoop, calls=%fused_computation.241 | loop fusion | bytes 16777216 | tf_op jit(solution)/shard_map/slice | solution.py:27
  265.4 2.3 fusion.34
  267.6 2.2 fusion.97
  277.7 1.3 fusion.81
  279.0 1.1 fusion.79
  280.1 1.1 fusion.77
  286.6 155.7 %all-to-all-done.2 = f32[128,1,64,256]{3,2,1,0:T(8,128)} async-done(((f32[128,1,64,256]{3,2,1,0:T(8,128)}), f32[128,1,64,256]{3,2,1,0:T(8,128)}, u32[]{:S(2)}, u32[]{:S(2)}) %all-to-all-start.2) | async-done | bytes 8388640 | tf_op jit(solution)/shard_map/all_to_all | solution.py:65
  442.3 5.5 %all-to-all-start.1 = ((f32[128,1,512]{2,1,0:T(1,128)}), f32[128,1,512]{2,1,0:T(1,128)S(1)}, u32[]{:S(2)}, u32[]{:S(2)}) async-start(f32[128,1,512]{2,1,0:T(1,128)} %copy.76), calls=%async_computation.1 | async-start | bytes 524288 | tf_op jit(solution)/shard_map/all_to_all | solution.py:73
  447.8 9.0 %fusion.144 = (f32[128,1,4,256]{3,2,1,0:T(4,128)S(1)}, f32[128,1,4,256]{3,2,1,0:T(4,128)S(1)}, f32[128,1,4,256]{3,2,1,0:T(4,128)S(1)}, f32[128,1,4,256]{3,2,1,0:...) fusion(f32[128,1,64,256]{3,2,1,0:T(8,128)} %all-to-all-done.2), kind=kLoop, calls=%fused_computation.240 | loop fusion | bytes 16777216 | tf_op jit(solution)/shard_map/slice | solution.py:27
  456.8 2.3 fusion.35
  459.1 2.2 fusion.96
  469.2 1.4 fusion.80
  478.2 13.9 %all-to-all-start.3 = ((f32[128,1,512]{2,1,0:T(1,128)}), f32[128,1,512]{2,1,0:T(1,128)S(1)}, u32[]{:S(2)}, u32[]{:S(2)}) async-start(f32[128,1,512]{2,1,0:T(1,128)} %copy.96), calls=%async_computation.3 | async-start | bytes 524288 | tf_op jit(solution)/shard_map/all_to_all | solution.py:73
  493.1 12.0 %all-to-all-done.3 = f32[128,1,512]{2,1,0:T(1,128)S(1)} async-done(((f32[128,1,512]{2,1,0:T(1,128)}), f32[128,1,512]{2,1,0:T(1,128)S(1)}, u32[]{:S(2)}, u32[]{:S(2)}) %all-to-all-start.3) | async-done | bytes 262176 | tf_op jit(solution)/shard_map/all_to_all | solution.py:73
  (90 shorter events, 36.3 us)
Async XLA Ops:
  6.5 1.9 copy-start
  6.5 19.6 %all-gather.2.cloned.1.call-start = ((), (), s32[]{:S(2)}) async-start(), calls=%async_computation.4 | async-start | bytes 1572864 | tf_op jit(solution)/shard_map/all_gather | solution.py:40
  45.1 202.9 %all-to-all-start = ((f32[128,1,64,256]{3,2,1,0:T(8,128)}), f32[128,1,64,256]{3,2,1,0:T(8,128)}, u32[]{:S(2)}, u32[]{:S(2)}) async-start(f32[128,1,64,256]{3,2,1,0:T(8,128)} %copy.59), calls=%async_computation | async-start | bytes 16777216 | tf_op jit(solution)/shard_map/all_to_all | solution.py:65
  59.3 1.2 copy-start.2
  77.1 179.5 %copy-start.14 = (s32[1,64,512]{2,1,0:T(8,128)S(1)}, s32[1,64,512]{2,1,0:T(8,128)}, u32[]{:S(2)}) copy-start(s32[1,64,512]{2,1,0:T(8,128)} %param.10) | copy-start | bytes 393220
  248.0 194.3 %all-to-all-start.2 = ((f32[128,1,64,256]{3,2,1,0:T(8,128)}), f32[128,1,64,256]{3,2,1,0:T(8,128)}, u32[]{:S(2)}, u32[]{:S(2)}) async-start(f32[128,1,64,256]{3,2,1,0:T(8,128)} %copy.79), calls=%async_computation.2 | async-start | bytes 16777216 | tf_op jit(solution)/shard_map/all_to_all | solution.py:65
  265.3 4.5 copy-start.13
  265.3 5.6 %copy-start.12 = (f32[128,1,4,256]{3,2,1,0:T(4,128)S(1)}, f32[128,1,4,256]{3,2,1,0:T(4,128)}, u32[]{:S(2)}) copy-start(f32[128,1,4,256]{3,2,1,0:T(4,128)} %get-tuple-element.41) | copy-start | bytes 1572868
  265.3 6.8 %copy-start.10 = (f32[128,1,4,256]{3,2,1,0:T(4,128)S(1)}, f32[128,1,4,256]{3,2,1,0:T(4,128)}, u32[]{:S(2)}) copy-start(f32[128,1,4,256]{3,2,1,0:T(4,128)} %get-tuple-element.40) | copy-start | bytes 1572868
  267.6 5.6 %copy-start.8 = (f32[128,1,4,256]{3,2,1,0:T(4,128)S(1)}, f32[128,1,4,256]{3,2,1,0:T(4,128)}, u32[]{:S(2)}) copy-start(f32[128,1,4,256]{3,2,1,0:T(4,128)} %get-tuple-element.39) | copy-start | bytes 1572868
  269.9 4.5 copy-start.7
  442.3 35.9 %all-to-all-start.1 = ((f32[128,1,512]{2,1,0:T(1,128)}), f32[128,1,512]{2,1,0:T(1,128)S(1)}, u32[]{:S(2)}, u32[]{:S(2)}) async-start(f32[128,1,512]{2,1,0:T(1,128)} %copy.76), calls=%async_computation.1 | async-start | bytes 524288 | tf_op jit(solution)/shard_map/all_to_all | solution.py:73
  456.8 4.5 copy-start.11
  456.8 5.7 %copy-start.9 = (f32[128,1,4,256]{3,2,1,0:T(4,128)S(1)}, f32[128,1,4,256]{3,2,1,0:T(4,128)}, u32[]{:S(2)}) copy-start(f32[128,1,4,256]{3,2,1,0:T(4,128)} %get-tuple-element.25) | copy-start | bytes 1572868
  456.8 6.8 %copy-start.6 = (f32[128,1,4,256]{3,2,1,0:T(4,128)S(1)}, f32[128,1,4,256]{3,2,1,0:T(4,128)}, u32[]{:S(2)}) copy-start(f32[128,1,4,256]{3,2,1,0:T(4,128)} %get-tuple-element.24) | copy-start | bytes 1572868
  459.1 5.6 %copy-start.5 = (f32[128,1,4,256]{3,2,1,0:T(4,128)S(1)}, f32[128,1,4,256]{3,2,1,0:T(4,128)}, u32[]{:S(2)}) copy-start(f32[128,1,4,256]{3,2,1,0:T(4,128)} %get-tuple-element.23) | copy-start | bytes 1572868
  461.3 4.5 copy-start.4
  462.5 4.5 copy-start.3
  474.0 18.1 %copy-start.15 = (s32[4,32]{1,0:T(4,128)S(1)}, s32[4,32]{1,0:T(4,128)}, u32[]{:S(2)}) copy-start(s32[4,32]{1,0:T(4,128)} %param.7) | copy-start | bytes 1540
  478.2 27.0 %all-to-all-start.3 = ((f32[128,1,512]{2,1,0:T(1,128)}), f32[128,1,512]{2,1,0:T(1,128)S(1)}, u32[]{:S(2)}, u32[]{:S(2)}) async-start(f32[128,1,512]{2,1,0:T(1,128)} %copy.96), calls=%async_computation.3 | async-start | bytes 524288 | tf_op jit(solution)/shard_map/all_to_all | solution.py:73
  492.4 14.4 %copy-start.1 = (f32[4,1024]{1,0:T(4,128)S(1)}, f32[4,1024]{1,0:T(4,128)}, u32[]{:S(2)}) copy-start(f32[4,1024]{1,0:T(4,128)} %param.6) | copy-start | bytes 49156
Sparse Core Ops, SparseCore 0:
  9.1 16.9 all-gather.1
where the time goes:
time: 523 us; the launch traced here: 514 us
  waiting for transfers between devices  354 us (68%)
  matrix products  57.9 us (11%)
  local copies, waits for them, and re-layouts  41.9 us (8%)
  starting transfers between devices  41.4 us (8%)
  between operations  15 us (3%)
    all_to_all x2, waiting for transfers between devices, body(): lax.all_to_all(tables_now, 'list', split_axis=0, concat_axis=0, tiled=True)  327 us
    dot_general x32, matrix products, score_levels(): jnp.einsum('scmk,cmkv->scv', table_part, one_hot, precision=lax.Precision...  40.6 us
    all_to_all x2, starting transfers between devices, body(): lax.all_to_all(tables_now, 'list', split_axis=0, concat_axis=0, tiled=True)  22 us
    all_to_all x2, starting transfers between devices, body(): lax.all_to_all(scored, 'list', split_axis=0, concat_axis=0, tiled=True)  19.4 us
    slice x2, local copies, waits for them, and re-layouts, score_levels(): table_part = level_tables[level][:, :, first_sub:first_sub + sub_block, :]  17.7 us
    dot_general x2, matrix products, make_tables(): jnp.einsum('scmd,mdk->scmk', residual, codebook_all, precision=lax.Precis...  17.3 us
    add x2, local copies, waits for them, and re-layouts, make_tables(): return own_norm - 2.0 * cross_terms + word_norm[None, None]  16.7 us
    all_gather x1, waiting for transfers between devices, body(): codebook_all = lax.all_gather(codebook, 'query', axis=0, tiled=True)  14.2 us
  transfers between devices with their start and end apart: 5, of which 4 were waited for; matrix products, arithmetic and copies ran while one was open for 16% of the time, Pallas kernels for 0%

commit v1 on v0

v1 whole, which is shorter than its diff:
```python
import jax
import jax.numpy as jnp
from jax import lax
from jax.sharding import PartitionSpec as P

slot_count = 2


def exact_parts(values):
    high = values.astype(jnp.bfloat16)
    rest = values - high.astype(jnp.float32)
    middle = rest.astype(jnp.bfloat16)
    low = (rest - middle.astype(jnp.float32)).astype(jnp.bfloat16)
    return jnp.concatenate([high, middle, low], axis=-1)


def rebuilt_slots(codebook_all, cell_codes):
    subspaces, sub_width, codewords = codebook_all.shape
    capacity = cell_codes.shape[1]
    parts = exact_parts(jnp.transpose(codebook_all, (0, 2, 1)))
    word_ids = jnp.arange(codewords, dtype=jnp.int32)
    one_hot = (cell_codes[:, :, None] == word_ids[None, None, :]).astype(jnp.bfloat16)
    picked = jnp.einsum("mvk,mkd->vmd", one_hot, parts, preferred_element_type=jnp.float32)
    rebuilt = (
        picked[..., :sub_width] + picked[..., sub_width : 2 * sub_width]
    ) + picked[..., 2 * sub_width :]
    return rebuilt.reshape(capacity, subspaces * sub_width)


def body(queries, probes, centroids, codebook, codes, cell_sizes):
    list_size = lax.axis_size("list")
    query_rows, probe_count = probes.shape
    cells_dev, subspaces, capacity = codes.shape
    dim = queries.shape[1]
    cell_count = cells_dev * list_size
    codebook_all = lax.all_gather(codebook, "query", axis=0, tiled=True)

    flat_cells = probes.reshape(-1)
    pair_count = flat_cells.shape[0]
    pair_order = jnp.arange(pair_count, dtype=jnp.int32)
    earlier_same = (flat_cells[:, None] == flat_cells[None, :]) & (
        pair_order[None, :] < pair_order[:, None]
    )
    slot_rank = jnp.sum(earlier_same.astype(jnp.int32), axis=1)
    owner_query = pair_order // probe_count
    cell_ids = jnp.arange(cell_count, dtype=jnp.int32)
    slot_ids = jnp.arange(slot_count, dtype=jnp.int32)
    chosen = (flat_cells[:, None, None] == cell_ids[None, :, None]) & (
        slot_rank[:, None, None] == slot_ids[None, None, :]
    )
    filled = jnp.any(chosen, axis=0)
    source = jnp.sum(jnp.where(chosen, owner_query[:, None, None], 0), axis=0)
    outgoing = jnp.where(filled[..., None], queries[source], jnp.zeros((), jnp.float32))
    outgoing = outgoing.reshape(list_size, cells_dev, slot_count, dim)
    arrived = lax.all_to_all(outgoing, "list", split_axis=0, concat_axis=0, tiled=True)

    first_cell = lax.axis_index("list") * cells_dev
    positions = jnp.arange(capacity, dtype=jnp.int32)
    scored = []
    for local in range(cells_dev):
        centroid = lax.dynamic_slice_in_dim(centroids, first_cell + local, 1, axis=0)
        residual = arrived[:, local].reshape(list_size * slot_count, dim) - centroid
        rebuilt = rebuilt_slots(codebook_all, codes[local])
        own_norm = jnp.sum(residual * residual, axis=1)
        slot_norm = jnp.sum(rebuilt * rebuilt, axis=1)
        cross = jnp.einsum(
            "sf,vf->sv", residual, rebuilt, precision=lax.Precision.HIGHEST
        )
        total = (own_norm[:, None] + slot_norm[None, :]) - 2.0 * cross
        valid = positions < cell_sizes[local]
        total = jnp.where(valid[None, :], total, jnp.zeros((), jnp.float32))
        scored.append(total.reshape(list_size, slot_count, capacity))
    scored = jnp.stack(scored, axis=1)
    returned = lax.all_to_all(scored, "list", split_axis=0, concat_axis=0, tiled=True)
    returned = returned.reshape(cell_count * slot_count, capacity)
    result = returned[flat_cells * slot_count + slot_rank]
    return result.reshape(query_rows, probe_count, capacity)


def solution(mesh):
    in_specs = (
        P(("query", "list"), None),
        P(("query", "list"), None),
        P(),
        P("query", None, None),
        P("list", None, None),
        P("list"),
    )
    out_specs = P(("query", "list"), None, None)
    return jax.shard_map(body, mesh=mesh, in_specs=in_specs, out_specs=out_specs, check_vma=False)
```

time: 523 us -> 103 us (0.20); the launches traced: 514 us -> 103 us
  waiting for transfers between devices: 354 us -> 28.8 us
  matrix products: 57.9 us -> 21 us
  local copies, waits for them, and re-layouts: 41.9 us -> 9.05 us
  starting transfers between devices: 41.4 us -> 22.1 us
    all_to_all x2 -> x1, waiting for transfers between devices: 327 us -> 9.59 us  [body(): lax.all_to_all(outgoing, 'list', split_axis=0, concat_axis=0, tiled=True)]
    dot_general x34 -> x2, matrix products: 57.9 us -> 21 us  [the longest x1 17.8 us: rebuilt_slots(): jnp.einsum('mvk,mkd->vmd', one_hot, parts, preferred_element_type=jnp.flo...]
    slice x2 -> x0, local copies, waits for them, and re-layouts: 17.7 us -> none  [score_levels(): table_part = level_tables[level][:, :, first_sub:first_sub + sub_block, :]]
    add x2 -> x1, local copies, waits for them, and re-layouts: 16.7 us -> 0.13 us  [body(): total = own_norm[:, None] + slot_norm[None, :] - 2.0 * cross]
    all_gather x1, waiting for transfers between devices: 14.2 us -> 0.02 us  [body(): codebook_all = lax.all_gather(codebook, 'query', axis=0, tiled=True)]
    all_to_all x2 -> x1, starting transfers between devices: 19.4 us -> 6.61 us  [body(): lax.all_to_all(scored, 'list', split_axis=0, concat_axis=0, tiled=True)]
    all_to_all x2 -> x1, starting transfers between devices: 22 us -> 15.5 us  [body(): lax.all_to_all(outgoing, 'list', split_axis=0, concat_axis=0, tiled=True)]
    all_to_all x2 -> x1, waiting for transfers between devices: 12 us -> 18.5 us  [body(): lax.all_to_all(scored, 'list', split_axis=0, concat_axis=0, tiled=True)]
  transfers between devices with their start and end apart: 5 -> 3, of which waited for: 4 -> 2; matrix products, arithmetic and copies ran while one was open for 16% -> 25% of each run, Pallas kernels for 0% -> 0%
where the time goes in v1:
time: 103 us
  waiting for transfers between devices  28.8 us (28%)
  starting transfers between devices  22.1 us (21%)
  matrix products  21 us (20%)
  between operations  14.3 us (14%)
  local copies, waits for them, and re-layouts  9.05 us (9%)
  other arithmetic  7.53 us (7%)
    all_to_all x1, waiting for transfers between devices, body(): lax.all_to_all(scored, 'list', split_axis=0, concat_axis=0, tiled=True)  18.5 us
    dot_general x1, matrix products, rebuilt_slots(): jnp.einsum('mvk,mkd->vmd', one_hot, parts, preferred_element_type=jnp.flo...  17.8 us
    all_to_all x1, starting transfers between devices, body(): lax.all_to_all(outgoing, 'list', split_axis=0, concat_axis=0, tiled=True)  15.5 us
    all_to_all x1, waiting for transfers between devices, body(): lax.all_to_all(outgoing, 'list', split_axis=0, concat_axis=0, tiled=True)  9.59 us
    all_to_all x1, starting transfers between devices, body(): lax.all_to_all(scored, 'list', split_axis=0, concat_axis=0, tiled=True)  6.61 us
    dot_general x1, matrix products, body(): jnp.einsum('sf,vf->sv', residual, rebuilt, precision=lax.Precision.HIGHEST)  3.16 us
    sub x1, local copies, waits for them, and re-layouts, body(): residual = arrived[:, local].reshape(list_size * slot_count, dim) - centroid  2.93 us
    reduce_sum x1, other arithmetic, body(): own_norm = jnp.sum(residual * residual, axis=1)  2.81 us
  transfers between devices with their start and end apart: 3, of which 2 were waited for; matrix products, arithmetic and copies ran while one was open for 25% of the time, Pallas kernels for 0%

profile of v1, /device:TPU:32, one launch (start us, length us, event | category | flops | bytes accessed | tf_op | source)
XLA Modules:
  0.0 102.7 jit_solution(5255662182002636953)
XLA Ops:
  6.5 0.7 all-gather.2.cloned.1.call-update
  7.3 0.8 eq.64
  8.0 0.2 convert_reduce_fusion
  8.4 0.1 fusion.11
  8.7 0.1 reshape.151
  8.9 1.0 %gather_fusion = f32[256,1024]{1,0:T(8,128)S(1)} fusion(f32[4,1024]{1,0:T(4,128)S(1)} %copy-done.1, s32[1024]{0:T(1024)S(1)} %pad_clamp_fusion.1), kind=kCustom, calls=%fused_computation | custom fusion | bytes 2098176 | tf_op jit(solution)/shard_map/gather | solution.py:53
  9.9 0.6 gather.9
  10.5 0.1 copy.9
  10.7 1.5 %bitcast_select_fusion = f32[128,1,2,1024]{3,2,1,0:T(2,128)} fusion(f32[128,1,2,1024]{3,2,0,1:T(2,128)S(1)} %gather.9, pred[128,2]{1,0:T(8,128)(4,1)S(1)} %copy.9), kind=kLoop, calls=%fused_computation.19 | loop fusion | flops 262144 | bytes 2097408 | tf_op jit(solution)/shard_map/jit(_where)/select_n | solution.py:53
  12.2 15.5 %all-to-all-start = ((f32[128,1,2,1024]{3,2,1,0:T(2,128)}), f32[128,1,2,1024]{3,2,1,0:T(2,128)}, u32[]{:S(2)}, u32[]{:S(2)}) async-start(f32[128,1,2,1024]{3,2,1,0:T(2,128)} %bitcast_select_fusion), calls=%async_computation | async-start | bytes 2097152 | tf_op jit(solution)/shard_map/all_to_all | solution.py:55
  28.5 1.4 %bitcast_convert_fusion = bf16[64,256,16]{1,2,0:T(8,128)(2,1)S(1)} fusion(f32[64,16,256]{2,1,0:T(8,128)} %all-gather.2.cloned.1.call-done), kind=kLoop, calls=%fused_computation.18 | loop fusion | flops 262144 | bytes 1572864 | tf_op jit(solution)/shard_map/convert_element_type | solution.py:10
  29.8 0.1 copy-done.2
  30.0 0.2 fusion.10
  30.2 17.8 %fusion.2 = f32[512,64,48]{0,2,1:T(8,128)S(1)} fusion(s32[64,512]{1,0:T(8,128)S(1)} %bitcast.38, bf16[64,256,16]{1,2,0:T(8,128)(2,1)S(1)} %get-tuple-element.10, bf16[64,256,16]{1,2,0:T(8,128)(2,1)S(1)} %get-tuple-element.9, bf16[64,256,16]{1,2,0:T(8,128)(2,1)S(1)} %bitcast_convert_fusion), kind=kOutput, calls=%fused_computation.5 | convolution fusion | flops 818413568 | bytes 7995392 | tf_op jit(solution)/shard_map/mvk,mkd->vmd/dot_general | solution.py:23
  48.0 1.1 %multiply_reduce_fusion = (f32[512]{0:T(512)S(1)}, f32[512,64,16]{0,2,1:T(8,128)S(1)}) fusion(f32[512,64,48]{0,2,1:T(8,128)S(1)} %fusion.2), kind=kLoop, calls=%fused_computation.8 | loop fusion | flops 2096640 | bytes 8390656 | tf_op jit(solution)/shard_map/reduce_sum | solution.py:65
  49.1 9.6 %all-to-all-done = f32[128,1,2,1024]{3,2,1,0:T(2,128)} async-done(((f32[128,1,2,1024]{3,2,1,0:T(2,128)}), f32[128,1,2,1024]{3,2,1,0:T(2,128)}, u32[]{:S(2)}, u32[]{:S(2)}) %all-to-all-start) | async-done | bytes 1048608 | tf_op jit(solution)/shard_map/all_to_all | solution.py:55
  58.7 2.8 %multiply_reduce_fusion.1 = (f32[128,2]{1,0:T(8,128)S(1)}, f32[128,1,2,1024]{3,2,1,0:T(2,128)}) fusion(f32[128,1,2,1024]{3,2,1,0:T(2,128)} %all-to-all-done, f32[1024]{0:T(1024)S(1)} %bitcast.37), kind=kLoop, calls=%fused_computation.21 | loop fusion | flops 786176 | bytes 2102272 | tf_op jit(solution)/shard_map/reduce_sum | solution.py:64
  61.5 2.9 %sub.35 = f32[256,1024]{1,0:T(8,128)} reshape(f32[128,1,2,1024]{3,2,1,0:T(2,128)} %get-tuple-element.6) | data formatting | bytes 2097152 | tf_op jit(solution)/shard_map/sub | solution.py:62
  64.6 3.2 %fusion.9 = f32[256,512]{1,0:T(8,128)S(1)} fusion(f32[256,1024]{1,0:T(8,128)} %sub.35, f32[512,1024]{0,1:T(8,128)S(1)} %bitcast.36, f32[512]{0:T(512)S(1)} %get-tuple-element.7, f32[256]{0:T(256)S(1)} %add.68, pred[512]{0:T(512)(128)(4,1)S(1)} %iota_compare_fusion.6), kind=kOutput, calls=%fused_computation.16 | convolution fusion | flops 1611137024 | bytes 3673600 | tf_op jit(solution)/shard_map/sf,vf->sv/dot_general | solution.py:66
  67.7 1.1 %stack_reshape.3 = f32[128,1,2,512]{3,2,0,1:T(2,128)} reshape(f32[256,512]{1,0:T(8,128)S(1)} %fusion.9) | data formatting | bytes 1048576 | tf_op jit(solution)/shard_map/stack;reshape | solution.py:73
  68.8 6.6 %all-to-all-start.1 = ((f32[128,1,2,512]{3,2,1,0:T(2,128)}), f32[128,1,2,512]{3,2,1,0:T(2,128)S(1)}, u32[]{:S(2)}, u32[]{:S(2)}) async-start(f32[128,1,2,512]{3,2,1,0:T(2,128)} %bitcast.8), calls=%async_computation.1 | async-start | bytes 1048576 | tf_op jit(solution)/shard_map/all_to_all | solution.py:74
  75.6 18.5 %all-to-all-done.1 = f32[128,1,2,512]{3,2,1,0:T(2,128)S(1)} async-done(((f32[128,1,2,512]{3,2,1,0:T(2,128)}), f32[128,1,2,512]{3,2,1,0:T(2,128)S(1)}, u32[]{:S(2)}, u32[]{:S(2)}) %all-to-all-start.1) | async-done | bytes 524320 | tf_op jit(solution)/shard_map/all_to_all | solution.py:74
  94.1 0.4 reshape.147
  94.4 1.5 %gather_fusion.1 = f32[128,512]{1,0:T(8,128)} fusion(f32[256,512]{1,0:T(8,128)S(1)} %reshape.147, s32[1024]{0:T(1024)S(1)} %pad_clamp_fusion), kind=kCustom, calls=%fused_computation.1 | custom fusion | bytes 524800 | tf_op jit(solution)/shard_map/gather | solution.py:76
  (25 shorter events, 0.6 us)
Async XLA Ops:
  6.5 21.9 %copy-start = (f32[128,1024]{1,0:T(8,128)S(1)}, f32[128,1024]{1,0:T(8,128)}, u32[]{:S(2)}) copy-start(f32[128,1024]{1,0:T(8,128)} %param.8) | copy-start | bytes 1572868
  6.5 2.3 %copy-start.1 = (f32[4,1024]{1,0:T(4,128)S(1)}, f32[4,1024]{1,0:T(4,128)}, u32[]{:S(2)}) copy-start(f32[4,1024]{1,0:T(4,128)} %param.6) | copy-start | bytes 49156
  6.5 21.9 %all-gather.2.cloned.1.call-start = ((), (), s32[]{:S(2)}) async-start(), calls=%async_computation.2 | async-start | bytes 1572864 | tf_op jit(solution)/shard_map/all_gather | solution.py:36
  12.2 46.5 %all-to-all-start = ((f32[128,1,2,1024]{3,2,1,0:T(2,128)}), f32[128,1,2,1024]{3,2,1,0:T(2,128)}, u32[]{:S(2)}, u32[]{:S(2)}) async-start(f32[128,1,2,1024]{3,2,1,0:T(2,128)} %bitcast_select_fusion), calls=%async_computation | async-start | bytes 2097152 | tf_op jit(solution)/shard_map/all_to_all | solution.py:55
  27.7 2.5 %copy-start.4 = (s32[1,64,512]{2,1,0:T(8,128)S(1)}, s32[1,64,512]{2,1,0:T(8,128)}, u32[]{:S(2)}) copy-start(s32[1,64,512]{2,1,0:T(8,128)} %param.10) | copy-start | bytes 393220
  28.5 1.5 %copy-start.2 = (f32[64,16,256]{2,1,0:T(8,128)S(1)}, f32[64,16,256]{2,1,0:T(8,128)}, u32[]{:S(2)}) copy-start(f32[64,16,256]{2,1,0:T(8,128)} %all-gather.2.cloned.1.call-done) | copy-start | bytes 3145732
  64.6 10.9 %copy-start.3 = (s32[4,32]{1,0:T(4,128)S(1)}, s32[4,32]{1,0:T(4,128)}, u32[]{:S(2)}) copy-start(s32[4,32]{1,0:T(4,128)} %param.7) | copy-start | bytes 1540
  68.8 25.2 %all-to-all-start.1 = ((f32[128,1,2,512]{3,2,1,0:T(2,128)}), f32[128,1,2,512]{3,2,1,0:T(2,128)S(1)}, u32[]{:S(2)}, u32[]{:S(2)}) async-start(f32[128,1,2,512]{3,2,1,0:T(2,128)} %bitcast.8), calls=%async_computation.1 | async-start | bytes 1048576 | tf_op jit(solution)/shard_map/all_to_all | solution.py:74
Sparse Core Ops, SparseCore 0:
  9.1 16.9 all-gather.1

commit v2 on v1

--- a/solution.py
+++ b/solution.py
@@ -33,7 +33,15 @@
     cells_dev, subspaces, capacity = codes.shape
     dim = queries.shape[1]
     cell_count = cells_dev * list_size
-    codebook_all = lax.all_gather(codebook, "query", axis=0, tiled=True)
+    query_size = lax.axis_size("query")
+    if query_size == 2:
+        other = lax.ppermute(codebook, "query", [(0, 1), (1, 0)])
+        first = lax.axis_index("query") == 0
+        low_half = jnp.where(first, codebook, other)
+        high_half = jnp.where(first, other, codebook)
+        codebook_all = jnp.concatenate([low_half, high_half], axis=0)
+    else:
+        codebook_all = lax.all_gather(codebook, "query", axis=0, tiled=True)
 
     flat_cells = probes.reshape(-1)
     pair_count = flat_cells.shape[0]

time: 103 us -> 89.1 us (0.87)
  between operations: 14.3 us -> 0.85 us
  other arithmetic: 7.53 us -> 6.37 us
    convert_element_type x1, other arithmetic: 1.38 us -> 0.06 us  [exact_parts(): high = values.astype(jnp.bfloat16)]
    ppermute x0 -> x1, waiting for transfers between devices: none -> 1.2 us  [body(): other = lax.ppermute(codebook, 'query', [(0, 1), (1, 0)])]
  transfers between devices with their start and end apart: 3 -> 3, of which waited for: 2 -> 3; matrix products, arithmetic and copies ran while one was open for 25% -> 22% of each run, Pallas kernels for 0% -> 0%
where the time goes in v2:
time: 89.1 us; the launch traced here: 88.8 us
  waiting for transfers between devices  28.8 us (32%)
  starting transfers between devices  22.2 us (25%)
  matrix products  20.9 us (23%)
  local copies, waits for them, and re-layouts  9.63 us (11%)
  other arithmetic  6.37 us (7%)
    all_to_all x1, waiting for transfers between devices, body(): lax.all_to_all(scored, 'list', split_axis=0, concat_axis=0, tiled=True)  18.5 us
    dot_general x1, matrix products, rebuilt_slots(): jnp.einsum('mvk,mkd->vmd', one_hot, parts, preferred_element_type=jnp.flo...  17.8 us
    all_to_all x1, starting transfers between devices, body(): lax.all_to_all(outgoing, 'list', split_axis=0, concat_axis=0, tiled=True)  15.5 us
    all_to_all x1, waiting for transfers between devices, body(): lax.all_to_all(outgoing, 'list', split_axis=0, concat_axis=0, tiled=True)  9.12 us
    all_to_all x1, starting transfers between devices, body(): lax.all_to_all(scored, 'list', split_axis=0, concat_axis=0, tiled=True)  6.62 us
    dot_general x1, matrix products, body(): jnp.einsum('sf,vf->sv', residual, rebuilt, precision=lax.Precision.HIGHEST)  3.16 us
    sub x1, local copies, waits for them, and re-layouts, body(): residual = arrived[:, local].reshape(list_size * slot_count, dim) - centroid  2.93 us
    reduce_sum x1, other arithmetic, body(): own_norm = jnp.sum(residual * residual, axis=1)  2.82 us
  transfers between devices with their start and end apart: 3, of which 3 were waited for; matrix products, arithmetic and copies ran while one was open for 22% of the time, Pallas kernels for 0%

profile of v2, /device:TPU:32, one launch (start us, length us, event | category | flops | bytes accessed | tf_op | source)
XLA Modules:
  0.0 88.8 jit_solution(15406450100209292241)
XLA Ops:
  0.0 0.8 eq.67
  0.8 0.2 convert_reduce_fusion
  1.3 0.1 fusion.12
  1.5 0.1 reshape.151
  1.7 1.0 %gather_fusion = f32[256,1024]{1,0:T(8,128)S(1)} fusion(f32[4,1024]{1,0:T(4,128)S(1)} %copy-done.1, s32[1024]{0:T(1024)S(1)} %pad_clamp_fusion.1), kind=kCustom, calls=%fused_computation | custom fusion | bytes 2098176 | tf_op jit(solution)/shard_map/gather | solution.py:61
  2.7 0.6 gather.9
  3.3 0.1 copy.9
  3.5 1.6 %bitcast_select_fusion = f32[128,1,2,1024]{3,2,1,0:T(2,128)} fusion(f32[128,1,2,1024]{3,2,0,1:T(2,128)S(1)} %gather.9, pred[128,2]{1,0:T(8,128)(4,1)S(1)} %copy.9), kind=kLoop, calls=%fused_computation.18 | loop fusion | flops 262144 | bytes 2097408 | tf_op jit(solution)/shard_map/jit(_where)/select_n | solution.py:61
  5.1 15.5 %all-to-all-start = ((f32[128,1,2,1024]{3,2,1,0:T(2,128)}), f32[128,1,2,1024]{3,2,1,0:T(2,128)}, u32[]{:S(2)}, u32[]{:S(2)}) async-start(f32[128,1,2,1024]{3,2,1,0:T(2,128)} %bitcast_select_fusion), calls=%async_computation | async-start | bytes 2097152 | tf_op jit(solution)/shard_map/all_to_all | solution.py:63
  21.3 1.2 %collective-permute-done = f32[32,16,256]{2,1,0:T(8,128)S(1)} collective-permute-done((f32[32,16,256]{2,1,0:T(8,128)S(1)}, f32[32,16,256]{2,1,0:T(8,128)S(1)}, u32[]{:S(2)}, u32[]{:S(2)}) %collective-permute-start) | collective-permute-done | bytes 524320 | tf_op jit(solution)/shard_map/ppermute | solution.py:38
  22.8 0.2 fusion.11
  22.9 0.7 copy-done.4
  23.6 17.8 %fusion.2 = f32[512,64,48]{0,2,1:T(8,128)S(1)} fusion(s32[64,512]{1,0:T(8,128)S(1)} %bitcast.41, bf16[64,256,16]{1,2,0:T(8,128)(2,1)S(1)} %get-tuple-element.10, bf16[64,256,16]{1,2,0:T(8,128)(2,1)S(1)} %get-tuple-element.9, bf16[64,256,16]{1,2,0:T(8,128)(2,1)S(1)} %fusion.10), kind=kOutput, calls=%fused_computation.5 | convolution fusion | flops 818413568 | bytes 7995392 | tf_op jit(solution)/shard_map/mvk,mkd->vmd/dot_general | solution.py:23
  41.3 1.1 %multiply_reduce_fusion = (f32[512]{0:T(512)S(1)}, f32[512,64,16]{0,2,1:T(8,128)S(1)}) fusion(f32[512,64,48]{0,2,1:T(8,128)S(1)} %fusion.2), kind=kLoop, calls=%fused_computation.8 | loop fusion | flops 2096640 | bytes 8390656 | tf_op jit(solution)/shard_map/reduce_sum | solution.py:73
  42.4 9.1 %all-to-all-done = f32[128,1,2,1024]{3,2,1,0:T(2,128)} async-done(((f32[128,1,2,1024]{3,2,1,0:T(2,128)}), f32[128,1,2,1024]{3,2,1,0:T(2,128)}, u32[]{:S(2)}, u32[]{:S(2)}) %all-to-all-start) | async-done | bytes 1048608 | tf_op jit(solution)/shard_map/all_to_all | solution.py:63
  51.5 2.8 %multiply_reduce_fusion.1 = (f32[128,2]{1,0:T(8,128)S(1)}, f32[128,1,2,1024]{3,2,1,0:T(2,128)}) fusion(f32[128,1,2,1024]{3,2,1,0:T(2,128)} %all-to-all-done, f32[1024]{0:T(1024)S(1)} %bitcast.40), kind=kLoop, calls=%fused_computation.21 | loop fusion | flops 786176 | bytes 2102272 | tf_op jit(solution)/shard_map/reduce_sum | solution.py:72
  54.4 2.9 %sub.35 = f32[256,1024]{1,0:T(8,128)} reshape(f32[128,1,2,1024]{3,2,1,0:T(2,128)} %get-tuple-element.6) | data formatting | bytes 2097152 | tf_op jit(solution)/shard_map/sub | solution.py:70
  57.3 0.1 add.68
  57.4 3.2 %fusion.9 = f32[256,512]{1,0:T(8,128)S(1)} fusion(f32[256,1024]{1,0:T(8,128)} %sub.35, f32[512,1024]{0,1:T(8,128)S(1)} %bitcast.39, f32[512]{0:T(512)S(1)} %get-tuple-element.7, f32[256]{0:T(256)S(1)} %add.68, pred[512]{0:T(512)(128)(4,1)S(1)} %iota_compare_fusion.6), kind=kOutput, calls=%fused_computation.16 | convolution fusion | flops 1611137024 | bytes 3673600 | tf_op jit(solution)/shard_map/sf,vf->sv/dot_general | solution.py:74
  60.6 1.1 %stack_reshape.3 = f32[128,1,2,512]{3,2,0,1:T(2,128)} reshape(f32[256,512]{1,0:T(8,128)S(1)} %fusion.9) | data formatting | bytes 1048576 | tf_op jit(solution)/shard_map/stack;reshape | solution.py:81
  61.7 6.6 %all-to-all-start.1 = ((f32[128,1,2,512]{3,2,1,0:T(2,128)}), f32[128,1,2,512]{3,2,1,0:T(2,128)S(1)}, u32[]{:S(2)}, u32[]{:S(2)}) async-start(f32[128,1,2,512]{3,2,1,0:T(2,128)} %bitcast.8), calls=%async_computation.1 | async-start | bytes 1048576 | tf_op jit(solution)/shard_map/all_to_all | solution.py:82
  68.5 18.5 %all-to-all-done.1 = f32[128,1,2,512]{3,2,1,0:T(2,128)S(1)} async-done(((f32[128,1,2,512]{3,2,1,0:T(2,128)}), f32[128,1,2,512]{3,2,1,0:T(2,128)S(1)}, u32[]{:S(2)}, u32[]{:S(2)}) %all-to-all-start.1) | async-done | bytes 524320 | tf_op jit(solution)/shard_map/all_to_all | solution.py:82
  87.0 0.4 reshape.147
  87.3 1.5 %gather_fusion.1 = f32[128,512]{1,0:T(8,128)} fusion(f32[256,512]{1,0:T(8,128)S(1)} %reshape.147, s32[1024]{0:T(1024)S(1)} %pad_clamp_fusion), kind=kCustom, calls=%fused_computation.1 | custom fusion | bytes 524800 | tf_op jit(solution)/shard_map/gather | solution.py:84
  (25 shorter events, 0.8 us)
Async XLA Ops:
  0.0 21.3 %copy-start = (f32[128,1024]{1,0:T(8,128)S(1)}, f32[128,1024]{1,0:T(8,128)}, u32[]{:S(2)}) copy-start(f32[128,1024]{1,0:T(8,128)} %param.8) | copy-start | bytes 1572868
  0.0 1.7 %copy-start.1 = (f32[4,1024]{1,0:T(4,128)S(1)}, f32[4,1024]{1,0:T(4,128)}, u32[]{:S(2)}) copy-start(f32[4,1024]{1,0:T(4,128)} %param.6) | copy-start | bytes 49156
  3.5 17.1 %copy-start.2 = (f32[32,16,256]{2,1,0:T(8,128)S(1)}, f32[32,16,256]{2,1,0:T(8,128)}, u32[]{:S(2)}) copy-start(f32[32,16,256]{2,1,0:T(8,128)} %param.9) | copy-start | bytes 1572868
  5.1 46.5 %all-to-all-start = ((f32[128,1,2,1024]{3,2,1,0:T(2,128)}), f32[128,1,2,1024]{3,2,1,0:T(2,128)}, u32[]{:S(2)}, u32[]{:S(2)}) async-start(f32[128,1,2,1024]{3,2,1,0:T(2,128)} %bitcast_select_fusion), calls=%async_computation | async-start | bytes 2097152 | tf_op jit(solution)/shard_map/all_to_all | solution.py:63
  20.5 2.0 %collective-permute-start = (f32[32,16,256]{2,1,0:T(8,128)S(1)}, f32[32,16,256]{2,1,0:T(8,128)S(1)}, u32[]{:S(2)}, u32[]{:S(2)}) collective-permute-start(f32[32,16,256]{2,1,0:T(8,128)S(1)} %copy-done.2), channel_id=1, source_target_pairs={{0,128},{128,0},{1,129},{129,1},{2,130},{130,2},{3,131},{131,3},{4... | collective-permute-start | bytes 1572872 | tf_op jit(solution)/shard_map/ppermute | solution.py:38
  22.7 0.9 %copy-start.4 = (s32[1,64,512]{2,1,0:T(8,128)S(1)}, s32[1,64,512]{2,1,0:T(8,128)}, u32[]{:S(2)}) copy-start(s32[1,64,512]{2,1,0:T(8,128)} %param.10) | copy-start | bytes 393220
  57.4 10.9 %copy-start.3 = (s32[4,32]{1,0:T(4,128)S(1)}, s32[4,32]{1,0:T(4,128)}, u32[]{:S(2)}) copy-start(s32[4,32]{1,0:T(4,128)} %param.7) | copy-start | bytes 1540
  61.7 25.3 %all-to-all-start.1 = ((f32[128,1,2,512]{3,2,1,0:T(2,128)}), f32[128,1,2,512]{3,2,1,0:T(2,128)S(1)}, u32[]{:S(2)}, u32[]{:S(2)}) async-start(f32[128,1,2,512]{3,2,1,0:T(2,128)} %bitcast.8), calls=%async_computation.1 | async-start | bytes 1048576 | tf_op jit(solution)/shard_map/all_to_all | solution.py:82

commit v3 on v2

--- a/solution.py
+++ b/solution.py
@@ -56,10 +56,14 @@
     chosen = (flat_cells[:, None, None] == cell_ids[None, :, None]) & (
         slot_rank[:, None, None] == slot_ids[None, None, :]
     )
-    filled = jnp.any(chosen, axis=0)
-    source = jnp.sum(jnp.where(chosen, owner_query[:, None, None], 0), axis=0)
-    outgoing = jnp.where(filled[..., None], queries[source], jnp.zeros((), jnp.float32))
-    outgoing = outgoing.reshape(list_size, cells_dev, slot_count, dim)
+    lanes = 128
+    tile_rows = dim // lanes
+    query_tiles = queries.reshape(query_rows, tile_rows, lanes)
+    outgoing = jnp.zeros((cell_count, slot_count, tile_rows, lanes), jnp.float32)
+    for row in range(query_rows):
+        taken = jnp.any(chosen & (owner_query == row)[:, None, None], axis=0)
+        outgoing = jnp.where(taken[:, :, None, None], query_tiles[row][None, None], outgoing)
+    outgoing = outgoing.reshape(list_size, cells_dev, slot_count, tile_rows, lanes)
     arrived = lax.all_to_all(outgoing, "list", split_axis=0, concat_axis=0, tiled=True)
 
     first_cell = lax.axis_index("list") * cells_dev
@@ -67,9 +71,10 @@
     scored = []
     for local in range(cells_dev):
         centroid = lax.dynamic_slice_in_dim(centroids, first_cell + local, 1, axis=0)
-        residual = arrived[:, local].reshape(list_size * slot_count, dim) - centroid
+        residual = arrived[:, local] - centroid.reshape(1, 1, tile_rows, lanes)
+        own_norm = jnp.sum(residual * residual, axis=(2, 3)).reshape(-1)
+        residual = residual.reshape(list_size * slot_count, dim)
         rebuilt = rebuilt_slots(codebook_all, codes[local])
-        own_norm = jnp.sum(residual * residual, axis=1)
         slot_norm = jnp.sum(rebuilt * rebuilt, axis=1)
         cross = jnp.einsum(
             "sf,vf->sv", residual, rebuilt, precision=lax.Precision.HIGHEST

time: 89.1 us -> 85.1 us (0.955)
  local copies, waits for them, and re-layouts: 9.63 us -> 7.61 us
  matrix products: 20.9 us -> 19.8 us
    sub x1 -> x0, local copies, waits for them, and re-layouts: 2.93 us -> none  [body(): residual = arrived[:, local].reshape(list_size * slot_count, dim) - centroid]
    reduce_sum x2 -> x1, other arithmetic: 2.96 us -> 0.49 us  [body(): own_norm = jnp.sum(residual * residual, axis=(2, 3)).reshape(-1)]
    gather x2 -> x0, local copies, waits for them, and re-layouts: 1.66 us -> none  [body(): queries[source]]
    unnamed x10, local copies, waits for them, and re-layouts: 0.68 us -> 2.18 us
    dot_general x1, matrix products: 3.16 us -> 2 us  [body(): jnp.einsum('sf,vf->sv', residual, rebuilt, precision=lax.Precision.HIGHEST)]
    reduce_sum x1, other arithmetic: 1.08 us -> 2.23 us  [body(): slot_norm = jnp.sum(rebuilt * rebuilt, axis=1)]
    select_n x3 -> x1, other arithmetic: 1.58 us -> 2.48 us  [body(): jnp.where(taken[:, :, None, None], query_tiles[row][None, None], outgoing)]
  transfers between devices with their start and end apart: 3 -> 3, of which waited for: 3 -> 3; matrix products, arithmetic and copies ran while one was open for 22% -> 24% of each run, Pallas kernels for 0% -> 0%
where the time goes in v3:
time: 85.1 us; the launch traced here: 84.7 us
  waiting for transfers between devices  28.7 us (34%)
  starting transfers between devices  21.7 us (25%)
  matrix products  19.8 us (23%)
  local copies, waits for them, and re-layouts  7.61 us (9%)
  other arithmetic  6.1 us (7%)
    all_to_all x1, waiting for transfers between devices, body(): lax.all_to_all(scored, 'list', split_axis=0, concat_axis=0, tiled=True)  19.2 us
    dot_general x1, matrix products, rebuilt_slots(): jnp.einsum('mvk,mkd->vmd', one_hot, parts, preferred_element_type=jnp.flo...  17.8 us
    all_to_all x1, starting transfers between devices, body(): lax.all_to_all(outgoing, 'list', split_axis=0, concat_axis=0, tiled=True)  15 us
    all_to_all x1, waiting for transfers between devices, body(): lax.all_to_all(outgoing, 'list', split_axis=0, concat_axis=0, tiled=True)  8.32 us
    all_to_all x1, starting transfers between devices, body(): lax.all_to_all(scored, 'list', split_axis=0, concat_axis=0, tiled=True)  6.62 us
    select_n x1, other arithmetic, body(): jnp.where(taken[:, :, None, None], query_tiles[row][None, None], outgoing)  2.48 us
    reduce_sum x1, other arithmetic, body(): slot_norm = jnp.sum(rebuilt * rebuilt, axis=1)  2.23 us
    unnamed x10, local copies, waits for them, and re-layouts  2.18 us
  transfers between devices with their start and end apart: 3, of which 3 were waited for; matrix products, arithmetic and copies ran while one was open for 24% of the time, Pallas kernels for 0%

profile of v3, /device:TPU:32, one launch (start us, length us, event | category | flops | bytes accessed | tf_op | source)
XLA Modules:
  0.0 84.7 jit_solution(2475026809639364656)
XLA Ops:
  0.0 0.9 %eq.99 = s32[128]{0:T(128)S(1)} reshape(s32[4,32]{1,0:T(4,128)} %param.7) | data formatting | bytes 1024 | tf_op jit(solution)/shard_map/eq | solution.py:56
  0.9 0.2 convert_reduce_fusion
  1.2 0.9 %fusion.23 = (f32[1,1024]{1,0:T(1,128)S(1)}, f32[1,1024]{1,0:T(1,128)S(1)}, f32[1,1024]{1,0:T(1,128)S(1)}, f32[1,1024]{1,0:T(1,128)S(1)}) fusion(f32[4,1024]{1,0:T(4,128)} %param.6), kind=kLoop, calls=%fused_computation.59 | loop fusion | bytes 32768 | tf_op jit(solution)/shard_map/slice | solution.py:65
  2.1 0.2 fusion.16
  2.2 0.1 copy.16
  2.4 0.1 copy.15
  2.5 0.1 copy.14
  2.7 0.1 copy.13
  2.8 2.5 %select_select_fusion = f32[128,1,2,8,128]{4,3,2,1,0:T(8,128)} fusion(f32[8,128]{1,0:T(8,128)S(1)} %bitcast.53, f32[8,128]{1,0:T(8,128)S(1)} %bitcast.54, f32[8,128]{1,0:T(8,128)S(1)} %bitcast.52, f32[8,128]{1,0:T(8,128)S(1)} %bitcast.51, pred[128,2]{1,0:T(8,128)(4,1)S(1)} %copy.16, pred[128,2]{1,0:T(8,128)(4,1)S(1)} %copy.15, pred[128,2]{1,0:T(8,128)(4,1)S(1)} %copy.14, ...), kind=kLoop, calls=%fused_computation.24 | loop fusion | flops 1048576 | bytes 1065984 | tf_op jit(solution)/shard_map/jit(_where)/select_n | solution.py:65
  5.3 15.0 %all-to-all-start = ((f32[128,1,2,8,128]{4,3,2,1,0:T(8,128)}), f32[128,1,2,8,128]{4,3,2,1,0:T(8,128)S(1)}, u32[]{:S(2)}, u32[]{:S(2)}) async-start(f32[128,1,2,8,128]{4,3,2,1,0:T(8,128)} %select_select_fusion), calls=%async_computation | async-start | bytes 2097152 | tf_op jit(solution)/shard_map/all_to_all | solution.py:67
  21.1 1.2 %collective-permute-done = f32[32,16,256]{2,1,0:T(8,128)S(1)} collective-permute-done((f32[32,16,256]{2,1,0:T(8,128)S(1)}, f32[32,16,256]{2,1,0:T(8,128)S(1)}, u32[]{:S(2)}, u32[]{:S(2)}) %collective-permute-start) | collective-permute-done | bytes 524320 | tf_op jit(solution)/shard_map/ppermute | solution.py:38
  22.5 0.2 fusion.15
  22.7 0.7 copy-done.4
  23.3 17.8 %fusion.2 = f32[512,64,48]{0,2,1:T(8,128)S(1)} fusion(s32[64,512]{1,0:T(8,128)S(1)} %bitcast.55, bf16[64,256,16]{1,2,0:T(8,128)(2,1)S(1)} %get-tuple-element.12, bf16[64,256,16]{1,2,0:T(8,128)(2,1)S(1)} %get-tuple-element.11, bf16[64,256,16]{1,2,0:T(8,128)(2,1)S(1)} %fusion.14), kind=kOutput, calls=%fused_computation.4 | convolution fusion | flops 818413568 | bytes 7995392 | tf_op jit(solution)/shard_map/mvk,mkd->vmd/dot_general | solution.py:23
  41.1 2.2 %multiply_reduce_fusion = (f32[512]{0:T(512)S(1)}, f32[512,64,16]{0,2,1:T(8,128)}) fusion(f32[512,64,48]{0,2,1:T(8,128)S(1)} %fusion.2), kind=kLoop, calls=%fused_computation.7 | loop fusion | flops 2096640 | bytes 8390656 | tf_op jit(solution)/shard_map/reduce_sum | solution.py:78
  43.3 8.3 %all-to-all-done = f32[128,1,2,8,128]{4,3,2,1,0:T(8,128)S(1)} async-done(((f32[128,1,2,8,128]{4,3,2,1,0:T(8,128)}), f32[128,1,2,8,128]{4,3,2,1,0:T(8,128)S(1)}, u32[]{:S(2)}, u32[]{:S(2)}) %all-to-all-start) | async-done | bytes 1048608 | tf_op jit(solution)/shard_map/all_to_all | solution.py:67
  51.7 0.5 fusion.13
  52.4 1.5 %copy-done.1 = f32[512,64,16]{0,2,1:T(8,128)S(1)} copy-done((f32[512,64,16]{0,2,1:T(8,128)S(1)}, f32[512,64,16]{0,2,1:T(8,128)}, u32[]{:S(2)}) %copy-start.1) | copy-done | bytes 2097176
  53.9 2.0 %fusion.9 = f32[256,512]{1,0:T(8,128)S(1)} fusion(f32[512,1024]{0,1:T(8,128)S(1)} %bitcast.47, f32[32,8,8,128]{3,2,1,0:T(8,128)S(1)} %bitcast.48, f32[512]{0:T(512)S(1)} %get-tuple-element.9, f32[256]{0:T(256)S(1)} %add.62, pred[512]{0:T(512)(128)(4,1)S(1)} %iota_compare_fusion.6), kind=kOutput, calls=%fused_computation.15 | convolution fusion | flops 1611137024 | bytes 3673600 | tf_op jit(solution)/shard_map/sf,vf->sv/dot_general | solution.py:79
  55.9 1.1 %stack_reshape.3 = f32[128,1,2,512]{3,2,0,1:T(2,128)} reshape(f32[256,512]{1,0:T(8,128)S(1)} %fusion.9) | data formatting | bytes 1048576 | tf_op jit(solution)/shard_map/stack;reshape | solution.py:86
  57.0 6.6 %all-to-all-start.1 = ((f32[128,1,2,512]{3,2,1,0:T(2,128)}), f32[128,1,2,512]{3,2,1,0:T(2,128)S(1)}, u32[]{:S(2)}, u32[]{:S(2)}) async-start(f32[128,1,2,512]{3,2,1,0:T(2,128)} %bitcast.11), calls=%async_computation.1 | async-start | bytes 1048576 | tf_op jit(solution)/shard_map/all_to_all | solution.py:87
  63.7 19.2 %all-to-all-done.1 = f32[128,1,2,512]{3,2,1,0:T(2,128)S(1)} async-done(((f32[128,1,2,512]{3,2,1,0:T(2,128)}), f32[128,1,2,512]{3,2,1,0:T(2,128)S(1)}, u32[]{:S(2)}, u32[]{:S(2)}) %all-to-all-start.1) | async-done | bytes 524320 | tf_op jit(solution)/shard_map/all_to_all | solution.py:87
  82.9 0.4 reshape.162
  83.3 1.5 %gather_fusion = f32[128,512]{1,0:T(8,128)} fusion(f32[256,512]{1,0:T(8,128)S(1)} %reshape.162, s32[1024]{0:T(1024)S(1)} %pad_clamp_fusion), kind=kCustom, calls=%fused_computation | custom fusion | bytes 524800 | tf_op jit(solution)/shard_map/gather | solution.py:89
  (23 shorter events, 0.7 us)
Async XLA Ops:
  0.0 21.1 %copy-start = (f32[128,1024]{1,0:T(8,128)S(1)}, f32[128,1024]{1,0:T(8,128)}, u32[]{:S(2)}) copy-start(f32[128,1024]{1,0:T(8,128)} %param.8) | copy-start | bytes 1572868
  0.0 20.3 %copy-start.2 = (f32[32,16,256]{2,1,0:T(8,128)S(1)}, f32[32,16,256]{2,1,0:T(8,128)}, u32[]{:S(2)}) copy-start(f32[32,16,256]{2,1,0:T(8,128)} %param.9) | copy-start | bytes 1572868
  5.3 46.4 %all-to-all-start = ((f32[128,1,2,8,128]{4,3,2,1,0:T(8,128)}), f32[128,1,2,8,128]{4,3,2,1,0:T(8,128)S(1)}, u32[]{:S(2)}, u32[]{:S(2)}) async-start(f32[128,1,2,8,128]{4,3,2,1,0:T(8,128)} %select_select_fusion), calls=%async_computation | async-start | bytes 2097152 | tf_op jit(solution)/shard_map/all_to_all | solution.py:67
  20.3 2.0 %collective-permute-start = (f32[32,16,256]{2,1,0:T(8,128)S(1)}, f32[32,16,256]{2,1,0:T(8,128)S(1)}, u32[]{:S(2)}, u32[]{:S(2)}) collective-permute-start(f32[32,16,256]{2,1,0:T(8,128)S(1)} %copy-done.2), channel_id=1, source_target_pairs={{0,128},{128,0},{1,129},{129,1},{2,130},{130,2},{3,131},{131,3},{4... | collective-permute-start | bytes 1572872 | tf_op jit(solution)/shard_map/ppermute | solution.py:38
  22.4 0.9 %copy-start.4 = (s32[1,64,512]{2,1,0:T(8,128)S(1)}, s32[1,64,512]{2,1,0:T(8,128)}, u32[]{:S(2)}) copy-start(s32[1,64,512]{2,1,0:T(8,128)} %param.10) | copy-start | bytes 393220
  52.3 1.6 %copy-start.1 = (f32[512,64,16]{0,2,1:T(8,128)S(1)}, f32[512,64,16]{0,2,1:T(8,128)}, u32[]{:S(2)}) copy-start(f32[512,64,16]{0,2,1:T(8,128)} %get-tuple-element.10) | copy-start | bytes 6291460
  53.9 9.7 %copy-start.3 = (s32[4,32]{1,0:T(4,128)S(1)}, s32[4,32]{1,0:T(4,128)}, u32[]{:S(2)}) copy-start(s32[4,32]{1,0:T(4,128)} %param.7) | copy-start | bytes 1540
  57.0 25.9 %all-to-all-start.1 = ((f32[128,1,2,512]{3,2,1,0:T(2,128)}), f32[128,1,2,512]{3,2,1,0:T(2,128)S(1)}, u32[]{:S(2)}, u32[]{:S(2)}) async-start(f32[128,1,2,512]{3,2,1,0:T(2,128)} %bitcast.11), calls=%async_computation.1 | async-start | bytes 1048576 | tf_op jit(solution)/shard_map/all_to_all | solution.py:87

commit v4 on v3

--- a/solution.py
+++ b/solution.py
@@ -1,3 +1,5 @@
+import functools
+
 import jax
 import jax.numpy as jnp
 from jax import lax
@@ -27,7 +29,46 @@
     return rebuilt.reshape(capacity, subspaces * sub_width)
 
 
-def body(queries, probes, centroids, codebook, codes, cell_sizes):
+def list_digits(mesh):
+    row = mesh.devices[0] if mesh.devices.ndim == 2 else None
+    if row is None or any(getattr(d, "coords", None) is None for d in row):
+        return None
+    coords = [tuple(d.coords) for d in row]
+    sizes = tuple(1 + max(c[axis] for c in coords) for axis in (1, 0, 2))
+    count = sizes[0] * sizes[1] * sizes[2]
+    if count != len(row):
+        return None
+    for place, (x, y, z) in enumerate(coords):
+        if place != (y * sizes[1] + x) * sizes[2] + z:
+            return None
+    return sizes
+
+
+def digit_groups(sizes):
+    first, second, third = sizes
+    index = lambda a, b, c: (a * second + b) * third + c
+    by_third = [[index(a, b, c) for c in range(third)] for a in range(first) for b in range(second)]
+    by_second = [[index(a, b, c) for b in range(second)] for a in range(first) for c in range(third)]
+    by_first = [[index(a, b, c) for a in range(first)] for b in range(second) for c in range(third)]
+    return (by_first, by_second, by_third)
+
+
+def list_exchange(values, sizes):
+    if sizes is None:
+        return lax.all_to_all(values, "list", split_axis=0, concat_axis=0, tiled=True)
+    rest = values.shape[1:]
+    staged = values.reshape(*sizes, *rest)
+    groups = digit_groups(sizes)
+    for digit in (2, 1, 0):
+        if sizes[digit] > 1:
+            staged = lax.all_to_all(
+                staged, "list", split_axis=digit, concat_axis=digit,
+                axis_index_groups=groups[digit], tiled=True,
+            )
+    return staged.reshape(values.shape)
+
+
+def body(sizes, queries, probes, centroids, codebook, codes, cell_sizes):
     list_size = lax.axis_size("list")
     query_rows, probe_count = probes.shape
     cells_dev, subspaces, capacity = codes.shape
@@ -64,7 +105,7 @@
         taken = jnp.any(chosen & (owner_query == row)[:, None, None], axis=0)
         outgoing = jnp.where(taken[:, :, None, None], query_tiles[row][None, None], outgoing)
     outgoing = outgoing.reshape(list_size, cells_dev, slot_count, tile_rows, lanes)
-    arrived = lax.all_to_all(outgoing, "list", split_axis=0, concat_axis=0, tiled=True)
+    arrived = list_exchange(outgoing, sizes)
 
     first_cell = lax.axis_index("list") * cells_dev
     positions = jnp.arange(capacity, dtype=jnp.int32)
@@ -84,7 +125,7 @@
         total = jnp.where(valid[None, :], total, jnp.zeros((), jnp.float32))
         scored.append(total.reshape(list_size, slot_count, capacity))
     scored = jnp.stack(scored, axis=1)
-    returned = lax.all_to_all(scored, "list", split_axis=0, concat_axis=0, tiled=True)
+    returned = list_exchange(scored, sizes)
     returned = returned.reshape(cell_count * slot_count, capacity)
     result = returned[flat_cells * slot_count + slot_rank]
     return result.reshape(query_rows, probe_count, capacity)
@@ -100,4 +141,5 @@
         P("list"),
     )
     out_specs = P(("query", "list"), None, None)
-    return jax.shard_map(body, mesh=mesh, in_specs=in_specs, out_specs=out_specs, check_vma=False)
+    sizes = list_digits(mesh)
+    return jax.shard_map(functools.partial(body, sizes), mesh=mesh, in_specs=in_specs, out_specs=out_specs, check_vma=False)

time: 85.1 us -> 139 us (1.63)
  blocking collectives: 0 us -> 31.4 us
  waiting for transfers between devices: 28.7 us -> 47.6 us
    all_to_all x0 -> x2, blocking collectives: none -> 31.4 us  [list_exchange(): lax.all_to_all(staged, 'list', split_axis=digit, concat_axis=digit, axis_...]
    all_to_all x2 -> x4, waiting for transfers between devices: 27.5 us -> 47.6 us  [list_exchange(): lax.all_to_all(staged, 'list', split_axis=digit, concat_axis=digit, axis_...]
    all_to_all x0 -> x4, local copies, waits for them, and re-layouts: none -> 3.1 us  [list_exchange(): lax.all_to_all(staged, 'list', split_axis=digit, concat_axis=digit, axis_...]
    reduce_sum x1, other arithmetic: 0.49 us -> 2.66 us  [body(): own_norm = jnp.sum(residual * residual, axis=(2, 3)).reshape(-1)]
    unnamed x10 -> x8, local copies, waits for them, and re-layouts: 2.18 us -> 0.02 us
    all_to_all x2 -> x4, starting transfers between devices: 21.6 us -> 21.8 us  [list_exchange(): lax.all_to_all(staged, 'list', split_axis=digit, concat_axis=digit, axis_...]
  transfers between devices with their start and end apart: 3 -> 5, of which waited for: 3 -> 3; matrix products, arithmetic and copies ran while one was open for 24% -> 15% of each run, Pallas kernels for 0% -> 0%
where the time goes in v4:
time: 139 us; the launch traced here: 138 us
  waiting for transfers between devices  47.6 us (34%)
  blocking collectives  31.4 us (23%)
  starting transfers between devices  21.8 us (16%)
  matrix products  21 us (15%)
  local copies, waits for them, and re-layouts  8.41 us (6%)
  other arithmetic  7.02 us (5%)
    all_to_all x4, waiting for transfers between devices, list_exchange(): lax.all_to_all(staged, 'list', split_axis=digit, concat_axis=digit, axis_...  47.6 us
    all_to_all x2, blocking collectives, list_exchange(): lax.all_to_all(staged, 'list', split_axis=digit, concat_axis=digit, axis_...  31.4 us
    all_to_all x4, starting transfers between devices, list_exchange(): lax.all_to_all(staged, 'list', split_axis=digit, concat_axis=digit, axis_...  21.8 us
    dot_general x1, matrix products, rebuilt_slots(): jnp.einsum('mvk,mkd->vmd', one_hot, parts, preferred_element_type=jnp.flo...  17.8 us
    dot_general x1, matrix products, body(): jnp.einsum('sf,vf->sv', residual, rebuilt, precision=lax.Precision.HIGHEST)  3.22 us
    all_to_all x4, local copies, waits for them, and re-layouts, list_exchange(): lax.all_to_all(staged, 'list', split_axis=digit, concat_axis=digit, axis_...  3.1 us
  transfers between devices with their start and end apart: 5, of which 3 were waited for; matrix products, arithmetic and copies ran while one was open for 15% of the time, Pallas kernels for 0%

profile of v4, /device:TPU:32, one launch (start us, length us, event | category | flops | bytes accessed | tf_op | source)
XLA Modules:
  0.0 138.0 jit_solution(11385077237975409601)
XLA Ops:
  0.0 0.9 eq.99
  1.2 0.9 fusion.21
  2.3 0.2 copy.34
  2.6 0.2 copy.33
  3.4 2.4 %select_select_fusion = f32[4,4,8,1,2,8,128]{6,5,4,3,1,0,2:T(8,128)} fusion(f32[8,128]{1,0:T(8,128)S(1)} %bitcast.57, f32[8,128]{1,0:T(8,128)S(1)} %bitcast.58, f32[8,128]{1,0:T(8,128)S(1)} %bitcast.56, f32[8,128]{1,0:T(8,128)S(1)} %bitcast.55, pred[4,4,8,2]{3,1,0,2:T(4,128)(4,1)S(1)} %copy.34, pred[4,4,8,2]{3,1,0,2:T(4,128)(4,1)S(1)} %copy.33, ...), kind=kLoop, calls=%fused_computation.22 | loop fusion | flops 1048576 | bytes 1065984 | tf_op jit(solution)/shard_map/jit(_where)/select_n | solution.py:106
  5.9 8.6 %all-to-all-start = ((f32[4,4,8,1,2,8,128]{6,5,4,3,1,0,2:T(8,128)}), f32[4,4,8,1,2,8,128]{6,5,4,3,1,0,2:T(8,128)S(1)}, u32[]{:S(2)}, u32[]{:S(2)}) async-start(f32[4,4,8,1,2,8,128]{6,5,4,3,1,0,2:T(8,128)} %select_select_fusion), calls=%async_computation | async-start | bytes 2097152 | tf_op jit(solution)/shard_map/all_to_all | solution.py:64
  14.4 27.3 %all-to-all-done = f32[4,4,8,1,2,8,128]{6,5,4,3,1,0,2:T(8,128)S(1)} async-done(((f32[4,4,8,1,2,8,128]{6,5,4,3,1,0,2:T(8,128)}), f32[4,4,8,1,2,8,128]{6,5,4,3,1,0,2:T(8,128)S(1)}, u32[]{:S(2)}, u32[]{:S(2)}) %all-to-all-start) | async-done | bytes 1048608 | tf_op jit(solution)/shard_map/all_to_all | solution.py:64
  41.7 1.1 copy.35
  42.8 4.3 %all-to-all-start.1 = ((f32[4,4,8,1,2,8,128]{6,5,4,3,2,0,1:T(8,128)}), f32[4,4,8,1,2,8,128]{6,5,4,3,2,0,1:T(8,128)S(1)}, u32[]{:S(2)}, u32[]{:S(2)}) async-start(f32[4,4,8,1,2,8,128]{6,5,4,3,2,0,1:T(8,128)} %copy.35), calls=%async_computation.1 | async-start | bytes 2097152 | tf_op jit(solution)/shard_map/all_to_all | solution.py:64
  48.2 12.3 %all-to-all-done.1 = f32[4,4,8,1,2,8,128]{6,5,4,3,2,0,1:T(8,128)S(1)} async-done(((f32[4,4,8,1,2,8,128]{6,5,4,3,2,0,1:T(8,128)}), f32[4,4,8,1,2,8,128]{6,5,4,3,2,0,1:T(8,128)S(1)}, u32[]{:S(2)}, u32[]{:S(2)}) %all-to-all-start.1) | async-done | bytes 1048608 | tf_op jit(solution)/shard_map/all_to_all | solution.py:64
  60.5 1.1 copy.36
  61.6 4.5 %all-to-all-start.2 = ((f32[4,4,8,1,2,8,128]{6,5,4,3,2,1,0:T(8,128)}), f32[4,4,8,1,2,8,128]{6,5,4,3,2,1,0:T(8,128)}, u32[]{:S(2)}, u32[]{:S(2)}) async-start(f32[4,4,8,1,2,8,128]{6,5,4,3,2,1,0:T(8,128)} %copy.36), calls=%async_computation.2 | async-start | bytes 2097152 | tf_op jit(solution)/shard_map/all_to_all | solution.py:64
  66.1 17.8 %fusion.2 = f32[512,64,48]{0,2,1:T(8,128)S(1)} fusion(s32[64,512]{1,0:T(8,128)S(1)} %bitcast.59, bf16[64,256,16]{1,2,0:T(8,128)(2,1)S(1)} %get-tuple-element.14, bf16[64,256,16]{1,2,0:T(8,128)(2,1)S(1)} %get-tuple-element.13, bf16[64,256,16]{1,2,0:T(8,128)(2,1)S(1)} %fusion.12), kind=kOutput, calls=%fused_computation.4 | convolution fusion | flops 818413568 | bytes 7995392 | tf_op jit(solution)/shard_map/mvk,mkd->vmd/dot_general | solution.py:25
  83.9 1.1 multiply_reduce_fusion
  85.0 2.7 %multiply_reduce_fusion.1 = (f32[4,4,8,2]{3,2,1,0:T(8,128)S(1)}, f32[4,4,8,1,2,8,128]{6,5,4,3,2,1,0:T(8,128)}) fusion(f32[4,4,8,1,2,8,128]{6,5,4,3,2,1,0:T(8,128)} %all-to-all-done.2, f32[8,128]{1,0:T(8,128)S(1)} %bitcast.54), kind=kLoop, calls=%fused_computation.21 | loop fusion | flops 786176 | bytes 2102272 | tf_op jit(solution)/shard_map/reduce_sum | solution.py:116
  87.8 3.2 %fusion.9 = f32[256,512]{1,0:T(8,128)S(1)} fusion(f32[512,1024]{0,1:T(8,128)S(1)} %bitcast.52, f32[32,8,8,128]{3,2,1,0:T(8,128)} %bitcast.53, f32[512]{0:T(512)S(1)} %get-tuple-element.11, f32[256]{0:T(256)S(1)} %add.62, pred[512]{0:T(512)(128)(4,1)S(1)} %iota_compare_fusion.6), kind=kOutput, calls=%fused_computation.15 | convolution fusion | flops 1611137024 | bytes 3673600 | tf_op jit(solution)/shard_map/sf,vf->sv/dot_general | solution.py:120
  91.0 0.3 reshape_stack_reshape.3
  91.4 21.0 %all_to_all.30 = f32[4,4,8,1,2,512]{5,4,1,0,3,2:T(2,128)S(1)} all-to-all(f32[4,4,8,1,2,512]{5,4,1,0,3,2:T(2,128)S(1)} %copy.39), channel_id=1, replica_groups={{0,1,2,3,4,5,6,7},{8,9,10,11,12,13,14,15},{16,17,18,19,20,21,22,23},{24..., dimensions={2} | all-to-all | bytes 1048576 | tf_op jit(solution)/shard_map/all_to_all | solution.py:64
  112.4 10.5 %all_to_all.31 = f32[4,4,8,1,2,512]{5,4,2,0,3,1:T(2,128)S(1)} all-to-all(f32[4,4,8,1,2,512]{5,4,2,0,3,1:T(2,128)S(1)} %copy.40), channel_id=1, replica_groups={{0,8,16,24},{1,9,17,25},{2,10,18,26},{3,11,19,27},{4,12,20,28},{5,13,21..., dimensions={1} | all-to-all | bytes 1048576 | tf_op jit(solution)/shard_map/all_to_all | solution.py:64
  122.9 0.8 copy.41
  123.7 4.5 %all-to-all-start.5 = ((f32[4,4,8,1,2,512]{5,4,2,1,3,0:T(2,128)}), f32[4,4,8,1,2,512]{5,4,2,1,3,0:T(2,128)S(1)}, u32[]{:S(2)}, u32[]{:S(2)}) async-start(f32[4,4,8,1,2,512]{5,4,2,1,3,0:T(2,128)} %copy.41), calls=%async_computation.5 | async-start | bytes 1048576 | tf_op jit(solution)/shard_map/all_to_all | solution.py:64
  128.3 8.0 %all-to-all-done.5 = f32[4,4,8,1,2,512]{5,4,2,1,3,0:T(2,128)S(1)} async-done(((f32[4,4,8,1,2,512]{5,4,2,1,3,0:T(2,128)}), f32[4,4,8,1,2,512]{5,4,2,1,3,0:T(2,128)S(1)}, u32[]{:S(2)}, u32[]{:S(2)}) %all-to-all-start.5) | async-done | bytes 524320 | tf_op jit(solution)/shard_map/all_to_all | solution.py:64
  136.2 0.4 reshape_reshape.4
  136.6 1.5 %gather_fusion = f32[128,512]{1,0:T(8,128)} fusion(f32[256,512]{1,0:T(8,128)S(1)} %reshape_reshape.4, s32[1024]{0:T(1024)S(1)} %pad_clamp_fusion), kind=kCustom, calls=%fused_computation | custom fusion | bytes 524800 | tf_op jit(solution)/shard_map/gather | solution.py:130
  (35 shorter events, 1.9 us)
Async XLA Ops:
  0.0 47.8 %copy-start = (f32[128,1024]{1,0:T(8,128)S(1)}, f32[128,1024]{1,0:T(8,128)}, u32[]{:S(2)}) copy-start(f32[128,1024]{1,0:T(8,128)} %param.8) | copy-start | bytes 1572868
  0.0 14.4 %copy-start.1 = (f32[32,16,256]{2,1,0:T(8,128)S(1)}, f32[32,16,256]{2,1,0:T(8,128)}, u32[]{:S(2)}) copy-start(f32[32,16,256]{2,1,0:T(8,128)} %param.9) | copy-start | bytes 1572868
  5.9 35.8 %all-to-all-start = ((f32[4,4,8,1,2,8,128]{6,5,4,3,1,0,2:T(8,128)}), f32[4,4,8,1,2,8,128]{6,5,4,3,1,0,2:T(8,128)S(1)}, u32[]{:S(2)}, u32[]{:S(2)}) async-start(f32[4,4,8,1,2,8,128]{6,5,4,3,1,0,2:T(8,128)} %select_select_fusion), calls=%async_computation | async-start | bytes 2097152 | tf_op jit(solution)/shard_map/all_to_all | solution.py:64
  14.4 33.4 %collective-permute-start = (f32[32,16,256]{2,1,0:T(8,128)S(1)}, f32[32,16,256]{2,1,0:T(8,128)S(1)}, u32[]{:S(2)}, u32[]{:S(2)}) collective-permute-start(f32[32,16,256]{2,1,0:T(8,128)S(1)} %copy-done.1), channel_id=1, source_target_pairs={{0,128},{128,0},{1,129},{129,1},{2,130},{130,2},{3,131},{131,3},{4... | collective-permute-start | bytes 1572872 | tf_op jit(solution)/shard_map/ppermute | solution.py:79
  42.8 17.7 %all-to-all-start.1 = ((f32[4,4,8,1,2,8,128]{6,5,4,3,2,0,1:T(8,128)}), f32[4,4,8,1,2,8,128]{6,5,4,3,2,0,1:T(8,128)S(1)}, u32[]{:S(2)}, u32[]{:S(2)}) async-start(f32[4,4,8,1,2,8,128]{6,5,4,3,2,0,1:T(8,128)} %copy.35), calls=%async_computation.1 | async-start | bytes 2097152 | tf_op jit(solution)/shard_map/all_to_all | solution.py:64
  48.2 17.9 %copy-start.3 = (s32[1,64,512]{2,1,0:T(8,128)S(1)}, s32[1,64,512]{2,1,0:T(8,128)}, u32[]{:S(2)}) copy-start(s32[1,64,512]{2,1,0:T(8,128)} %param.10) | copy-start | bytes 393220
  61.6 23.3 %all-to-all-start.2 = ((f32[4,4,8,1,2,8,128]{6,5,4,3,2,1,0:T(8,128)}), f32[4,4,8,1,2,8,128]{6,5,4,3,2,1,0:T(8,128)}, u32[]{:S(2)}, u32[]{:S(2)}) async-start(f32[4,4,8,1,2,8,128]{6,5,4,3,2,1,0:T(8,128)} %copy.36), calls=%async_computation.2 | async-start | bytes 2097152 | tf_op jit(solution)/shard_map/all_to_all | solution.py:64
  112.3 15.8 %copy-start.2 = (s32[4,32]{1,0:T(4,128)S(1)}, s32[4,32]{1,0:T(4,128)}, u32[]{:S(2)}) copy-start(s32[4,32]{1,0:T(4,128)} %param.7) | copy-start | bytes 1540
  123.7 12.5 %all-to-all-start.5 = ((f32[4,4,8,1,2,512]{5,4,2,1,3,0:T(2,128)}), f32[4,4,8,1,2,512]{5,4,2,1,3,0:T(2,128)S(1)}, u32[]{:S(2)}, u32[]{:S(2)}) async-start(f32[4,4,8,1,2,512]{5,4,2,1,3,0:T(2,128)} %copy.41), calls=%async_computation.5 | async-start | bytes 1048576 | tf_op jit(solution)/shard_map/all_to_all | solution.py:64

commit v5 on v3

--- a/solution.py
+++ b/solution.py
@@ -44,25 +44,23 @@
         codebook_all = lax.all_gather(codebook, "query", axis=0, tiled=True)
 
     flat_cells = probes.reshape(-1)
-    pair_count = flat_cells.shape[0]
-    pair_order = jnp.arange(pair_count, dtype=jnp.int32)
-    earlier_same = (flat_cells[:, None] == flat_cells[None, :]) & (
-        pair_order[None, :] < pair_order[:, None]
-    )
-    slot_rank = jnp.sum(earlier_same.astype(jnp.int32), axis=1)
-    owner_query = pair_order // probe_count
     cell_ids = jnp.arange(cell_count, dtype=jnp.int32)
-    slot_ids = jnp.arange(slot_count, dtype=jnp.int32)
-    chosen = (flat_cells[:, None, None] == cell_ids[None, :, None]) & (
-        slot_rank[:, None, None] == slot_ids[None, None, :]
-    )
+    contains = jnp.any(probes[:, :, None] == cell_ids[None, None, :], axis=1)
+    counted = contains.astype(jnp.int32)
+    earlier_rows = jnp.cumsum(counted, axis=0) - counted
+    rank_of = jnp.take_along_axis(earlier_rows, probes, axis=1)
+    slot_rank = rank_of.reshape(-1)
     lanes = 128
     tile_rows = dim // lanes
     query_tiles = queries.reshape(query_rows, tile_rows, lanes)
+    row_at = jnp.full((cell_count, slot_count), -1, jnp.int32)
+    for row in range(query_rows):
+        here = contains[row][:, None] & (earlier_rows[row][:, None] == jnp.arange(slot_count)[None, :])
+        row_at = jnp.where(here, row, row_at)
+    row_at = row_at[:, :, None, None]
     outgoing = jnp.zeros((cell_count, slot_count, tile_rows, lanes), jnp.float32)
     for row in range(query_rows):
-        taken = jnp.any(chosen & (owner_query == row)[:, None, None], axis=0)
-        outgoing = jnp.where(taken[:, :, None, None], query_tiles[row][None, None], outgoing)
+        outgoing = jnp.where(row_at == row, query_tiles[row][None, None], outgoing)
     outgoing = outgoing.reshape(list_size, cells_dev, slot_count, tile_rows, lanes)
     arrived = lax.all_to_all(outgoing, "list", split_axis=0, concat_axis=0, tiled=True)
 
@@ -77,7 +75,7 @@
         rebuilt = rebuilt_slots(codebook_all, codes[local])
         slot_norm = jnp.sum(rebuilt * rebuilt, axis=1)
         cross = jnp.einsum(
-            "sf,vf->sv", residual, rebuilt, precision=lax.Precision.HIGHEST
+            "sf,vf->sv", residual, rebuilt, precision=lax.Precision.HIGH
         )
         total = (own_norm[:, None] + slot_norm[None, :]) - 2.0 * cross
         valid = positions < cell_sizes[local]

time: 85.1 us -> 83.6 us (0.982)
  waiting for transfers between devices: 28.7 us -> 27 us
    all_to_all x1, waiting for transfers between devices: 19.2 us -> 17.4 us  [body(): lax.all_to_all(scored, 'list', split_axis=0, concat_axis=0, tiled=True)]
    gather x0 -> x3, local copies, waits for them, and re-layouts: none -> 1.67 us  [body(): rank_of = jnp.take_along_axis(earlier_rows, probes, axis=1)]
  transfers between devices with their start and end apart: 3 -> 3, of which waited for: 3 -> 3; matrix products, arithmetic and copies ran while one was open for 24% -> 27% of each run, Pallas kernels for 0% -> 0%
where the time goes in v5:
time: 83.6 us; the launch traced here: 83.2 us
  waiting for transfers between devices  27 us (32%)
  starting transfers between devices  21.7 us (26%)
  matrix products  19 us (23%)
  local copies, waits for them, and re-layouts  7.89 us (9%)
  other arithmetic  6.72 us (8%)
    dot_general x1, matrix products, rebuilt_slots(): jnp.einsum('mvk,mkd->vmd', one_hot, parts, preferred_element_type=jnp.flo...  17.8 us
    all_to_all x1, waiting for transfers between devices, body(): lax.all_to_all(scored, 'list', split_axis=0, concat_axis=0, tiled=True)  17.4 us
    all_to_all x1, starting transfers between devices, body(): lax.all_to_all(outgoing, 'list', split_axis=0, concat_axis=0, tiled=True)  15 us
    all_to_all x1, waiting for transfers between devices, body(): lax.all_to_all(outgoing, 'list', split_axis=0, concat_axis=0, tiled=True)  8.36 us
    all_to_all x1, starting transfers between devices, body(): lax.all_to_all(scored, 'list', split_axis=0, concat_axis=0, tiled=True)  6.63 us
    select_n x1, other arithmetic, body(): outgoing = jnp.where(row_at == row, query_tiles[row][None, None], outgoing)  2.46 us
    reduce_sum x1, other arithmetic, body(): slot_norm = jnp.sum(rebuilt * rebuilt, axis=1)  2.22 us
    unnamed x10, local copies, waits for them, and re-layouts  2.18 us
  transfers between devices with their start and end apart: 3, of which 3 were waited for; matrix products, arithmetic and copies ran while one was open for 27% of the time, Pallas kernels for 0%

profile of v5, /device:TPU:32, one launch (start us, length us, event | category | flops | bytes accessed | tf_op | source)
XLA Modules:
  0.0 83.2 jit_solution(2646393362999713285)
XLA Ops:
  0.0 0.9 %fusion.16 = pred[4,128]{1,0:T(4,128)(4,1)S(1)} fusion(s32[4,32]{1,0:T(4,128)} %param.7), kind=kLoop, calls=%fused_computation.37 | loop fusion | flops 32256 | bytes 1024 | tf_op jit(solution)/shard_map/reduce_or | solution.py:48
  0.9 0.9 %fusion.23 = (f32[1,1024]{1,0:T(1,128)S(1)}, f32[1,1024]{1,0:T(1,128)S(1)}, f32[1,1024]{1,0:T(1,128)S(1)}, f32[1,1024]{1,0:T(1,128)S(1)}) fusion(f32[4,1024]{1,0:T(4,128)} %param.6), kind=kLoop, calls=%fused_computation.64 | loop fusion | bytes 32768 | tf_op jit(solution)/shard_map/slice | solution.py:63
  1.8 0.2 broadcast_compare_fusion.3
  2.1 2.5 %select_select_fusion = f32[128,1,2,8,128]{4,3,2,1,0:T(8,128)} fusion(f32[8,128]{1,0:T(8,128)S(1)} %bitcast.69, f32[8,128]{1,0:T(8,128)S(1)} %bitcast.70, f32[8,128]{1,0:T(8,128)S(1)} %bitcast.68, f32[8,128]{1,0:T(8,128)S(1)} %bitcast.67, pred[128,2]{1,0:T(8,128)(4,1)S(1)} %get-tuple-element.18, pred[128,2]{1,0:T(8,128)(4,1)S(1)} %get-tuple-element.17, ...), kind=kLoop, calls=%fused_computation.25 | loop fusion | flops 1048576 | bytes 1065984 | tf_op jit(solution)/shard_map/jit(_where)/select_n | solution.py:63
  4.5 15.0 %all-to-all-start = ((f32[128,1,2,8,128]{4,3,2,1,0:T(8,128)}), f32[128,1,2,8,128]{4,3,2,1,0:T(8,128)S(1)}, u32[]{:S(2)}, u32[]{:S(2)}) async-start(f32[128,1,2,8,128]{4,3,2,1,0:T(8,128)} %select_select_fusion), calls=%async_computation | async-start | bytes 2097152 | tf_op jit(solution)/shard_map/all_to_all | solution.py:65
  19.5 0.1 collective-permute-start
  20.3 1.2 %collective-permute-done = f32[32,16,256]{2,1,0:T(8,128)S(1)} collective-permute-done((f32[32,16,256]{2,1,0:T(8,128)S(1)}, f32[32,16,256]{2,1,0:T(8,128)S(1)}, u32[]{:S(2)}, u32[]{:S(2)}) %collective-permute-start) | collective-permute-done | bytes 524320 | tf_op jit(solution)/shard_map/ppermute | solution.py:38
  21.5 0.1 broadcast_select_fusion.1
  21.7 0.2 fusion.15
  21.9 0.7 copy-done.4
  22.6 17.8 %fusion.2 = f32[512,64,48]{0,2,1:T(8,128)S(1)} fusion(s32[64,512]{1,0:T(8,128)S(1)} %bitcast.71, bf16[64,256,16]{1,2,0:T(8,128)(2,1)S(1)} %get-tuple-element.8, bf16[64,256,16]{1,2,0:T(8,128)(2,1)S(1)} %get-tuple-element.7, bf16[64,256,16]{1,2,0:T(8,128)(2,1)S(1)} %fusion.14), kind=kOutput, calls=%fused_computation.5 | convolution fusion | flops 818413568 | bytes 7995392 | tf_op jit(solution)/shard_map/mvk,mkd->vmd/dot_general | solution.py:23
  40.3 2.2 %multiply_reduce_fusion = (f32[512]{0:T(512)S(1)}, f32[512,64,16]{0,2,1:T(8,128)}) fusion(f32[512,64,48]{0,2,1:T(8,128)S(1)} %fusion.2), kind=kLoop, calls=%fused_computation.8 | loop fusion | flops 2096640 | bytes 8390656 | tf_op jit(solution)/shard_map/reduce_sum | solution.py:76
  42.5 8.4 %all-to-all-done = f32[128,1,2,8,128]{4,3,2,1,0:T(8,128)S(1)} async-done(((f32[128,1,2,8,128]{4,3,2,1,0:T(8,128)}), f32[128,1,2,8,128]{4,3,2,1,0:T(8,128)S(1)}, u32[]{:S(2)}, u32[]{:S(2)}) %all-to-all-start) | async-done | bytes 1048608 | tf_op jit(solution)/shard_map/all_to_all | solution.py:65
  50.9 0.5 fusion.13
  51.4 0.1 add.59
  51.6 1.5 %copy-done.1 = f32[512,64,16]{0,2,1:T(8,128)S(1)} copy-done((f32[512,64,16]{0,2,1:T(8,128)S(1)}, f32[512,64,16]{0,2,1:T(8,128)}, u32[]{:S(2)}) %copy-start.1) | copy-done | bytes 2097176
  53.1 1.2 %fusion.9 = f32[256,512]{1,0:T(8,128)S(1)} fusion(f32[512,1024]{0,1:T(8,128)S(1)} %bitcast.63, f32[32,8,8,128]{3,2,1,0:T(8,128)S(1)} %bitcast.64, f32[512]{0:T(512)S(1)} %get-tuple-element.5, f32[256]{0:T(256)S(1)} %add.59, pred[512]{0:T(512)(128)(4,1)S(1)} %iota_compare_fusion.9), kind=kOutput, calls=%fused_computation.16 | convolution fusion | flops 805830656 | bytes 3673600 | tf_op jit(solution)/shard_map/sf,vf->sv/dot_general | solution.py:77
  54.4 1.1 %stack_reshape.3 = f32[128,1,2,512]{3,2,0,1:T(2,128)} reshape(f32[256,512]{1,0:T(8,128)S(1)} %fusion.9) | data formatting | bytes 1048576 | tf_op jit(solution)/shard_map/stack;reshape | solution.py:84
  55.5 6.6 %all-to-all-start.1 = ((f32[128,1,2,512]{3,2,1,0:T(2,128)}), f32[128,1,2,512]{3,2,1,0:T(2,128)S(1)}, u32[]{:S(2)}, u32[]{:S(2)}) async-start(f32[128,1,2,512]{3,2,1,0:T(2,128)} %bitcast.19), calls=%async_computation.1 | async-start | bytes 1048576 | tf_op jit(solution)/shard_map/all_to_all | solution.py:85
  62.2 1.5 %gather_fusion.1 = s32[128]{0:T(128)S(1)} fusion(s32[4,128]{1,0:T(4,128)S(1)} %convert_subtract_fusion.1, s32[128]{0:T(128)S(1)} %reshape.764), kind=kCustom, calls=%fused_computation.1 | custom fusion | bytes 2048 | tf_op jit(solution)/shard_map/jit(take_along_axis)/gather | solution.py:51
  63.8 0.1 add.68
  63.9 17.4 %all-to-all-done.1 = f32[128,1,2,512]{3,2,1,0:T(2,128)S(1)} async-done(((f32[128,1,2,512]{3,2,1,0:T(2,128)}), f32[128,1,2,512]{3,2,1,0:T(2,128)S(1)}, u32[]{:S(2)}, u32[]{:S(2)}) %all-to-all-start.1) | async-done | bytes 524320 | tf_op jit(solution)/shard_map/all_to_all | solution.py:85
  81.4 0.4 reshape.753
  81.7 1.5 %gather_fusion = f32[128,512]{1,0:T(8,128)} fusion(f32[256,512]{1,0:T(8,128)S(1)} %reshape.753, s32[1024]{0:T(1024)S(1)} %pad_clamp_fusion), kind=kCustom, calls=%fused_computation | custom fusion | bytes 524800 | tf_op jit(solution)/shard_map/gather | solution.py:87
  (23 shorter events, 0.4 us)
Async XLA Ops:
  0.0 20.3 %copy-start = (f32[128,1024]{1,0:T(8,128)S(1)}, f32[128,1024]{1,0:T(8,128)}, u32[]{:S(2)}) copy-start(f32[128,1024]{1,0:T(8,128)} %param.8) | copy-start | bytes 1572868
  0.0 19.5 %copy-start.2 = (f32[32,16,256]{2,1,0:T(8,128)S(1)}, f32[32,16,256]{2,1,0:T(8,128)}, u32[]{:S(2)}) copy-start(f32[32,16,256]{2,1,0:T(8,128)} %param.9) | copy-start | bytes 1572868
  4.5 46.4 %all-to-all-start = ((f32[128,1,2,8,128]{4,3,2,1,0:T(8,128)}), f32[128,1,2,8,128]{4,3,2,1,0:T(8,128)S(1)}, u32[]{:S(2)}, u32[]{:S(2)}) async-start(f32[128,1,2,8,128]{4,3,2,1,0:T(8,128)} %select_select_fusion), calls=%async_computation | async-start | bytes 2097152 | tf_op jit(solution)/shard_map/all_to_all | solution.py:65
  19.5 2.0 %collective-permute-start = (f32[32,16,256]{2,1,0:T(8,128)S(1)}, f32[32,16,256]{2,1,0:T(8,128)S(1)}, u32[]{:S(2)}, u32[]{:S(2)}) collective-permute-start(f32[32,16,256]{2,1,0:T(8,128)S(1)} %copy-done.2), channel_id=1, source_target_pairs={{0,128},{128,0},{1,129},{129,1},{2,130},{130,2},{3,131},{131,3},{4... | collective-permute-start | bytes 1572872 | tf_op jit(solution)/shard_map/ppermute | solution.py:38
  21.6 0.9 %copy-start.4 = (s32[1,64,512]{2,1,0:T(8,128)S(1)}, s32[1,64,512]{2,1,0:T(8,128)}, u32[]{:S(2)}) copy-start(s32[1,64,512]{2,1,0:T(8,128)} %param.10) | copy-start | bytes 393220
  51.5 1.6 %copy-start.1 = (f32[512,64,16]{0,2,1:T(8,128)S(1)}, f32[512,64,16]{0,2,1:T(8,128)}, u32[]{:S(2)}) copy-start(f32[512,64,16]{0,2,1:T(8,128)} %get-tuple-element.6) | copy-start | bytes 6291460
  53.1 9.0 %copy-start.3 = (s32[4,32]{1,0:T(4,128)S(1)}, s32[4,32]{1,0:T(4,128)}, u32[]{:S(2)}) copy-start(s32[4,32]{1,0:T(4,128)} %param.7) | copy-start | bytes 1540
  55.5 25.9 %all-to-all-start.1 = ((f32[128,1,2,512]{3,2,1,0:T(2,128)}), f32[128,1,2,512]{3,2,1,0:T(2,128)S(1)}, u32[]{:S(2)}, u32[]{:S(2)}) async-start(f32[128,1,2,512]{3,2,1,0:T(2,128)} %bitcast.19), calls=%async_computation.1 | async-start | bytes 1048576 | tf_op jit(solution)/shard_map/all_to_all | solution.py:85

commit v6 on v5

--- a/solution.py
+++ b/solution.py
@@ -57,10 +57,10 @@
     for row in range(query_rows):
         here = contains[row][:, None] & (earlier_rows[row][:, None] == jnp.arange(slot_count)[None, :])
         row_at = jnp.where(here, row, row_at)
-    row_at = row_at[:, :, None, None]
-    outgoing = jnp.zeros((cell_count, slot_count, tile_rows, lanes), jnp.float32)
-    for row in range(query_rows):
-        outgoing = jnp.where(row_at == row, query_tiles[row][None, None], outgoing)
+    selector = (row_at[:, :, None] == jnp.arange(query_rows)[None, None, :]).astype(jnp.float32)
+    outgoing = jnp.einsum(
+        "ckr,rij->ckij", selector, query_tiles, precision=lax.Precision.HIGHEST
+    )
     outgoing = outgoing.reshape(list_size, cells_dev, slot_count, tile_rows, lanes)
     arrived = lax.all_to_all(outgoing, "list", split_axis=0, concat_axis=0, tiled=True)
 

time: 83.6 us -> 82.9 us (level)
  other arithmetic: 6.72 us -> 4.02 us
  matrix products: 19 us -> 20.4 us
    select_n x1, other arithmetic: 2.46 us -> 0.01 us  [body(): row_at = jnp.where(here, row, row_at)]
    reshape x0 -> x1, local copies, waits for them, and re-layouts: none -> 1.61 us  [body(): outgoing.reshape(list_size, cells_dev, slot_count, tile_rows, lanes)]
    dot_general x0 -> x1, matrix products: none -> 1.36 us  [body(): jnp.einsum('ckr,rij->ckij', selector, query_tiles, precision=lax.Precisio...]
    slice x1 -> x0, local copies, waits for them, and re-layouts: 0.89 us -> none  [body(): outgoing = jnp.where(row_at == row, query_tiles[row][None, None], outgoing)]
where the time goes in v6:
time: 82.9 us; the launch traced here: 82.6 us
  waiting for transfers between devices  27 us (33%)
  starting transfers between devices  21.7 us (26%)
  matrix products  20.4 us (25%)
  local copies, waits for them, and re-layouts  8.62 us (10%)
  other arithmetic  4.02 us (5%)
  between operations  0.84 us (1%)
    dot_general x1, matrix products, rebuilt_slots(): jnp.einsum('mvk,mkd->vmd', one_hot, parts, preferred_element_type=jnp.flo...  17.8 us
    all_to_all x1, waiting for transfers between devices, body(): lax.all_to_all(scored, 'list', split_axis=0, concat_axis=0, tiled=True)  17.4 us
    all_to_all x1, starting transfers between devices, body(): lax.all_to_all(outgoing, 'list', split_axis=0, concat_axis=0, tiled=True)  15 us
    all_to_all x1, waiting for transfers between devices, body(): lax.all_to_all(outgoing, 'list', split_axis=0, concat_axis=0, tiled=True)  8.36 us
    all_to_all x1, starting transfers between devices, body(): lax.all_to_all(scored, 'list', split_axis=0, concat_axis=0, tiled=True)  6.62 us
    reduce_sum x1, other arithmetic, body(): slot_norm = jnp.sum(rebuilt * rebuilt, axis=1)  2.21 us
    unnamed x10, local copies, waits for them, and re-layouts  2.18 us
    gather x3, local copies, waits for them, and re-layouts, body(): rank_of = jnp.take_along_axis(earlier_rows, probes, axis=1)  1.67 us
  transfers between devices with their start and end apart: 3, of which 3 were waited for; matrix products, arithmetic and copies ran while one was open for 27% of the time, Pallas kernels for 0%

profile of v6, /device:TPU:32, one launch (start us, length us, event | category | flops | bytes accessed | tf_op | source)
XLA Modules:
  0.0 82.6 jit_solution(16335934318026563725)
XLA Ops:
  0.0 0.8 %fusion.16 = pred[4,128]{1,0:T(4,128)(4,1)S(1)} fusion(s32[4,32]{1,0:T(4,128)} %param.7), kind=kLoop, calls=%fused_computation.32 | loop fusion | flops 32256 | bytes 1024 | tf_op jit(solution)/shard_map/reduce_or | solution.py:48
  0.9 1.4 %convolution_bitcast_fusion = f32[128,1,2,8,128]{4,0,3,2,1:T(8,128)S(1)} fusion(f32[4,1024]{1,0:T(4,128)} %param.6, s32[128,2]{0,1:T(2,128)S(1)} %and_select_fusion.3), kind=kOutput, calls=%fused_computation.14 | convolution fusion | flops 12583936 | bytes 1065984 | tf_op jit(solution)/shard_map/ckr,rij->ckij/dot_general | solution.py:61
  2.3 1.6 %copy.16 = f32[128,1,2,8,128]{4,3,2,1,0:T(8,128)} copy(f32[128,1,2,8,128]{4,0,3,2,1:T(8,128)S(1)} %convolution_bitcast_fusion) | data formatting | bytes 2097152 | tf_op jit(solution)/shard_map/reshape | solution.py:64
  3.9 15.0 %all-to-all-start = ((f32[128,1,2,8,128]{4,3,2,1,0:T(8,128)}), f32[128,1,2,8,128]{4,3,2,1,0:T(8,128)S(1)}, u32[]{:S(2)}, u32[]{:S(2)}) async-start(f32[128,1,2,8,128]{4,3,2,1,0:T(8,128)} %copy.16), calls=%async_computation | async-start | bytes 2097152 | tf_op jit(solution)/shard_map/all_to_all | solution.py:65
  18.9 0.1 collective-permute-start
  19.7 1.2 %collective-permute-done = f32[32,16,256]{2,1,0:T(8,128)S(1)} collective-permute-done((f32[32,16,256]{2,1,0:T(8,128)S(1)}, f32[32,16,256]{2,1,0:T(8,128)S(1)}, u32[]{:S(2)}, u32[]{:S(2)}) %collective-permute-start) | collective-permute-done | bytes 524320 | tf_op jit(solution)/shard_map/ppermute | solution.py:38
  20.9 0.1 broadcast_select_fusion.1
  21.1 0.2 fusion.15
  21.3 0.7 copy-done.4
  21.9 17.8 %fusion.2 = f32[512,64,48]{0,2,1:T(8,128)S(1)} fusion(s32[64,512]{1,0:T(8,128)S(1)} %bitcast.75, bf16[64,256,16]{1,2,0:T(8,128)(2,1)S(1)} %get-tuple-element.8, bf16[64,256,16]{1,2,0:T(8,128)(2,1)S(1)} %get-tuple-element.7, bf16[64,256,16]{1,2,0:T(8,128)(2,1)S(1)} %fusion.14), kind=kOutput, calls=%fused_computation.5 | convolution fusion | flops 818413568 | bytes 7995392 | tf_op jit(solution)/shard_map/mvk,mkd->vmd/dot_general | solution.py:23
  39.7 2.2 %multiply_reduce_fusion = (f32[512]{0:T(512)S(1)}, f32[512,64,16]{0,2,1:T(8,128)}) fusion(f32[512,64,48]{0,2,1:T(8,128)S(1)} %fusion.2), kind=kLoop, calls=%fused_computation.8 | loop fusion | flops 2096640 | bytes 8390656 | tf_op jit(solution)/shard_map/reduce_sum | solution.py:76
  41.9 8.4 %all-to-all-done = f32[128,1,2,8,128]{4,3,2,1,0:T(8,128)S(1)} async-done(((f32[128,1,2,8,128]{4,3,2,1,0:T(8,128)}), f32[128,1,2,8,128]{4,3,2,1,0:T(8,128)S(1)}, u32[]{:S(2)}, u32[]{:S(2)}) %all-to-all-start) | async-done | bytes 1048608 | tf_op jit(solution)/shard_map/all_to_all | solution.py:65
  50.3 0.5 fusion.13
  50.8 0.1 add.59
  51.0 1.5 %copy-done.1 = f32[512,64,16]{0,2,1:T(8,128)S(1)} copy-done((f32[512,64,16]{0,2,1:T(8,128)S(1)}, f32[512,64,16]{0,2,1:T(8,128)}, u32[]{:S(2)}) %copy-start.1) | copy-done | bytes 2097176
  52.5 1.2 %fusion.9 = f32[256,512]{1,0:T(8,128)S(1)} fusion(f32[512,1024]{0,1:T(8,128)S(1)} %bitcast.71, f32[32,8,8,128]{3,2,1,0:T(8,128)S(1)} %bitcast.72, f32[512]{0:T(512)S(1)} %get-tuple-element.5, f32[256]{0:T(256)S(1)} %add.59, pred[512]{0:T(512)(128)(4,1)S(1)} %iota_compare_fusion.6), kind=kOutput, calls=%fused_computation.17 | convolution fusion | flops 805830656 | bytes 3673600 | tf_op jit(solution)/shard_map/sf,vf->sv/dot_general | solution.py:77
  53.8 1.1 %stack_reshape.3 = f32[128,1,2,512]{3,2,0,1:T(2,128)} reshape(f32[256,512]{1,0:T(8,128)S(1)} %fusion.9) | data formatting | bytes 1048576 | tf_op jit(solution)/shard_map/stack;reshape | solution.py:84
  54.9 6.6 %all-to-all-start.1 = ((f32[128,1,2,512]{3,2,1,0:T(2,128)}), f32[128,1,2,512]{3,2,1,0:T(2,128)S(1)}, u32[]{:S(2)}, u32[]{:S(2)}) async-start(f32[128,1,2,512]{3,2,1,0:T(2,128)} %bitcast.20), calls=%async_computation.1 | async-start | bytes 1048576 | tf_op jit(solution)/shard_map/all_to_all | solution.py:85
  61.5 0.1 reshape.282
  61.6 1.5 %gather_fusion.1 = s32[128]{0:T(128)S(1)} fusion(s32[4,128]{1,0:T(4,128)S(1)} %convert_subtract_fusion.1, s32[128]{0:T(128)S(1)} %reshape.282), kind=kCustom, calls=%fused_computation.1 | custom fusion | bytes 2048 | tf_op jit(solution)/shard_map/jit(take_along_axis)/gather | solution.py:51
  63.2 0.1 add.68
  63.3 17.4 %all-to-all-done.1 = f32[128,1,2,512]{3,2,1,0:T(2,128)S(1)} async-done(((f32[128,1,2,512]{3,2,1,0:T(2,128)}), f32[128,1,2,512]{3,2,1,0:T(2,128)S(1)}, u32[]{:S(2)}, u32[]{:S(2)}) %all-to-all-start.1) | async-done | bytes 524320 | tf_op jit(solution)/shard_map/all_to_all | solution.py:85
  80.8 0.4 reshape.271
  81.1 1.5 %gather_fusion = f32[128,512]{1,0:T(8,128)} fusion(f32[256,512]{1,0:T(8,128)S(1)} %reshape.271, s32[1024]{0:T(1024)S(1)} %pad_clamp_fusion), kind=kCustom, calls=%fused_computation | custom fusion | bytes 524800 | tf_op jit(solution)/shard_map/gather | solution.py:87
  (23 shorter events, 0.4 us)
Async XLA Ops:
  0.0 19.7 %copy-start = (f32[128,1024]{1,0:T(8,128)S(1)}, f32[128,1024]{1,0:T(8,128)}, u32[]{:S(2)}) copy-start(f32[128,1024]{1,0:T(8,128)} %param.8) | copy-start | bytes 1572868
  2.3 16.6 %copy-start.2 = (f32[32,16,256]{2,1,0:T(8,128)S(1)}, f32[32,16,256]{2,1,0:T(8,128)}, u32[]{:S(2)}) copy-start(f32[32,16,256]{2,1,0:T(8,128)} %param.9) | copy-start | bytes 1572868
  3.9 46.4 %all-to-all-start = ((f32[128,1,2,8,128]{4,3,2,1,0:T(8,128)}), f32[128,1,2,8,128]{4,3,2,1,0:T(8,128)S(1)}, u32[]{:S(2)}, u32[]{:S(2)}) async-start(f32[128,1,2,8,128]{4,3,2,1,0:T(8,128)} %copy.16), calls=%async_computation | async-start | bytes 2097152 | tf_op jit(solution)/shard_map/all_to_all | solution.py:65
  18.9 2.0 %collective-permute-start = (f32[32,16,256]{2,1,0:T(8,128)S(1)}, f32[32,16,256]{2,1,0:T(8,128)S(1)}, u32[]{:S(2)}, u32[]{:S(2)}) collective-permute-start(f32[32,16,256]{2,1,0:T(8,128)S(1)} %copy-done.2), channel_id=1, source_target_pairs={{0,128},{128,0},{1,129},{129,1},{2,130},{130,2},{3,131},{131,3},{4... | collective-permute-start | bytes 1572872 | tf_op jit(solution)/shard_map/ppermute | solution.py:38
  21.0 0.9 %copy-start.4 = (s32[1,64,512]{2,1,0:T(8,128)S(1)}, s32[1,64,512]{2,1,0:T(8,128)}, u32[]{:S(2)}) copy-start(s32[1,64,512]{2,1,0:T(8,128)} %param.10) | copy-start | bytes 393220
  50.9 1.6 %copy-start.1 = (f32[512,64,16]{0,2,1:T(8,128)S(1)}, f32[512,64,16]{0,2,1:T(8,128)}, u32[]{:S(2)}) copy-start(f32[512,64,16]{0,2,1:T(8,128)} %get-tuple-element.6) | copy-start | bytes 6291460
  52.5 9.0 %copy-start.3 = (s32[4,32]{1,0:T(4,128)S(1)}, s32[4,32]{1,0:T(4,128)}, u32[]{:S(2)}) copy-start(s32[4,32]{1,0:T(4,128)} %param.7) | copy-start | bytes 1540
  54.9 25.9 %all-to-all-start.1 = ((f32[128,1,2,512]{3,2,1,0:T(2,128)}), f32[128,1,2,512]{3,2,1,0:T(2,128)S(1)}, u32[]{:S(2)}, u32[]{:S(2)}) async-start(f32[128,1,2,512]{3,2,1,0:T(2,128)} %bitcast.20), calls=%async_computation.1 | async-start | bytes 1048576 | tf_op jit(solution)/shard_map/all_to_all | solution.py:85

commit v7 on v6

--- a/solution.py
+++ b/solution.py
@@ -57,10 +57,10 @@
     for row in range(query_rows):
         here = contains[row][:, None] & (earlier_rows[row][:, None] == jnp.arange(slot_count)[None, :])
         row_at = jnp.where(here, row, row_at)
-    selector = (row_at[:, :, None] == jnp.arange(query_rows)[None, None, :]).astype(jnp.float32)
-    outgoing = jnp.einsum(
-        "ckr,rij->ckij", selector, query_tiles, precision=lax.Precision.HIGHEST
+    tile_table = jnp.concatenate(
+        [query_tiles, jnp.zeros((1, tile_rows, lanes), jnp.float32)], axis=0
     )
+    outgoing = tile_table[jnp.where(row_at >= 0, row_at, query_rows)]
     outgoing = outgoing.reshape(list_size, cells_dev, slot_count, tile_rows, lanes)
     arrived = lax.all_to_all(outgoing, "list", split_axis=0, concat_axis=0, tiled=True)
 

time: 82.9 us -> 83.1 us (level)
  matrix products: 20.4 us -> 19 us
  local copies, waits for them, and re-layouts: 8.62 us -> 9.89 us
    gather x0 -> x1, local copies, waits for them, and re-layouts: none -> 2.02 us  [body(): outgoing = tile_table[jnp.where(row_at >= 0, row_at, query_rows)]]
    reshape x1 -> x0, local copies, waits for them, and re-layouts: 1.61 us -> none  [body(): outgoing.reshape(list_size, cells_dev, slot_count, tile_rows, lanes)]
    dot_general x1 -> x0, matrix products: 1.36 us -> none  [body(): jnp.einsum('ckr,rij->ckij', selector, query_tiles, precision=lax.Precisio...]
    unnamed x10 -> x11, local copies, waits for them, and re-layouts: 2.18 us -> 2.9 us
where the time goes in v7:
time: 83.1 us; the launch traced here: 82.7 us
  waiting for transfers between devices  27 us (32%)
  starting transfers between devices  21.7 us (26%)
  matrix products  19 us (23%)
  local copies, waits for them, and re-layouts  9.89 us (12%)
  other arithmetic  4.22 us (5%)
  between operations  0.86 us (1%)
    dot_general x1, matrix products, rebuilt_slots(): jnp.einsum('mvk,mkd->vmd', one_hot, parts, preferred_element_type=jnp.flo...  17.8 us
    all_to_all x1, waiting for transfers between devices, body(): lax.all_to_all(scored, 'list', split_axis=0, concat_axis=0, tiled=True)  17.4 us
    all_to_all x1, starting transfers between devices, body(): lax.all_to_all(outgoing, 'list', split_axis=0, concat_axis=0, tiled=True)  15 us
    all_to_all x1, waiting for transfers between devices, body(): lax.all_to_all(outgoing, 'list', split_axis=0, concat_axis=0, tiled=True)  8.36 us
    all_to_all x1, starting transfers between devices, body(): lax.all_to_all(scored, 'list', split_axis=0, concat_axis=0, tiled=True)  6.62 us
    unnamed x11, local copies, waits for them, and re-layouts  2.9 us
    reduce_sum x1, other arithmetic, body(): slot_norm = jnp.sum(rebuilt * rebuilt, axis=1)  2.21 us
    gather x1, local copies, waits for them, and re-layouts, body(): outgoing = tile_table[jnp.where(row_at >= 0, row_at, query_rows)]  2.02 us
  transfers between devices with their start and end apart: 3, of which 3 were waited for; matrix products, arithmetic and copies ran while one was open for 27% of the time, Pallas kernels for 0%

profile of v7, /device:TPU:32, one launch (start us, length us, event | category | flops | bytes accessed | tf_op | source)
XLA Modules:
  0.0 82.7 jit_solution(18102921855202567170)
XLA Ops:
  0.0 0.8 %fusion.16 = pred[4,128]{1,0:T(4,128)(4,1)S(1)} fusion(s32[4,32]{1,0:T(4,128)} %param.7), kind=kLoop, calls=%fused_computation.38 | loop fusion | flops 32256 | bytes 1024 | tf_op jit(solution)/shard_map/reduce_or | solution.py:48
  0.9 0.7 copy.16
  1.6 0.2 compare_select_fusion
  1.9 0.1 reshape.375
  2.0 2.0 %gather_fusion = f32[256,8,128]{2,1,0:T(8,128)} fusion(f32[5,8,128]{2,1,0:T(8,128)S(1)} %concatenate.9, s32[1024]{0:T(1024)S(1)} %pad_clamp_fusion.1), kind=kCustom, calls=%fused_computation | custom fusion | bytes 2098176 | tf_op jit(solution)/shard_map/gather | solution.py:63
  4.1 15.0 %all-to-all-start = ((f32[128,1,2,8,128]{4,3,2,1,0:T(8,128)}), f32[128,1,2,8,128]{4,3,2,1,0:T(8,128)S(1)}, u32[]{:S(2)}, u32[]{:S(2)}) async-start(f32[128,1,2,8,128]{4,3,2,1,0:T(8,128)} %bitcast.9), calls=%async_computation | async-start | bytes 2097152 | tf_op jit(solution)/shard_map/all_to_all | solution.py:65
  19.1 0.1 collective-permute-start
  19.9 1.2 %collective-permute-done = f32[32,16,256]{2,1,0:T(8,128)S(1)} collective-permute-done((f32[32,16,256]{2,1,0:T(8,128)S(1)}, f32[32,16,256]{2,1,0:T(8,128)S(1)}, u32[]{:S(2)}, u32[]{:S(2)}) %collective-permute-start) | collective-permute-done | bytes 524320 | tf_op jit(solution)/shard_map/ppermute | solution.py:38
  21.1 0.1 broadcast_select_fusion.1
  21.3 0.2 fusion.15
  21.4 0.7 copy-done.4
  22.1 17.8 %fusion.2 = f32[512,64,48]{0,2,1:T(8,128)S(1)} fusion(s32[64,512]{1,0:T(8,128)S(1)} %bitcast.72, bf16[64,256,16]{1,2,0:T(8,128)(2,1)S(1)} %get-tuple-element.8, bf16[64,256,16]{1,2,0:T(8,128)(2,1)S(1)} %get-tuple-element.7, bf16[64,256,16]{1,2,0:T(8,128)(2,1)S(1)} %fusion.14), kind=kOutput, calls=%fused_computation.6 | convolution fusion | flops 818413568 | bytes 7995392 | tf_op jit(solution)/shard_map/mvk,mkd->vmd/dot_general | solution.py:23
  39.9 2.2 %multiply_reduce_fusion = (f32[512]{0:T(512)S(1)}, f32[512,64,16]{0,2,1:T(8,128)}) fusion(f32[512,64,48]{0,2,1:T(8,128)S(1)} %fusion.2), kind=kLoop, calls=%fused_computation.9 | loop fusion | flops 2096640 | bytes 8390656 | tf_op jit(solution)/shard_map/reduce_sum | solution.py:76
  42.1 8.4 %all-to-all-done = f32[128,1,2,8,128]{4,3,2,1,0:T(8,128)S(1)} async-done(((f32[128,1,2,8,128]{4,3,2,1,0:T(8,128)}), f32[128,1,2,8,128]{4,3,2,1,0:T(8,128)S(1)}, u32[]{:S(2)}, u32[]{:S(2)}) %all-to-all-start) | async-done | bytes 1048608 | tf_op jit(solution)/shard_map/all_to_all | solution.py:65
  50.4 0.5 fusion.13
  50.9 0.1 add.76
  51.1 1.5 %copy-done.1 = f32[512,64,16]{0,2,1:T(8,128)S(1)} copy-done((f32[512,64,16]{0,2,1:T(8,128)S(1)}, f32[512,64,16]{0,2,1:T(8,128)}, u32[]{:S(2)}) %copy-start.1) | copy-done | bytes 2097176
  52.7 1.2 %fusion.9 = f32[256,512]{1,0:T(8,128)S(1)} fusion(f32[512,1024]{0,1:T(8,128)S(1)} %bitcast.66, f32[32,8,8,128]{3,2,1,0:T(8,128)S(1)} %bitcast.67, f32[512]{0:T(512)S(1)} %get-tuple-element.5, f32[256]{0:T(256)S(1)} %add.76, pred[512]{0:T(512)(128)(4,1)S(1)} %iota_compare_fusion.9), kind=kOutput, calls=%fused_computation.17 | convolution fusion | flops 805830656 | bytes 3673600 | tf_op jit(solution)/shard_map/sf,vf->sv/dot_general | solution.py:77
  53.9 1.1 %stack_reshape.3 = f32[128,1,2,512]{3,2,0,1:T(2,128)} reshape(f32[256,512]{1,0:T(8,128)S(1)} %fusion.9) | data formatting | bytes 1048576 | tf_op jit(solution)/shard_map/stack;reshape | solution.py:84
  55.0 6.6 %all-to-all-start.1 = ((f32[128,1,2,512]{3,2,1,0:T(2,128)}), f32[128,1,2,512]{3,2,1,0:T(2,128)S(1)}, u32[]{:S(2)}, u32[]{:S(2)}) async-start(f32[128,1,2,512]{3,2,1,0:T(2,128)} %bitcast.16), calls=%async_computation.1 | async-start | bytes 1048576 | tf_op jit(solution)/shard_map/all_to_all | solution.py:85
  61.7 1.5 %gather_fusion.2 = s32[128]{0:T(128)S(1)} fusion(s32[4,128]{1,0:T(4,128)S(1)} %convert_subtract_fusion.1, s32[128]{0:T(128)S(1)} %reshape.389), kind=kCustom, calls=%fused_computation.2 | custom fusion | bytes 2048 | tf_op jit(solution)/shard_map/jit(take_along_axis)/gather | solution.py:51
  63.4 17.4 %all-to-all-done.1 = f32[128,1,2,512]{3,2,1,0:T(2,128)S(1)} async-done(((f32[128,1,2,512]{3,2,1,0:T(2,128)}), f32[128,1,2,512]{3,2,1,0:T(2,128)S(1)}, u32[]{:S(2)}, u32[]{:S(2)}) %all-to-all-start.1) | async-done | bytes 524320 | tf_op jit(solution)/shard_map/all_to_all | solution.py:85
  80.9 0.4 reshape.370
  81.2 1.5 %gather_fusion.1 = f32[128,512]{1,0:T(8,128)} fusion(f32[256,512]{1,0:T(8,128)S(1)} %reshape.370, s32[1024]{0:T(1024)S(1)} %pad_clamp_fusion), kind=kCustom, calls=%fused_computation.1 | custom fusion | bytes 524800 | tf_op jit(solution)/shard_map/gather | solution.py:87
  (26 shorter events, 0.5 us)
Async XLA Ops:
  0.0 19.8 %copy-start = (f32[128,1024]{1,0:T(8,128)S(1)}, f32[128,1024]{1,0:T(8,128)}, u32[]{:S(2)}) copy-start(f32[128,1024]{1,0:T(8,128)} %param.8) | copy-start | bytes 1572868
  2.0 17.0 %copy-start.2 = (f32[32,16,256]{2,1,0:T(8,128)S(1)}, f32[32,16,256]{2,1,0:T(8,128)}, u32[]{:S(2)}) copy-start(f32[32,16,256]{2,1,0:T(8,128)} %param.9) | copy-start | bytes 1572868
  4.1 46.4 %all-to-all-start = ((f32[128,1,2,8,128]{4,3,2,1,0:T(8,128)}), f32[128,1,2,8,128]{4,3,2,1,0:T(8,128)S(1)}, u32[]{:S(2)}, u32[]{:S(2)}) async-start(f32[128,1,2,8,128]{4,3,2,1,0:T(8,128)} %bitcast.9), calls=%async_computation | async-start | bytes 2097152 | tf_op jit(solution)/shard_map/all_to_all | solution.py:65
  19.1 2.0 %collective-permute-start = (f32[32,16,256]{2,1,0:T(8,128)S(1)}, f32[32,16,256]{2,1,0:T(8,128)S(1)}, u32[]{:S(2)}, u32[]{:S(2)}) collective-permute-start(f32[32,16,256]{2,1,0:T(8,128)S(1)} %copy-done.2), channel_id=1, source_target_pairs={{0,128},{128,0},{1,129},{129,1},{2,130},{130,2},{3,131},{131,3},{4... | collective-permute-start | bytes 1572872 | tf_op jit(solution)/shard_map/ppermute | solution.py:38
  21.2 0.9 %copy-start.4 = (s32[1,64,512]{2,1,0:T(8,128)S(1)}, s32[1,64,512]{2,1,0:T(8,128)}, u32[]{:S(2)}) copy-start(s32[1,64,512]{2,1,0:T(8,128)} %param.10) | copy-start | bytes 393220
  51.1 1.6 %copy-start.1 = (f32[512,64,16]{0,2,1:T(8,128)S(1)}, f32[512,64,16]{0,2,1:T(8,128)}, u32[]{:S(2)}) copy-start(f32[512,64,16]{0,2,1:T(8,128)} %get-tuple-element.6) | copy-start | bytes 6291460
  52.7 9.0 %copy-start.3 = (s32[4,32]{1,0:T(4,128)S(1)}, s32[4,32]{1,0:T(4,128)}, u32[]{:S(2)}) copy-start(s32[4,32]{1,0:T(4,128)} %param.7) | copy-start | bytes 1540
  55.0 25.9 %all-to-all-start.1 = ((f32[128,1,2,512]{3,2,1,0:T(2,128)}), f32[128,1,2,512]{3,2,1,0:T(2,128)S(1)}, u32[]{:S(2)}, u32[]{:S(2)}) async-start(f32[128,1,2,512]{3,2,1,0:T(2,128)} %bitcast.16), calls=%async_computation.1 | async-start | bytes 1048576 | tf_op jit(solution)/shard_map/all_to_all | solution.py:85

commit v8 on v6

--- a/solution.py
+++ b/solution.py
@@ -70,21 +70,21 @@
     for local in range(cells_dev):
         centroid = lax.dynamic_slice_in_dim(centroids, first_cell + local, 1, axis=0)
         residual = arrived[:, local] - centroid.reshape(1, 1, tile_rows, lanes)
-        own_norm = jnp.sum(residual * residual, axis=(2, 3)).reshape(-1)
-        residual = residual.reshape(list_size * slot_count, dim)
+        own_norm = jnp.sum(residual * residual, axis=(2, 3))
         rebuilt = rebuilt_slots(codebook_all, codes[local])
         slot_norm = jnp.sum(rebuilt * rebuilt, axis=1)
         cross = jnp.einsum(
-            "sf,vf->sv", residual, rebuilt, precision=lax.Precision.HIGH
+            "skij,vij->skv", residual, rebuilt.reshape(capacity, tile_rows, lanes),
+            precision=lax.Precision.HIGH,
         )
-        total = (own_norm[:, None] + slot_norm[None, :]) - 2.0 * cross
+        total = (own_norm[:, :, None] + slot_norm[None, None, :]) - 2.0 * cross
         valid = positions < cell_sizes[local]
-        total = jnp.where(valid[None, :], total, jnp.zeros((), jnp.float32))
-        scored.append(total.reshape(list_size, slot_count, capacity))
+        total = jnp.where(valid[None, None, :], total, jnp.zeros((), jnp.float32))
+        scored.append(total)
     scored = jnp.stack(scored, axis=1)
     returned = lax.all_to_all(scored, "list", split_axis=0, concat_axis=0, tiled=True)
-    returned = returned.reshape(cell_count * slot_count, capacity)
-    result = returned[flat_cells * slot_count + slot_rank]
+    returned = returned.reshape(cell_count, slot_count, capacity)
+    result = returned[flat_cells, slot_rank]
     return result.reshape(query_rows, probe_count, capacity)
 
 

time: 82.9 us -> 83.1 us (level)
  no operation moved by 1% of the time
where the time goes in v8:
time: 83.1 us; the launch traced here: 82.7 us
  waiting for transfers between devices  26.9 us (32%)
  starting transfers between devices  21.7 us (26%)
  matrix products  20.5 us (25%)
  local copies, waits for them, and re-layouts  8.69 us (10%)
  other arithmetic  4.03 us (5%)
    dot_general x1, matrix products, rebuilt_slots(): jnp.einsum('mvk,mkd->vmd', one_hot, parts, preferred_element_type=jnp.flo...  17.8 us
    all_to_all x1, waiting for transfers between devices, body(): lax.all_to_all(scored, 'list', split_axis=0, concat_axis=0, tiled=True)  17.4 us
    all_to_all x1, starting transfers between devices, body(): lax.all_to_all(outgoing, 'list', split_axis=0, concat_axis=0, tiled=True)  15 us
    all_to_all x1, waiting for transfers between devices, body(): lax.all_to_all(outgoing, 'list', split_axis=0, concat_axis=0, tiled=True)  8.36 us
    all_to_all x1, starting transfers between devices, body(): lax.all_to_all(scored, 'list', split_axis=0, concat_axis=0, tiled=True)  6.62 us
    reduce_sum x1, other arithmetic, body(): slot_norm = jnp.sum(rebuilt * rebuilt, axis=1)  2.21 us
    unnamed x10, local copies, waits for them, and re-layouts  2.19 us
    gather x1, local copies, waits for them, and re-layouts, body(): result = returned[flat_cells, slot_rank]  1.76 us
  transfers between devices with their start and end apart: 3, of which 3 were waited for; matrix products, arithmetic and copies ran while one was open for 27% of the time, Pallas kernels for 0%

profile of v8, /device:TPU:32, one launch (start us, length us, event | category | flops | bytes accessed | tf_op | source)
XLA Modules:
  0.0 82.7 jit_solution(9449904150384501842)
XLA Ops:
  0.0 0.8 %fusion.17 = pred[4,128]{1,0:T(4,128)(4,1)S(1)} fusion(s32[4,32]{1,0:T(4,128)} %param.7), kind=kLoop, calls=%fused_computation.33 | loop fusion | flops 32256 | bytes 1024 | tf_op jit(solution)/shard_map/reduce_or | solution.py:48
  0.9 1.4 %convolution_bitcast_fusion = f32[128,1,2,8,128]{4,0,3,2,1:T(8,128)S(1)} fusion(f32[4,1024]{1,0:T(4,128)} %param.6, s32[128,2]{0,1:T(2,128)S(1)} %and_select_fusion.4), kind=kOutput, calls=%fused_computation.14 | convolution fusion | flops 12583936 | bytes 1065984 | tf_op jit(solution)/shard_map/ckr,rij->ckij/dot_general | solution.py:61
  2.3 1.6 %copy.25 = f32[128,1,2,8,128]{4,3,2,1,0:T(8,128)} copy(f32[128,1,2,8,128]{4,0,3,2,1:T(8,128)S(1)} %convolution_bitcast_fusion) | data formatting | bytes 2097152 | tf_op jit(solution)/shard_map/reshape | solution.py:64
  3.9 15.0 %all-to-all-start = ((f32[128,1,2,8,128]{4,3,2,1,0:T(8,128)}), f32[128,1,2,8,128]{4,3,2,1,0:T(8,128)S(1)}, u32[]{:S(2)}, u32[]{:S(2)}) async-start(f32[128,1,2,8,128]{4,3,2,1,0:T(8,128)} %copy.25), calls=%async_computation | async-start | bytes 2097152 | tf_op jit(solution)/shard_map/all_to_all | solution.py:65
  18.9 0.1 collective-permute-start
  19.7 1.2 %collective-permute-done = f32[32,16,256]{2,1,0:T(8,128)S(1)} collective-permute-done((f32[32,16,256]{2,1,0:T(8,128)S(1)}, f32[32,16,256]{2,1,0:T(8,128)S(1)}, u32[]{:S(2)}, u32[]{:S(2)}) %collective-permute-start) | collective-permute-done | bytes 524320 | tf_op jit(solution)/shard_map/ppermute | solution.py:38
  20.9 0.1 broadcast_select_fusion.1
  21.1 0.2 fusion.16
  21.3 0.7 copy-done.4
  21.9 17.8 %fusion.2 = f32[512,64,48]{0,2,1:T(8,128)S(1)} fusion(s32[64,512]{1,0:T(8,128)S(1)} %bitcast.87, bf16[64,256,16]{1,2,0:T(8,128)(2,1)S(1)} %get-tuple-element.8, bf16[64,256,16]{1,2,0:T(8,128)(2,1)S(1)} %get-tuple-element.7, bf16[64,256,16]{1,2,0:T(8,128)(2,1)S(1)} %fusion.15), kind=kOutput, calls=%fused_computation.5 | convolution fusion | flops 818413568 | bytes 7995392 | tf_op jit(solution)/shard_map/mvk,mkd->vmd/dot_general | solution.py:23
  39.7 2.2 %multiply_reduce_fusion = (f32[512]{0:T(512)S(1)}, f32[512,64,16]{0,2,1:T(8,128)}) fusion(f32[512,64,48]{0,2,1:T(8,128)S(1)} %fusion.2), kind=kLoop, calls=%fused_computation.8 | loop fusion | flops 2096640 | bytes 8390656 | tf_op jit(solution)/shard_map/reduce_sum | solution.py:75
  41.9 8.4 %all-to-all-done = f32[128,1,2,8,128]{4,3,2,1,0:T(8,128)S(1)} async-done(((f32[128,1,2,8,128]{4,3,2,1,0:T(8,128)}), f32[128,1,2,8,128]{4,3,2,1,0:T(8,128)S(1)}, u32[]{:S(2)}, u32[]{:S(2)}) %all-to-all-start) | async-done | bytes 1048608 | tf_op jit(solution)/shard_map/all_to_all | solution.py:65
  50.3 0.5 fusion.13
  50.8 0.1 subtract_bitcast_fusion
  50.9 1.5 %copy-done.1 = f32[512,64,16]{0,2,1:T(8,128)S(1)} copy-done((f32[512,64,16]{0,2,1:T(8,128)S(1)}, f32[512,64,16]{0,2,1:T(8,128)}, u32[]{:S(2)}) %copy-start.1) | copy-done | bytes 2097176
  52.5 1.4 %fusion.11 = f32[128,1,2,512]{3,0,2,1:T(8,128)S(1)} fusion(f32[512,8,128,1]{0,2,1,3:T(8,128)S(1)} %bitcast.84, f32[128,2,8,128]{3,2,1,0:T(8,128)S(1)} %subtract_bitcast_fusion, f32[512]{0:T(512)S(1)} %get-tuple-element.5, f32[128,2]{0,1:T(2,128)S(1)} %copy.26, pred[512]{0:T(512)(128)(4,1)S(1)} %iota_compare_fusion.6), kind=kOutput, calls=%fused_computation.19 | convolution fusion | flops 805830656 | bytes 3673600 | tf_op jit(solution)/shard_map/skij,vij->skv/dot_general | solution.py:76
  53.9 1.2 %copy.29 = f32[128,1,2,512]{3,2,1,0:T(2,128)} copy(f32[128,1,2,512]{3,0,2,1:T(8,128)S(1)} %fusion.11) | data formatting | bytes 1048576 | tf_op jit(solution)/shard_map/stack | solution.py:84
  55.1 6.6 %all-to-all-start.1 = ((f32[128,1,2,512]{3,2,1,0:T(2,128)}), f32[128,1,2,512]{3,2,1,0:T(2,128)S(1)}, u32[]{:S(2)}, u32[]{:S(2)}) async-start(f32[128,1,2,512]{3,2,1,0:T(2,128)} %copy.29), calls=%async_computation.1 | async-start | bytes 1048576 | tf_op jit(solution)/shard_map/all_to_all | solution.py:85
  61.7 0.1 reshape.274
  61.8 0.1 reshape.283
  61.9 1.5 %gather_fusion.1 = s32[128]{0:T(128)S(1)} fusion(s32[4,128]{1,0:T(4,128)S(1)} %convert_subtract_fusion.1, s32[128]{0:T(128)S(1)} %reshape.283), kind=kCustom, calls=%fused_computation.1 | custom fusion | bytes 2048 | tf_op jit(solution)/shard_map/jit(take_along_axis)/gather | solution.py:51
  63.5 0.1 select_n.99
  63.6 17.4 %all-to-all-done.1 = f32[128,1,2,512]{3,2,1,0:T(2,128)S(1)} async-done(((f32[128,1,2,512]{3,2,1,0:T(2,128)}), f32[128,1,2,512]{3,2,1,0:T(2,128)S(1)}, u32[]{:S(2)}, u32[]{:S(2)}) %all-to-all-start.1) | async-done | bytes 524320 | tf_op jit(solution)/shard_map/all_to_all | solution.py:85
  81.0 1.8 %gather_fusion = f32[128,512]{1,0:T(8,128)} fusion(f32[128,2,512]{2,1,0:T(2,128)S(1)} %bitcast.83, s32[128]{0:T(128)S(1)} %fusion.27), kind=kCustom, calls=%fused_computation | custom fusion | bytes 525312 | tf_op jit(solution)/shard_map/gather | solution.py:87
  (22 shorter events, 0.3 us)
Async XLA Ops:
  0.0 19.7 %copy-start = (f32[128,1024]{1,0:T(8,128)S(1)}, f32[128,1024]{1,0:T(8,128)}, u32[]{:S(2)}) copy-start(f32[128,1024]{1,0:T(8,128)} %param.8) | copy-start | bytes 1572868
  2.3 16.6 %copy-start.2 = (f32[32,16,256]{2,1,0:T(8,128)S(1)}, f32[32,16,256]{2,1,0:T(8,128)}, u32[]{:S(2)}) copy-start(f32[32,16,256]{2,1,0:T(8,128)} %param.9) | copy-start | bytes 1572868
  3.9 46.4 %all-to-all-start = ((f32[128,1,2,8,128]{4,3,2,1,0:T(8,128)}), f32[128,1,2,8,128]{4,3,2,1,0:T(8,128)S(1)}, u32[]{:S(2)}, u32[]{:S(2)}) async-start(f32[128,1,2,8,128]{4,3,2,1,0:T(8,128)} %copy.25), calls=%async_computation | async-start | bytes 2097152 | tf_op jit(solution)/shard_map/all_to_all | solution.py:65
  18.9 2.0 %collective-permute-start = (f32[32,16,256]{2,1,0:T(8,128)S(1)}, f32[32,16,256]{2,1,0:T(8,128)S(1)}, u32[]{:S(2)}, u32[]{:S(2)}) collective-permute-start(f32[32,16,256]{2,1,0:T(8,128)S(1)} %copy-done.2), channel_id=1, source_target_pairs={{0,128},{128,0},{1,129},{129,1},{2,130},{130,2},{3,131},{131,3},{4... | collective-permute-start | bytes 1572872 | tf_op jit(solution)/shard_map/ppermute | solution.py:38
  21.0 0.9 %copy-start.4 = (s32[1,64,512]{2,1,0:T(8,128)S(1)}, s32[1,64,512]{2,1,0:T(8,128)}, u32[]{:S(2)}) copy-start(s32[1,64,512]{2,1,0:T(8,128)} %param.10) | copy-start | bytes 393220
  50.8 1.6 %copy-start.1 = (f32[512,64,16]{0,2,1:T(8,128)S(1)}, f32[512,64,16]{0,2,1:T(8,128)}, u32[]{:S(2)}) copy-start(f32[512,64,16]{0,2,1:T(8,128)} %get-tuple-element.6) | copy-start | bytes 6291460
  52.5 9.2 %copy-start.3 = (s32[4,32]{1,0:T(4,128)S(1)}, s32[4,32]{1,0:T(4,128)}, u32[]{:S(2)}) copy-start(s32[4,32]{1,0:T(4,128)} %param.7) | copy-start | bytes 1540
  55.1 25.9 %all-to-all-start.1 = ((f32[128,1,2,512]{3,2,1,0:T(2,128)}), f32[128,1,2,512]{3,2,1,0:T(2,128)S(1)}, u32[]{:S(2)}, u32[]{:S(2)}) async-start(f32[128,1,2,512]{3,2,1,0:T(2,128)} %copy.29), calls=%async_computation.1 | async-start | bytes 1048576 | tf_op jit(solution)/shard_map/all_to_all | solution.py:85

commit v9 on v6

--- a/solution.py
+++ b/solution.py
@@ -17,14 +17,19 @@
 def rebuilt_slots(codebook_all, cell_codes):
     subspaces, sub_width, codewords = codebook_all.shape
     capacity = cell_codes.shape[1]
-    parts = exact_parts(jnp.transpose(codebook_all, (0, 2, 1)))
+    word_norm = jnp.sum(codebook_all * codebook_all, axis=1)
+    columns = jnp.concatenate(
+        [jnp.transpose(codebook_all, (0, 2, 1)), word_norm[:, :, None]], axis=-1
+    )
+    parts = exact_parts(columns)
+    width = sub_width + 1
     word_ids = jnp.arange(codewords, dtype=jnp.int32)
     one_hot = (cell_codes[:, :, None] == word_ids[None, None, :]).astype(jnp.bfloat16)
     picked = jnp.einsum("mvk,mkd->vmd", one_hot, parts, preferred_element_type=jnp.float32)
-    rebuilt = (
-        picked[..., :sub_width] + picked[..., sub_width : 2 * sub_width]
-    ) + picked[..., 2 * sub_width :]
-    return rebuilt.reshape(capacity, subspaces * sub_width)
+    joined = (picked[..., :width] + picked[..., width : 2 * width]) + picked[..., 2 * width :]
+    rebuilt = joined[..., :sub_width].reshape(capacity, subspaces * sub_width)
+    slot_norm = jnp.sum(joined[..., sub_width], axis=1)
+    return rebuilt, slot_norm
 
 
 def body(queries, probes, centroids, codebook, codes, cell_sizes):
@@ -72,8 +77,7 @@
         residual = arrived[:, local] - centroid.reshape(1, 1, tile_rows, lanes)
         own_norm = jnp.sum(residual * residual, axis=(2, 3)).reshape(-1)
         residual = residual.reshape(list_size * slot_count, dim)
-        rebuilt = rebuilt_slots(codebook_all, codes[local])
-        slot_norm = jnp.sum(rebuilt * rebuilt, axis=1)
+        rebuilt, slot_norm = rebuilt_slots(codebook_all, codes[local])
         cross = jnp.einsum(
             "sf,vf->sv", residual, rebuilt, precision=lax.Precision.HIGH
         )

time: 82.9 us -> 83.8 us (1.011)
  waiting for transfers between devices: 27 us -> 25.5 us
  local copies, waits for them, and re-layouts: 8.62 us -> 9.83 us
  matrix products: 20.4 us -> 21.4 us
    reduce_sum x1, other arithmetic: 2.21 us -> 0.11 us  [rebuilt_slots(): slot_norm = jnp.sum(joined[..., sub_width], axis=1)]
    add x0 -> x1, other arithmetic: none -> 1.85 us  [rebuilt_slots(): picked[..., :width] + picked[..., width:2 * width] + picked[..., 2 * width:]]
    slice x0 -> x2, local copies, waits for them, and re-layouts: none -> 1.5 us  [rebuilt_slots(): rebuilt = joined[..., :sub_width].reshape(capacity, subspaces * sub_width)]
    ppermute x1, waiting for transfers between devices: 1.2 us -> 0.01 us  [body(): other = lax.ppermute(codebook, 'query', [(0, 1), (1, 0)])]
    dot_general x1, matrix products: 17.8 us -> 18.7 us  [rebuilt_slots(): jnp.einsum('mvk,mkd->vmd', one_hot, parts, preferred_element_type=jnp.flo...]
  transfers between devices with their start and end apart: 3 -> 3, of which waited for: 3 -> 2; matrix products, arithmetic and copies ran while one was open for 27% -> 33% of each run, Pallas kernels for 0% -> 0%
where the time goes in v9:
time: 83.8 us; the launch traced here: 83.4 us
  waiting for transfers between devices  25.5 us (30%)
  starting transfers between devices  21.6 us (26%)
  matrix products  21.4 us (26%)
  local copies, waits for them, and re-layouts  9.83 us (12%)
  other arithmetic  4.19 us (5%)
  between operations  0.88 us (1%)
    dot_general x1, matrix products, rebuilt_slots(): jnp.einsum('mvk,mkd->vmd', one_hot, parts, preferred_element_type=jnp.flo...  18.7 us
    all_to_all x1, waiting for transfers between devices, body(): lax.all_to_all(scored, 'list', split_axis=0, concat_axis=0, tiled=True)  17.7 us
    all_to_all x1, starting transfers between devices, body(): lax.all_to_all(outgoing, 'list', split_axis=0, concat_axis=0, tiled=True)  15 us
    all_to_all x1, waiting for transfers between devices, body(): lax.all_to_all(outgoing, 'list', split_axis=0, concat_axis=0, tiled=True)  7.83 us
    all_to_all x1, starting transfers between devices, body(): lax.all_to_all(scored, 'list', split_axis=0, concat_axis=0, tiled=True)  6.62 us
    unnamed x10, local copies, waits for them, and re-layouts  1.88 us
    add x1, other arithmetic, rebuilt_slots(): picked[..., :width] + picked[..., width:2 * width] + picked[..., 2 * width:]  1.85 us
  transfers between devices with their start and end apart: 3, of which 2 were waited for; matrix products, arithmetic and copies ran while one was open for 33% of the time, Pallas kernels for 0%

profile of v9, /device:TPU:32, one launch (start us, length us, event | category | flops | bytes accessed | tf_op | source)
XLA Modules:
  0.0 83.4 jit_solution(13149059727347154757)
XLA Ops:
  0.0 0.9 %fusion.17 = pred[4,128]{1,0:T(4,128)(4,1)S(1)} fusion(s32[4,32]{1,0:T(4,128)} %param.7), kind=kLoop, calls=%fused_computation.35 | loop fusion | flops 32256 | bytes 1024 | tf_op jit(solution)/shard_map/reduce_or | solution.py:53
  1.0 1.4 %convolution_bitcast_fusion = f32[128,1,2,8,128]{4,0,3,2,1:T(8,128)S(1)} fusion(f32[4,1024]{1,0:T(4,128)} %param.6, s32[128,2]{0,1:T(2,128)S(1)} %and_select_fusion.3), kind=kOutput, calls=%fused_computation.17 | convolution fusion | flops 12583936 | bytes 1065984 | tf_op jit(solution)/shard_map/ckr,rij->ckij/dot_general | solution.py:66
  2.3 1.6 %copy.16 = f32[128,1,2,8,128]{4,3,2,1,0:T(8,128)} copy(f32[128,1,2,8,128]{4,0,3,2,1:T(8,128)S(1)} %convolution_bitcast_fusion) | data formatting | bytes 2097152 | tf_op jit(solution)/shard_map/reshape | solution.py:69
  3.9 15.0 %all-to-all-start = ((f32[128,1,2,8,128]{4,3,2,1,0:T(8,128)}), f32[128,1,2,8,128]{4,3,2,1,0:T(8,128)S(1)}, u32[]{:S(2)}, u32[]{:S(2)}) async-start(f32[128,1,2,8,128]{4,3,2,1,0:T(8,128)} %copy.16), calls=%async_computation | async-start | bytes 2097152 | tf_op jit(solution)/shard_map/all_to_all | solution.py:70
  19.7 0.1 broadcast_select_fusion.1
  19.8 0.3 fusion.16
  20.1 0.1 fusion.8
  20.2 0.2 fusion.15
  20.5 0.2 copy-done.4
  20.7 18.7 %fusion.2 = f32[512,64,51]{0,2,1:T(8,128)S(1)} fusion(s32[64,512]{1,0:T(8,128)S(1)} %bitcast.61, bf16[64,256,17]{1,2,0:T(8,128)(2,1)S(1)} %get-tuple-element.6, bf16[64,256,17]{1,2,0:T(8,128)(2,1)S(1)} %get-tuple-element.5, bf16[64,256,17]{1,2,0:T(8,128)(2,1)S(1)} %fusion.8), kind=kOutput, calls=%fused_computation.7 | convolution fusion | flops 869040128 | bytes 8486912 | tf_op jit(solution)/shard_map/mvk,mkd->vmd/dot_general | solution.py:28
  39.4 1.8 %slice_add_fusion = f32[512,64,17]{0,2,1:T(8,128)S(1)} fusion(f32[512,64,51]{0,2,1:T(8,128)S(1)} %fusion.2), kind=kLoop, calls=%fused_computation.5 | loop fusion | flops 1114112 | bytes 8912896 | tf_op jit(solution)/shard_map/add | solution.py:29
  41.3 1.6 %copy-done.1 = f32[512,64,17]{0,2,1:T(8,128)} copy-done((f32[512,64,17]{0,2,1:T(8,128)}, f32[512,64,17]{0,2,1:T(8,128)S(1)}, u32[]{:S(2)}) %copy-start.1) | copy-done | bytes 2228248
  42.9 0.1 slice_reduce_fusion
  43.0 7.8 %all-to-all-done = f32[128,1,2,8,128]{4,3,2,1,0:T(8,128)S(1)} async-done(((f32[128,1,2,8,128]{4,3,2,1,0:T(8,128)}), f32[128,1,2,8,128]{4,3,2,1,0:T(8,128)S(1)}, u32[]{:S(2)}, u32[]{:S(2)}) %all-to-all-start) | async-done | bytes 1048608 | tf_op jit(solution)/shard_map/all_to_all | solution.py:70
  50.9 0.5 fusion.14
  51.4 0.1 add.59
  51.6 1.5 %slice-done = f32[512,64,16]{0,2,1:T(8,128)S(1)} async-done(((f32[512,64,17]{0,2,1:T(8,128)}), f32[512,64,16]{0,2,1:T(8,128)S(1)}, s32[]{:S(2)}) %slice-start) | async-done | bytes 2097176 | tf_op jit(solution)/shard_map/slice | solution.py:30
  53.1 1.2 %fusion.10 = f32[256,512]{1,0:T(8,128)S(1)} fusion(f32[512,1024]{0,1:T(8,128)S(1)} %bitcast.57, f32[32,8,8,128]{3,2,1,0:T(8,128)S(1)} %bitcast.58, f32[512]{0:T(512)S(1)} %slice_reduce_fusion, f32[256]{0:T(256)S(1)} %add.59, pred[512]{0:T(512)(128)(4,1)S(1)} %iota_compare_fusion.6), kind=kOutput, calls=%fused_computation.20 | convolution fusion | flops 805830656 | bytes 3673600 | tf_op jit(solution)/shard_map/sf,vf->sv/dot_general | solution.py:81
  54.4 1.1 %stack_reshape.3 = f32[128,1,2,512]{3,2,0,1:T(2,128)} reshape(f32[256,512]{1,0:T(8,128)S(1)} %fusion.10) | data formatting | bytes 1048576 | tf_op jit(solution)/shard_map/stack;reshape | solution.py:88
  55.5 6.6 %all-to-all-start.1 = ((f32[128,1,2,512]{3,2,1,0:T(2,128)}), f32[128,1,2,512]{3,2,1,0:T(2,128)S(1)}, u32[]{:S(2)}, u32[]{:S(2)}) async-start(f32[128,1,2,512]{3,2,1,0:T(2,128)} %bitcast.20), calls=%async_computation.1 | async-start | bytes 1048576 | tf_op jit(solution)/shard_map/all_to_all | solution.py:89
  62.2 1.5 %gather_fusion.1 = s32[128]{0:T(128)S(1)} fusion(s32[4,128]{1,0:T(4,128)S(1)} %convert_subtract_fusion.1, s32[128]{0:T(128)S(1)} %reshape.282), kind=kCustom, calls=%fused_computation.1 | custom fusion | bytes 2048 | tf_op jit(solution)/shard_map/jit(take_along_axis)/gather | solution.py:56
  63.9 17.7 %all-to-all-done.1 = f32[128,1,2,512]{3,2,1,0:T(2,128)S(1)} async-done(((f32[128,1,2,512]{3,2,1,0:T(2,128)}), f32[128,1,2,512]{3,2,1,0:T(2,128)S(1)}, u32[]{:S(2)}, u32[]{:S(2)}) %all-to-all-start.1) | async-done | bytes 524320 | tf_op jit(solution)/shard_map/all_to_all | solution.py:89
  81.6 0.4 reshape.271
  81.9 1.5 %gather_fusion = f32[128,512]{1,0:T(8,128)} fusion(f32[256,512]{1,0:T(8,128)S(1)} %reshape.271, s32[1024]{0:T(1024)S(1)} %pad_clamp_fusion), kind=kCustom, calls=%fused_computation | custom fusion | bytes 524800 | tf_op jit(solution)/shard_map/gather | solution.py:91
  (28 shorter events, 0.5 us)
Async XLA Ops:
  0.0 19.6 %copy-start = (f32[128,1024]{1,0:T(8,128)S(1)}, f32[128,1024]{1,0:T(8,128)}, u32[]{:S(2)}) copy-start(f32[128,1024]{1,0:T(8,128)} %param.8) | copy-start | bytes 1572868
  0.0 19.6 %copy-start.2 = (f32[32,16,256]{2,1,0:T(8,128)S(1)}, f32[32,16,256]{2,1,0:T(8,128)}, u32[]{:S(2)}) copy-start(f32[32,16,256]{2,1,0:T(8,128)} %param.9) | copy-start | bytes 1572868
  0.0 19.6 %collective-permute-start = (f32[32,16,256]{2,1,0:T(8,128)}, f32[32,16,256]{2,1,0:T(8,128)S(1)}, u32[]{:S(2)}, u32[]{:S(2)}) collective-permute-start(f32[32,16,256]{2,1,0:T(8,128)} %param.9), channel_id=1, source_target_pairs={{0,128},{128,0},{1,129},{129,1},{2,130},{130,2},{3,131},{131,3},{4... | collective-permute-start | bytes 1572872 | tf_op jit(solution)/shard_map/ppermute | solution.py:43
  3.9 46.9 %all-to-all-start = ((f32[128,1,2,8,128]{4,3,2,1,0:T(8,128)}), f32[128,1,2,8,128]{4,3,2,1,0:T(8,128)S(1)}, u32[]{:S(2)}, u32[]{:S(2)}) async-start(f32[128,1,2,8,128]{4,3,2,1,0:T(8,128)} %copy.16), calls=%async_computation | async-start | bytes 2097152 | tf_op jit(solution)/shard_map/all_to_all | solution.py:70
  19.8 0.9 %copy-start.4 = (s32[1,64,512]{2,1,0:T(8,128)S(1)}, s32[1,64,512]{2,1,0:T(8,128)}, u32[]{:S(2)}) copy-start(s32[1,64,512]{2,1,0:T(8,128)} %param.10) | copy-start | bytes 393220
  41.3 1.7 %copy-start.1 = (f32[512,64,17]{0,2,1:T(8,128)}, f32[512,64,17]{0,2,1:T(8,128)S(1)}, u32[]{:S(2)}) copy-start(f32[512,64,17]{0,2,1:T(8,128)S(1)} %slice_add_fusion) | copy-start | bytes 6684676
  51.5 1.6 %slice-start = ((f32[512,64,17]{0,2,1:T(8,128)}), f32[512,64,16]{0,2,1:T(8,128)S(1)}, s32[]{:S(2)}) async-start(f32[512,64,17]{0,2,1:T(8,128)} %copy-done.1), calls=%async_computation.2 | async-start | bytes 4194304 | tf_op jit(solution)/shard_map/slice | solution.py:30
  51.6 10.5 %copy-start.3 = (s32[4,32]{1,0:T(4,128)S(1)}, s32[4,32]{1,0:T(4,128)}, u32[]{:S(2)}) copy-start(s32[4,32]{1,0:T(4,128)} %param.7) | copy-start | bytes 1540
  55.5 26.1 %all-to-all-start.1 = ((f32[128,1,2,512]{3,2,1,0:T(2,128)}), f32[128,1,2,512]{3,2,1,0:T(2,128)S(1)}, u32[]{:S(2)}, u32[]{:S(2)}) async-start(f32[128,1,2,512]{3,2,1,0:T(2,128)} %bitcast.20), calls=%async_computation.1 | async-start | bytes 1048576 | tf_op jit(solution)/shard_map/all_to_all | solution.py:89

commit v10 on v6

--- a/solution.py
+++ b/solution.py
@@ -74,8 +74,16 @@
         residual = residual.reshape(list_size * slot_count, dim)
         rebuilt = rebuilt_slots(codebook_all, codes[local])
         slot_norm = jnp.sum(rebuilt * rebuilt, axis=1)
-        cross = jnp.einsum(
-            "sf,vf->sv", residual, rebuilt, precision=lax.Precision.HIGH
+        half = capacity // 2
+        cross = jnp.concatenate(
+            [
+                jnp.einsum(
+                    "sf,vf->sv", residual, rebuilt[part * half : (part + 1) * half],
+                    precision=lax.Precision.HIGH,
+                )
+                for part in range(2)
+            ],
+            axis=1,
         )
         total = (own_norm[:, None] + slot_norm[None, :]) - 2.0 * cross
         valid = positions < cell_sizes[local]
@@ -83,8 +91,8 @@
         scored.append(total.reshape(list_size, slot_count, capacity))
     scored = jnp.stack(scored, axis=1)
     returned = lax.all_to_all(scored, "list", split_axis=0, concat_axis=0, tiled=True)
-    returned = returned.reshape(cell_count * slot_count, capacity)
-    result = returned[flat_cells * slot_count + slot_rank]
+    returned = returned.reshape(cell_count, slot_count, capacity)
+    result = returned[flat_cells, slot_rank]
     return result.reshape(query_rows, probe_count, capacity)
 
 

time: 82.9 us -> 84.5 us (1.019)
  local copies, waits for them, and re-layouts: 8.62 us -> 10.3 us
  other arithmetic: 4.02 us -> 3.17 us
    slice x0 -> x1, local copies, waits for them, and re-layouts: none -> 1.67 us  [body(): rebuilt[part * half:(part + 1) * half]]
    all_to_all x1, waiting for transfers between devices: 8.36 us -> 9.71 us  [body(): lax.all_to_all(outgoing, 'list', split_axis=0, concat_axis=0, tiled=True)]
    select_n x0 -> x2, local copies, waits for them, and re-layouts: none -> 1.28 us  [the longest x1 1.19 us: body(): total = jnp.where(valid[None, :], total, jnp.zeros((), jnp.float32))]
    ppermute x1, waiting for transfers between devices: 1.2 us -> 0.01 us  [body(): other = lax.ppermute(codebook, 'query', [(0, 1), (1, 0)])]
    reduce_sum x1, other arithmetic: 2.21 us -> 1.08 us  [body(): slot_norm = jnp.sum(rebuilt * rebuilt, axis=1)]
    another operation x1 -> x0, local copies, waits for them, and re-layouts: 1.09 us -> none  [body(): scored = jnp.stack(scored, axis=1)]
    dot_general x1 -> x2, matrix products: 1.25 us -> 2.03 us  [body(): jnp.einsum('sf,vf->sv', residual, rebuilt[part * half:(part + 1) * half],...]
    unnamed x10 -> x12, local copies, waits for them, and re-layouts: 2.18 us -> 1.67 us
  transfers between devices with their start and end apart: 3 -> 3, of which waited for: 3 -> 2; matrix products, arithmetic and copies ran while one was open for 27% -> 32% of each run, Pallas kernels for 0% -> 0%
where the time goes in v10:
time: 84.5 us; the launch traced here: 84.1 us
  waiting for transfers between devices  27.1 us (32%)
  starting transfers between devices  21.6 us (26%)
  matrix products  21.2 us (25%)
  local copies, waits for them, and re-layouts  10.3 us (12%)
  other arithmetic  3.17 us (4%)
  between operations  0.88 us (1%)
    dot_general x1, matrix products, rebuilt_slots(): jnp.einsum('mvk,mkd->vmd', one_hot, parts, preferred_element_type=jnp.flo...  17.8 us
    all_to_all x1, waiting for transfers between devices, body(): lax.all_to_all(scored, 'list', split_axis=0, concat_axis=0, tiled=True)  17.3 us
    all_to_all x1, starting transfers between devices, body(): lax.all_to_all(outgoing, 'list', split_axis=0, concat_axis=0, tiled=True)  15 us
    all_to_all x1, waiting for transfers between devices, body(): lax.all_to_all(outgoing, 'list', split_axis=0, concat_axis=0, tiled=True)  9.71 us
    all_to_all x1, starting transfers between devices, body(): lax.all_to_all(scored, 'list', split_axis=0, concat_axis=0, tiled=True)  6.62 us
    dot_general x2, matrix products, body(): jnp.einsum('sf,vf->sv', residual, rebuilt[part * half:(part + 1) * half],...  2.03 us
    gather x1, local copies, waits for them, and re-layouts, body(): result = returned[flat_cells, slot_rank]  1.76 us
  transfers between devices with their start and end apart: 3, of which 2 were waited for; matrix products, arithmetic and copies ran while one was open for 32% of the time, Pallas kernels for 0%

profile of v10, /device:TPU:32, one launch (start us, length us, event | category | flops | bytes accessed | tf_op | source)
XLA Modules:
  0.0 84.1 jit_solution(3792695274167288736)
XLA Ops:
  0.0 0.8 fusion.14
  0.9 1.4 %convolution_bitcast_fusion = f32[128,1,2,8,128]{4,0,3,2,1:T(8,128)S(1)} fusion(f32[4,1024]{1,0:T(4,128)} %param.6, s32[128,2]{0,1:T(2,128)S(1)} %and_select_fusion.4), kind=kOutput, calls=%fused_computation.14 | convolution fusion | flops 12583936 | bytes 1065984 | tf_op jit(solution)/shard_map/ckr,rij->ckij/dot_general | solution.py:61
  2.3 1.6 %copy.36 = f32[128,1,2,8,128]{4,3,2,1,0:T(8,128)} copy(f32[128,1,2,8,128]{4,0,3,2,1:T(8,128)S(1)} %convolution_bitcast_fusion) | data formatting | bytes 2097152 | tf_op jit(solution)/shard_map/reshape | solution.py:64
  3.9 15.0 %all-to-all-start = ((f32[128,1,2,8,128]{4,3,2,1,0:T(8,128)}), f32[128,1,2,8,128]{4,3,2,1,0:T(8,128)S(1)}, u32[]{:S(2)}, u32[]{:S(2)}) async-start(f32[128,1,2,8,128]{4,3,2,1,0:T(8,128)} %copy.36), calls=%async_computation | async-start | bytes 2097152 | tf_op jit(solution)/shard_map/all_to_all | solution.py:65
  19.6 0.1 broadcast_select_fusion.1
  19.8 0.2 fusion.11
  20.0 0.7 copy-done.5
  20.6 17.8 %fusion.2 = f32[512,64,48]{0,2,1:T(8,128)S(1)} fusion(s32[64,512]{1,0:T(8,128)S(1)} %bitcast.86, bf16[64,256,16]{1,2,0:T(8,128)(2,1)S(1)} %get-tuple-element.10, bf16[64,256,16]{1,2,0:T(8,128)(2,1)S(1)} %get-tuple-element.9, bf16[64,256,16]{1,2,0:T(8,128)(2,1)S(1)} %fusion.10), kind=kOutput, calls=%fused_computation.5 | convolution fusion | flops 818413568 | bytes 7995392 | tf_op jit(solution)/shard_map/mvk,mkd->vmd/dot_general | solution.py:23
  38.4 1.1 %multiply_reduce_fusion = (f32[512]{0:T(512)S(1)}, f32[512,64,16]{0,2,1:T(8,128)S(1)}) fusion(f32[512,64,48]{0,2,1:T(8,128)S(1)} %fusion.2), kind=kLoop, calls=%fused_computation.8 | loop fusion | flops 2096640 | bytes 8390656 | tf_op jit(solution)/shard_map/reduce_sum | solution.py:76
  39.5 1.7 %fusion.26 = (f32[256,64,16]{0,2,1:T(8,128)}, f32[256,64,16]{0,2,1:T(8,128)}) fusion(f32[512,64,16]{0,2,1:T(8,128)S(1)} %get-tuple-element.6), kind=kLoop, calls=%fused_computation.64 | loop fusion | bytes 4194304 | tf_op jit(solution)/shard_map/slice | solution.py:81
  41.2 9.7 %all-to-all-done = f32[128,1,2,8,128]{4,3,2,1,0:T(8,128)S(1)} async-done(((f32[128,1,2,8,128]{4,3,2,1,0:T(8,128)}), f32[128,1,2,8,128]{4,3,2,1,0:T(8,128)S(1)}, u32[]{:S(2)}, u32[]{:S(2)}) %all-to-all-start) | async-done | bytes 1048608 | tf_op jit(solution)/shard_map/all_to_all | solution.py:65
  50.9 0.5 fusion.9
  51.4 0.4 copy.38
  51.9 0.2 broadcast_subtract_fusion
  52.1 1.0 %copy-done.2 = f32[256,64,16]{0,2,1:T(8,128)S(1)} copy-done((f32[256,64,16]{0,2,1:T(8,128)S(1)}, f32[256,64,16]{0,2,1:T(8,128)}, u32[]{:S(2)}) %copy-start.2) | copy-done | bytes 1048600
  53.1 1.0 %convolution_bitcast_fusion.2 = f32[128,1,2,256]{3,0,2,1:T(8,128)S(1)} fusion(f32[128,2,1024]{0,2,1:T(8,128)S(1)} %bitcast.80, f32[256,1024,1]{0,1,2:T(8,128)S(1)} %bitcast.83), kind=kOutput, calls=%fused_computation.16 | convolution fusion | flops 402653184 | bytes 2359296 | tf_op jit(solution)/shard_map/sf,vf->sv/dot_general | solution.py:80
  54.1 1.0 %convolution_bitcast_fusion.1 = f32[128,1,2,256]{3,0,2,1:T(8,128)S(1)} fusion(f32[128,2,1024]{0,2,1:T(8,128)S(1)} %bitcast.81, f32[256,1024,1]{0,1,2:T(8,128)S(1)} %bitcast.82), kind=kOutput, calls=%fused_computation.15 | convolution fusion | flops 402653184 | bytes 2359296 | tf_op jit(solution)/shard_map/sf,vf->sv/dot_general | solution.py:80
  55.2 0.1 fusion.13
  55.3 1.2 %copy.43 = f32[128,1,2,512]{3,2,1,0:T(2,128)} copy(f32[128,1,2,512]{3,0,2,1:T(8,128)S(1)} %fusion.13) | data formatting | bytes 1048576 | tf_op jit(solution)/shard_map/jit(_where)/select_n | solution.py:90
  56.5 6.6 %all-to-all-start.1 = ((f32[128,1,2,512]{3,2,1,0:T(2,128)}), f32[128,1,2,512]{3,2,1,0:T(2,128)S(1)}, u32[]{:S(2)}, u32[]{:S(2)}) async-start(f32[128,1,2,512]{3,2,1,0:T(2,128)} %copy.43), calls=%async_computation.1 | async-start | bytes 1048576 | tf_op jit(solution)/shard_map/all_to_all | solution.py:93
  63.2 0.1 reshape.366
  63.3 1.5 %gather_fusion.1 = s32[128]{0:T(128)S(1)} fusion(s32[4,128]{1,0:T(4,128)S(1)} %convert_subtract_fusion.1, s32[128]{0:T(128)S(1)} %reshape.366), kind=kCustom, calls=%fused_computation.1 | custom fusion | bytes 2048 | tf_op jit(solution)/shard_map/jit(take_along_axis)/gather | solution.py:51
  65.0 17.3 %all-to-all-done.1 = f32[128,1,2,512]{3,2,1,0:T(2,128)S(1)} async-done(((f32[128,1,2,512]{3,2,1,0:T(2,128)}), f32[128,1,2,512]{3,2,1,0:T(2,128)S(1)}, u32[]{:S(2)}, u32[]{:S(2)}) %all-to-all-start.1) | async-done | bytes 524320 | tf_op jit(solution)/shard_map/all_to_all | solution.py:93
  82.4 1.8 %gather_fusion = f32[128,512]{1,0:T(8,128)} fusion(f32[128,2,512]{2,1,0:T(2,128)S(1)} %bitcast.79, s32[128]{0:T(128)S(1)} %fusion.24), kind=kCustom, calls=%fused_computation | custom fusion | bytes 525312 | tf_op jit(solution)/shard_map/gather | solution.py:95
  (28 shorter events, 0.5 us)
Async XLA Ops:
  0.0 19.6 %copy-start = (f32[128,1024]{1,0:T(8,128)S(1)}, f32[128,1024]{1,0:T(8,128)}, u32[]{:S(2)}) copy-start(f32[128,1024]{1,0:T(8,128)} %param.8) | copy-start | bytes 1572868
  0.0 19.6 %collective-permute-start = (f32[32,16,256]{2,1,0:T(8,128)}, f32[32,16,256]{2,1,0:T(8,128)S(1)}, u32[]{:S(2)}, u32[]{:S(2)}) collective-permute-start(f32[32,16,256]{2,1,0:T(8,128)} %param.9), channel_id=1, source_target_pairs={{0,128},{128,0},{1,129},{129,1},{2,130},{130,2},{3,131},{131,3},{4... | collective-permute-start | bytes 1572872 | tf_op jit(solution)/shard_map/ppermute | solution.py:38
  2.3 17.3 %copy-start.3 = (f32[32,16,256]{2,1,0:T(8,128)S(1)}, f32[32,16,256]{2,1,0:T(8,128)}, u32[]{:S(2)}) copy-start(f32[32,16,256]{2,1,0:T(8,128)} %param.9) | copy-start | bytes 1572868
  3.9 47.0 %all-to-all-start = ((f32[128,1,2,8,128]{4,3,2,1,0:T(8,128)}), f32[128,1,2,8,128]{4,3,2,1,0:T(8,128)S(1)}, u32[]{:S(2)}, u32[]{:S(2)}) async-start(f32[128,1,2,8,128]{4,3,2,1,0:T(8,128)} %copy.36), calls=%async_computation | async-start | bytes 2097152 | tf_op jit(solution)/shard_map/all_to_all | solution.py:65
  19.7 0.9 %copy-start.5 = (s32[1,64,512]{2,1,0:T(8,128)S(1)}, s32[1,64,512]{2,1,0:T(8,128)}, u32[]{:S(2)}) copy-start(s32[1,64,512]{2,1,0:T(8,128)} %param.10) | copy-start | bytes 393220
  51.9 1.2 %copy-start.2 = (f32[256,64,16]{0,2,1:T(8,128)S(1)}, f32[256,64,16]{0,2,1:T(8,128)}, u32[]{:S(2)}) copy-start(f32[256,64,16]{0,2,1:T(8,128)} %get-tuple-element.7) | copy-start | bytes 3145732
  51.9 2.2 %copy-start.1 = (f32[256,64,16]{0,2,1:T(8,128)S(1)}, f32[256,64,16]{0,2,1:T(8,128)}, u32[]{:S(2)}) copy-start(f32[256,64,16]{0,2,1:T(8,128)} %get-tuple-element.8) | copy-start | bytes 3145732
  55.2 8.0 %copy-start.4 = (s32[4,32]{1,0:T(4,128)S(1)}, s32[4,32]{1,0:T(4,128)}, u32[]{:S(2)}) copy-start(s32[4,32]{1,0:T(4,128)} %param.7) | copy-start | bytes 1540
  56.5 25.9 %all-to-all-start.1 = ((f32[128,1,2,512]{3,2,1,0:T(2,128)}), f32[128,1,2,512]{3,2,1,0:T(2,128)S(1)}, u32[]{:S(2)}, u32[]{:S(2)}) async-start(f32[128,1,2,512]{3,2,1,0:T(2,128)} %copy.43), calls=%async_computation.1 | async-start | bytes 1048576 | tf_op jit(solution)/shard_map/all_to_all | solution.py:93

commit v11 on v6

--- a/solution.py
+++ b/solution.py
@@ -57,9 +57,13 @@
     for row in range(query_rows):
         here = contains[row][:, None] & (earlier_rows[row][:, None] == jnp.arange(slot_count)[None, :])
         row_at = jnp.where(here, row, row_at)
-    selector = (row_at[:, :, None] == jnp.arange(query_rows)[None, None, :]).astype(jnp.float32)
+    selector = (row_at[:, :, None] == jnp.arange(query_rows)[None, None, :]).astype(jnp.bfloat16)
+    selector = jnp.concatenate([selector] * 3, axis=-1)
+    query_parts = exact_parts(queries.reshape(query_rows, 1, dim))
+    query_parts = jnp.transpose(query_parts.reshape(query_rows, 3, dim), (1, 0, 2))
+    query_parts = query_parts.reshape(3 * query_rows, tile_rows, lanes)
     outgoing = jnp.einsum(
-        "ckr,rij->ckij", selector, query_tiles, precision=lax.Precision.HIGHEST
+        "ckr,rij->ckij", selector, query_parts, preferred_element_type=jnp.float32
     )
     outgoing = outgoing.reshape(list_size, cells_dev, slot_count, tile_rows, lanes)
     arrived = lax.all_to_all(outgoing, "list", split_axis=0, concat_axis=0, tiled=True)

time: 82.9 us -> 82.9 us (level)
  matrix products: 20.4 us -> 19.4 us
    dot_general x1, matrix products: 1.36 us -> 0.34 us  [body(): jnp.einsum('ckr,rij->ckij', selector, query_parts, preferred_element_type...]
where the time goes in v11:
time: 82.9 us; the launch traced here: 82.4 us
  waiting for transfers between devices  27 us (33%)
  starting transfers between devices  21.7 us (26%)
  matrix products  19.4 us (23%)
  local copies, waits for them, and re-layouts  8.64 us (10%)
  other arithmetic  4.84 us (6%)
  between operations  0.86 us (1%)
    dot_general x1, matrix products, rebuilt_slots(): jnp.einsum('mvk,mkd->vmd', one_hot, parts, preferred_element_type=jnp.flo...  17.8 us
    all_to_all x1, waiting for transfers between devices, body(): lax.all_to_all(scored, 'list', split_axis=0, concat_axis=0, tiled=True)  17.4 us
    all_to_all x1, starting transfers between devices, body(): lax.all_to_all(outgoing, 'list', split_axis=0, concat_axis=0, tiled=True)  15 us
    all_to_all x1, waiting for transfers between devices, body(): lax.all_to_all(outgoing, 'list', split_axis=0, concat_axis=0, tiled=True)  8.37 us
    all_to_all x1, starting transfers between devices, body(): lax.all_to_all(scored, 'list', split_axis=0, concat_axis=0, tiled=True)  6.62 us
    reduce_sum x1, other arithmetic, body(): slot_norm = jnp.sum(rebuilt * rebuilt, axis=1)  2.2 us
    unnamed x10, local copies, waits for them, and re-layouts  2.18 us
    gather x3, local copies, waits for them, and re-layouts, body(): rank_of = jnp.take_along_axis(earlier_rows, probes, axis=1)  1.67 us
  transfers between devices with their start and end apart: 3, of which 3 were waited for; matrix products, arithmetic and copies ran while one was open for 27% of the time, Pallas kernels for 0%

profile of v11, /device:TPU:32, one launch (start us, length us, event | category | flops | bytes accessed | tf_op | source)
XLA Modules:
  0.0 82.4 jit_solution(3970921175098499407)
XLA Ops:
  0.0 0.8 %fusion.16 = pred[4,128]{1,0:T(4,128)(4,1)S(1)} fusion(s32[4,32]{1,0:T(4,128)} %param.7), kind=kLoop, calls=%fused_computation.32 | loop fusion | flops 32256 | bytes 1024 | tf_op jit(solution)/shard_map/reduce_or | solution.py:48
  0.9 0.8 convert_bitcast_fusion
  1.8 0.3 convolution_bitcast_fusion
  2.2 1.6 %copy.15 = f32[128,1,2,8,128]{4,3,2,1,0:T(8,128)} copy(f32[128,1,2,8,128]{4,0,3,2,1:T(8,128)S(1)} %convolution_bitcast_fusion) | data formatting | bytes 2097152 | tf_op jit(solution)/shard_map/reshape | solution.py:68
  3.8 15.0 %all-to-all-start = ((f32[128,1,2,8,128]{4,3,2,1,0:T(8,128)}), f32[128,1,2,8,128]{4,3,2,1,0:T(8,128)S(1)}, u32[]{:S(2)}, u32[]{:S(2)}) async-start(f32[128,1,2,8,128]{4,3,2,1,0:T(8,128)} %copy.15), calls=%async_computation | async-start | bytes 2097152 | tf_op jit(solution)/shard_map/all_to_all | solution.py:69
  18.8 0.1 collective-permute-start
  19.6 1.2 %collective-permute-done = f32[32,16,256]{2,1,0:T(8,128)S(1)} collective-permute-done((f32[32,16,256]{2,1,0:T(8,128)S(1)}, f32[32,16,256]{2,1,0:T(8,128)S(1)}, u32[]{:S(2)}, u32[]{:S(2)}) %collective-permute-start) | collective-permute-done | bytes 524320 | tf_op jit(solution)/shard_map/ppermute | solution.py:38
  20.8 0.1 broadcast_select_fusion.1
  21.0 0.2 fusion.15
  21.1 0.7 copy-done.4
  21.8 17.8 %fusion.2 = f32[512,64,48]{0,2,1:T(8,128)S(1)} fusion(s32[64,512]{1,0:T(8,128)S(1)} %bitcast.83, bf16[64,256,16]{1,2,0:T(8,128)(2,1)S(1)} %get-tuple-element.8, bf16[64,256,16]{1,2,0:T(8,128)(2,1)S(1)} %get-tuple-element.7, bf16[64,256,16]{1,2,0:T(8,128)(2,1)S(1)} %fusion.14), kind=kOutput, calls=%fused_computation.5 | convolution fusion | flops 818413568 | bytes 7995392 | tf_op jit(solution)/shard_map/mvk,mkd->vmd/dot_general | solution.py:23
  39.6 2.2 %multiply_reduce_fusion = (f32[512]{0:T(512)S(1)}, f32[512,64,16]{0,2,1:T(8,128)}) fusion(f32[512,64,48]{0,2,1:T(8,128)S(1)} %fusion.2), kind=kLoop, calls=%fused_computation.8 | loop fusion | flops 2096640 | bytes 8390656 | tf_op jit(solution)/shard_map/reduce_sum | solution.py:80
  41.8 8.4 %all-to-all-done = f32[128,1,2,8,128]{4,3,2,1,0:T(8,128)S(1)} async-done(((f32[128,1,2,8,128]{4,3,2,1,0:T(8,128)}), f32[128,1,2,8,128]{4,3,2,1,0:T(8,128)S(1)}, u32[]{:S(2)}, u32[]{:S(2)}) %all-to-all-start) | async-done | bytes 1048608 | tf_op jit(solution)/shard_map/all_to_all | solution.py:69
  50.1 0.5 fusion.13
  50.6 0.1 add.59
  50.9 1.5 %copy-done.1 = f32[512,64,16]{0,2,1:T(8,128)S(1)} copy-done((f32[512,64,16]{0,2,1:T(8,128)S(1)}, f32[512,64,16]{0,2,1:T(8,128)}, u32[]{:S(2)}) %copy-start.1) | copy-done | bytes 2097176
  52.4 1.2 %fusion.9 = f32[256,512]{1,0:T(8,128)S(1)} fusion(f32[512,1024]{0,1:T(8,128)S(1)} %bitcast.78, f32[32,8,8,128]{3,2,1,0:T(8,128)S(1)} %bitcast.79, f32[512]{0:T(512)S(1)} %get-tuple-element.5, f32[256]{0:T(256)S(1)} %add.59, pred[512]{0:T(512)(128)(4,1)S(1)} %iota_compare_fusion.6), kind=kOutput, calls=%fused_computation.17 | convolution fusion | flops 805830656 | bytes 3673600 | tf_op jit(solution)/shard_map/sf,vf->sv/dot_general | solution.py:81
  53.6 1.1 %stack_reshape.3 = f32[128,1,2,512]{3,2,0,1:T(2,128)} reshape(f32[256,512]{1,0:T(8,128)S(1)} %fusion.9) | data formatting | bytes 1048576 | tf_op jit(solution)/shard_map/stack;reshape | solution.py:88
  54.7 6.6 %all-to-all-start.1 = ((f32[128,1,2,512]{3,2,1,0:T(2,128)}), f32[128,1,2,512]{3,2,1,0:T(2,128)S(1)}, u32[]{:S(2)}, u32[]{:S(2)}) async-start(f32[128,1,2,512]{3,2,1,0:T(2,128)} %bitcast.24), calls=%async_computation.1 | async-start | bytes 1048576 | tf_op jit(solution)/shard_map/all_to_all | solution.py:89
  61.5 1.5 %gather_fusion.1 = s32[128]{0:T(128)S(1)} fusion(s32[4,128]{1,0:T(4,128)S(1)} %convert_subtract_fusion.2, s32[128]{0:T(128)S(1)} %reshape.294), kind=kCustom, calls=%fused_computation.1 | custom fusion | bytes 2048 | tf_op jit(solution)/shard_map/jit(take_along_axis)/gather | solution.py:51
  63.1 0.1 add.68
  63.2 17.4 %all-to-all-done.1 = f32[128,1,2,512]{3,2,1,0:T(2,128)S(1)} async-done(((f32[128,1,2,512]{3,2,1,0:T(2,128)}), f32[128,1,2,512]{3,2,1,0:T(2,128)S(1)}, u32[]{:S(2)}, u32[]{:S(2)}) %all-to-all-start.1) | async-done | bytes 524320 | tf_op jit(solution)/shard_map/all_to_all | solution.py:89
  80.6 0.4 reshape.283
  81.0 1.5 %gather_fusion = f32[128,512]{1,0:T(8,128)} fusion(f32[256,512]{1,0:T(8,128)S(1)} %reshape.283, s32[1024]{0:T(1024)S(1)} %pad_clamp_fusion), kind=kCustom, calls=%fused_computation | custom fusion | bytes 524800 | tf_op jit(solution)/shard_map/gather | solution.py:91
  (27 shorter events, 0.5 us)
Async XLA Ops:
  0.0 19.6 %copy-start = (f32[128,1024]{1,0:T(8,128)S(1)}, f32[128,1024]{1,0:T(8,128)}, u32[]{:S(2)}) copy-start(f32[128,1024]{1,0:T(8,128)} %param.8) | copy-start | bytes 1572868
  2.2 16.6 %copy-start.2 = (f32[32,16,256]{2,1,0:T(8,128)S(1)}, f32[32,16,256]{2,1,0:T(8,128)}, u32[]{:S(2)}) copy-start(f32[32,16,256]{2,1,0:T(8,128)} %param.9) | copy-start | bytes 1572868
  3.8 46.4 %all-to-all-start = ((f32[128,1,2,8,128]{4,3,2,1,0:T(8,128)}), f32[128,1,2,8,128]{4,3,2,1,0:T(8,128)S(1)}, u32[]{:S(2)}, u32[]{:S(2)}) async-start(f32[128,1,2,8,128]{4,3,2,1,0:T(8,128)} %copy.15), calls=%async_computation | async-start | bytes 2097152 | tf_op jit(solution)/shard_map/all_to_all | solution.py:69
  18.8 2.0 %collective-permute-start = (f32[32,16,256]{2,1,0:T(8,128)S(1)}, f32[32,16,256]{2,1,0:T(8,128)S(1)}, u32[]{:S(2)}, u32[]{:S(2)}) collective-permute-start(f32[32,16,256]{2,1,0:T(8,128)S(1)} %copy-done.2), channel_id=1, source_target_pairs={{0,128},{128,0},{1,129},{129,1},{2,130},{130,2},{3,131},{131,3},{4... | collective-permute-start | bytes 1572872 | tf_op jit(solution)/shard_map/ppermute | solution.py:38
  20.9 0.9 %copy-start.4 = (s32[1,64,512]{2,1,0:T(8,128)S(1)}, s32[1,64,512]{2,1,0:T(8,128)}, u32[]{:S(2)}) copy-start(s32[1,64,512]{2,1,0:T(8,128)} %param.10) | copy-start | bytes 393220
  50.8 1.6 %copy-start.1 = (f32[512,64,16]{0,2,1:T(8,128)S(1)}, f32[512,64,16]{0,2,1:T(8,128)}, u32[]{:S(2)}) copy-start(f32[512,64,16]{0,2,1:T(8,128)} %get-tuple-element.6) | copy-start | bytes 6291460
  52.4 9.0 %copy-start.3 = (s32[4,32]{1,0:T(4,128)S(1)}, s32[4,32]{1,0:T(4,128)}, u32[]{:S(2)}) copy-start(s32[4,32]{1,0:T(4,128)} %param.7) | copy-start | bytes 1540
  54.7 25.9 %all-to-all-start.1 = ((f32[128,1,2,512]{3,2,1,0:T(2,128)}), f32[128,1,2,512]{3,2,1,0:T(2,128)S(1)}, u32[]{:S(2)}, u32[]{:S(2)}) async-start(f32[128,1,2,512]{3,2,1,0:T(2,128)} %bitcast.24), calls=%async_computation.1 | async-start | bytes 1048576 | tf_op jit(solution)/shard_map/all_to_all | solution.py:89

commit v12 on v11

--- a/solution.py
+++ b/solution.py
@@ -7,11 +7,11 @@
 
 
 def exact_parts(values):
-    high = values.astype(jnp.bfloat16)
-    rest = values - high.astype(jnp.float32)
-    middle = rest.astype(jnp.bfloat16)
-    low = (rest - middle.astype(jnp.float32)).astype(jnp.bfloat16)
-    return jnp.concatenate([high, middle, low], axis=-1)
+    high = lax.reduce_precision(values, exponent_bits=8, mantissa_bits=7)
+    rest = values - high
+    middle = lax.reduce_precision(rest, exponent_bits=8, mantissa_bits=7)
+    low = rest - middle
+    return jnp.concatenate([high, middle, low], axis=-1).astype(jnp.bfloat16)
 
 
 def rebuilt_slots(codebook_all, cell_codes):

time: 82.9 us -> 82.2 us (level)
    convert_element_type x3 -> x0, other arithmetic: 1.03 us -> none  [the longest x2 0.87 us: exact_parts(): high = values.astype(jnp.bfloat16)]
where the time goes in v12:
time: 82.2 us; the launch traced here: 81.8 us
  waiting for transfers between devices  27 us (33%)
  starting transfers between devices  21.7 us (26%)
  matrix products  19.4 us (24%)
  local copies, waits for them, and re-layouts  7.98 us (10%)
  other arithmetic  4.83 us (6%)
  between operations  0.85 us (1%)
    dot_general x1, matrix products, rebuilt_slots(): jnp.einsum('mvk,mkd->vmd', one_hot, parts, preferred_element_type=jnp.flo...  17.8 us
    all_to_all x1, waiting for transfers between devices, body(): lax.all_to_all(scored, 'list', split_axis=0, concat_axis=0, tiled=True)  16.9 us
    all_to_all x1, starting transfers between devices, body(): lax.all_to_all(outgoing, 'list', split_axis=0, concat_axis=0, tiled=True)  15 us
    all_to_all x1, waiting for transfers between devices, body(): lax.all_to_all(outgoing, 'list', split_axis=0, concat_axis=0, tiled=True)  8.91 us
    all_to_all x1, starting transfers between devices, body(): lax.all_to_all(scored, 'list', split_axis=0, concat_axis=0, tiled=True)  6.62 us
    reduce_sum x1, other arithmetic, body(): slot_norm = jnp.sum(rebuilt * rebuilt, axis=1)  2.2 us
    gather x3, local copies, waits for them, and re-layouts, body(): rank_of = jnp.take_along_axis(earlier_rows, probes, axis=1)  1.67 us
  transfers between devices with their start and end apart: 3, of which 3 were waited for; matrix products, arithmetic and copies ran while one was open for 27% of the time, Pallas kernels for 0%

profile of v12, /device:TPU:32, one launch (start us, length us, event | category | flops | bytes accessed | tf_op | source)
XLA Modules:
  0.0 81.8 jit_solution(6656988356764465926)
XLA Ops:
  0.0 0.8 %fusion.15 = pred[4,128]{1,0:T(4,128)(4,1)S(1)} fusion(s32[4,32]{1,0:T(4,128)} %param.7), kind=kLoop, calls=%fused_computation.33 | loop fusion | flops 32256 | bytes 1024 | tf_op jit(solution)/shard_map/reduce_or | solution.py:48
  0.9 0.7 fusion.24
  1.7 0.3 convolution_bitcast_fusion
  2.1 1.6 %copy.15 = f32[128,1,2,8,128]{4,3,2,1,0:T(8,128)} copy(f32[128,1,2,8,128]{4,0,3,2,1:T(8,128)S(1)} %convolution_bitcast_fusion) | data formatting | bytes 2097152 | tf_op jit(solution)/shard_map/reshape | solution.py:68
  3.7 15.0 %all-to-all-start = ((f32[128,1,2,8,128]{4,3,2,1,0:T(8,128)}), f32[128,1,2,8,128]{4,3,2,1,0:T(8,128)S(1)}, u32[]{:S(2)}, u32[]{:S(2)}) async-start(f32[128,1,2,8,128]{4,3,2,1,0:T(8,128)} %copy.15), calls=%async_computation | async-start | bytes 2097152 | tf_op jit(solution)/shard_map/all_to_all | solution.py:69
  18.7 0.1 collective-permute-start
  19.5 1.2 %collective-permute-done = f32[32,16,256]{2,1,0:T(8,128)S(1)} collective-permute-done((f32[32,16,256]{2,1,0:T(8,128)S(1)}, f32[32,16,256]{2,1,0:T(8,128)S(1)}, u32[]{:S(2)}, u32[]{:S(2)}) %collective-permute-start) | collective-permute-done | bytes 524320 | tf_op jit(solution)/shard_map/ppermute | solution.py:38
  20.7 0.1 broadcast_select_fusion.1
  20.8 0.3 reduce-precision_convert_fusion.1
  21.1 17.8 %fusion.2 = f32[512,64,48]{0,2,1:T(8,128)S(1)} fusion(s32[64,512]{1,0:T(8,128)S(1)} %bitcast.75, bf16[64,256,16]{1,2,0:T(8,128)(2,1)S(1)} %get-tuple-element.9, bf16[64,256,16]{1,2,0:T(8,128)(2,1)S(1)} %get-tuple-element.8, bf16[64,256,16]{1,2,0:T(8,128)(2,1)S(1)} %get-tuple-element.7), kind=kOutput, calls=%fused_computation.5 | convolution fusion | flops 818413568 | bytes 7995392 | tf_op jit(solution)/shard_map/mvk,mkd->vmd/dot_general | solution.py:23
  38.9 2.2 %multiply_reduce_fusion = (f32[512]{0:T(512)S(1)}, f32[512,64,16]{0,2,1:T(8,128)}) fusion(f32[512,64,48]{0,2,1:T(8,128)S(1)} %fusion.2), kind=kLoop, calls=%fused_computation.8 | loop fusion | flops 2096640 | bytes 8390656 | tf_op jit(solution)/shard_map/reduce_sum | solution.py:80
  41.2 8.9 %all-to-all-done = f32[128,1,2,8,128]{4,3,2,1,0:T(8,128)S(1)} async-done(((f32[128,1,2,8,128]{4,3,2,1,0:T(8,128)}), f32[128,1,2,8,128]{4,3,2,1,0:T(8,128)S(1)}, u32[]{:S(2)}, u32[]{:S(2)}) %all-to-all-start) | async-done | bytes 1048608 | tf_op jit(solution)/shard_map/all_to_all | solution.py:69
  50.1 0.5 fusion.14
  50.6 0.1 add.59
  50.8 1.5 %copy-done.1 = f32[512,64,16]{0,2,1:T(8,128)S(1)} copy-done((f32[512,64,16]{0,2,1:T(8,128)S(1)}, f32[512,64,16]{0,2,1:T(8,128)}, u32[]{:S(2)}) %copy-start.1) | copy-done | bytes 2097176
  52.3 1.2 %fusion.9 = f32[256,512]{1,0:T(8,128)S(1)} fusion(f32[512,1024]{0,1:T(8,128)S(1)} %bitcast.70, f32[32,8,8,128]{3,2,1,0:T(8,128)S(1)} %bitcast.71, f32[512]{0:T(512)S(1)} %get-tuple-element.5, f32[256]{0:T(256)S(1)} %add.59, pred[512]{0:T(512)(128)(4,1)S(1)} %iota_compare_fusion.6), kind=kOutput, calls=%fused_computation.21 | convolution fusion | flops 805830656 | bytes 3673600 | tf_op jit(solution)/shard_map/sf,vf->sv/dot_general | solution.py:81
  53.5 1.1 %stack_reshape.3 = f32[128,1,2,512]{3,2,0,1:T(2,128)} reshape(f32[256,512]{1,0:T(8,128)S(1)} %fusion.9) | data formatting | bytes 1048576 | tf_op jit(solution)/shard_map/stack;reshape | solution.py:88
  54.6 6.6 %all-to-all-start.1 = ((f32[128,1,2,512]{3,2,1,0:T(2,128)}), f32[128,1,2,512]{3,2,1,0:T(2,128)S(1)}, u32[]{:S(2)}, u32[]{:S(2)}) async-start(f32[128,1,2,512]{3,2,1,0:T(2,128)} %bitcast.24), calls=%async_computation.1 | async-start | bytes 1048576 | tf_op jit(solution)/shard_map/all_to_all | solution.py:89
  61.3 0.1 reshape.306
  61.4 1.5 %gather_fusion.1 = s32[128]{0:T(128)S(1)} fusion(s32[4,128]{1,0:T(4,128)S(1)} %convert_subtract_fusion, s32[128]{0:T(128)S(1)} %reshape.306), kind=kCustom, calls=%fused_computation.1 | custom fusion | bytes 2048 | tf_op jit(solution)/shard_map/jit(take_along_axis)/gather | solution.py:51
  63.0 0.1 add.68
  63.1 16.9 %all-to-all-done.1 = f32[128,1,2,512]{3,2,1,0:T(2,128)S(1)} async-done(((f32[128,1,2,512]{3,2,1,0:T(2,128)}), f32[128,1,2,512]{3,2,1,0:T(2,128)S(1)}, u32[]{:S(2)}, u32[]{:S(2)}) %all-to-all-start.1) | async-done | bytes 524320 | tf_op jit(solution)/shard_map/all_to_all | solution.py:89
  80.0 0.4 reshape.295
  80.3 1.5 %gather_fusion = f32[128,512]{1,0:T(8,128)} fusion(f32[256,512]{1,0:T(8,128)S(1)} %reshape.295, s32[1024]{0:T(1024)S(1)} %pad_clamp_fusion), kind=kCustom, calls=%fused_computation | custom fusion | bytes 524800 | tf_op jit(solution)/shard_map/gather | solution.py:91
  (26 shorter events, 0.3 us)
Async XLA Ops:
  0.0 19.5 %copy-start = (f32[128,1024]{1,0:T(8,128)S(1)}, f32[128,1024]{1,0:T(8,128)}, u32[]{:S(2)}) copy-start(f32[128,1024]{1,0:T(8,128)} %param.8) | copy-start | bytes 1572868
  2.1 16.6 %copy-start.2 = (f32[32,16,256]{2,1,0:T(8,128)S(1)}, f32[32,16,256]{2,1,0:T(8,128)}, u32[]{:S(2)}) copy-start(f32[32,16,256]{2,1,0:T(8,128)} %param.9) | copy-start | bytes 1572868
  3.7 46.4 %all-to-all-start = ((f32[128,1,2,8,128]{4,3,2,1,0:T(8,128)}), f32[128,1,2,8,128]{4,3,2,1,0:T(8,128)S(1)}, u32[]{:S(2)}, u32[]{:S(2)}) async-start(f32[128,1,2,8,128]{4,3,2,1,0:T(8,128)} %copy.15), calls=%async_computation | async-start | bytes 2097152 | tf_op jit(solution)/shard_map/all_to_all | solution.py:69
  18.7 2.0 %collective-permute-start = (f32[32,16,256]{2,1,0:T(8,128)S(1)}, f32[32,16,256]{2,1,0:T(8,128)S(1)}, u32[]{:S(2)}, u32[]{:S(2)}) collective-permute-start(f32[32,16,256]{2,1,0:T(8,128)S(1)} %copy-done.2), channel_id=1, source_target_pairs={{0,128},{128,0},{1,129},{129,1},{2,130},{130,2},{3,131},{131,3},{4... | collective-permute-start | bytes 1572872 | tf_op jit(solution)/shard_map/ppermute | solution.py:38
  19.5 1.6 %copy-start.4 = (s32[1,64,512]{2,1,0:T(8,128)S(1)}, s32[1,64,512]{2,1,0:T(8,128)}, u32[]{:S(2)}) copy-start(s32[1,64,512]{2,1,0:T(8,128)} %param.10) | copy-start | bytes 393220
  50.7 1.6 %copy-start.1 = (f32[512,64,16]{0,2,1:T(8,128)S(1)}, f32[512,64,16]{0,2,1:T(8,128)}, u32[]{:S(2)}) copy-start(f32[512,64,16]{0,2,1:T(8,128)} %get-tuple-element.6) | copy-start | bytes 6291460
  52.3 9.0 %copy-start.3 = (s32[4,32]{1,0:T(4,128)S(1)}, s32[4,32]{1,0:T(4,128)}, u32[]{:S(2)}) copy-start(s32[4,32]{1,0:T(4,128)} %param.7) | copy-start | bytes 1540
  54.6 25.3 %all-to-all-start.1 = ((f32[128,1,2,512]{3,2,1,0:T(2,128)}), f32[128,1,2,512]{3,2,1,0:T(2,128)S(1)}, u32[]{:S(2)}, u32[]{:S(2)}) async-start(f32[128,1,2,512]{3,2,1,0:T(2,128)} %bitcast.24), calls=%async_computation.1 | async-start | bytes 1048576 | tf_op jit(solution)/shard_map/all_to_all | solution.py:89

commit v13 on v12

--- a/solution.py
+++ b/solution.py
@@ -45,8 +45,13 @@
 
     flat_cells = probes.reshape(-1)
     cell_ids = jnp.arange(cell_count, dtype=jnp.int32)
-    contains = jnp.any(probes[:, :, None] == cell_ids[None, None, :], axis=1)
-    counted = contains.astype(jnp.int32)
+    probe_hot = (flat_cells[:, None] == cell_ids[None, :]).astype(jnp.bfloat16)
+    row_of = jnp.arange(query_rows * probe_count, dtype=jnp.int32) // probe_count
+    row_hot = (jnp.arange(query_rows)[:, None] == row_of[None, :]).astype(jnp.bfloat16)
+    counted = jnp.einsum(
+        "rp,pc->rc", row_hot, probe_hot, preferred_element_type=jnp.float32
+    ).astype(jnp.int32)
+    contains = counted > 0
     earlier_rows = jnp.cumsum(counted, axis=0) - counted
     rank_of = jnp.take_along_axis(earlier_rows, probes, axis=1)
     slot_rank = rank_of.reshape(-1)

time: 82.2 us -> 82.4 us (level)
    reduce_or x1 -> x0, other arithmetic: 0.84 us -> none  [body(): contains = jnp.any(probes[:, :, None] == cell_ids[None, None, :], axis=1)]
where the time goes in v13:
time: 82.4 us; the launch traced here: 82 us
  waiting for transfers between devices  27 us (33%)
  starting transfers between devices  21.7 us (26%)
  matrix products  19.6 us (24%)
  local copies, waits for them, and re-layouts  8.75 us (11%)
  other arithmetic  4.06 us (5%)
  between operations  0.84 us (1%)
    dot_general x1, matrix products, rebuilt_slots(): jnp.einsum('mvk,mkd->vmd', one_hot, parts, preferred_element_type=jnp.flo...  17.8 us
    all_to_all x1, waiting for transfers between devices, body(): lax.all_to_all(scored, 'list', split_axis=0, concat_axis=0, tiled=True)  16.9 us
    all_to_all x1, starting transfers between devices, body(): lax.all_to_all(outgoing, 'list', split_axis=0, concat_axis=0, tiled=True)  15 us
    all_to_all x1, waiting for transfers between devices, body(): lax.all_to_all(outgoing, 'list', split_axis=0, concat_axis=0, tiled=True)  8.89 us
    all_to_all x1, starting transfers between devices, body(): lax.all_to_all(scored, 'list', split_axis=0, concat_axis=0, tiled=True)  6.63 us
    reduce_sum x1, other arithmetic, body(): slot_norm = jnp.sum(rebuilt * rebuilt, axis=1)  2.22 us
    gather x3, local copies, waits for them, and re-layouts, body(): rank_of = jnp.take_along_axis(earlier_rows, probes, axis=1)  1.67 us
  transfers between devices with their start and end apart: 3, of which 3 were waited for; matrix products, arithmetic and copies ran while one was open for 27% of the time, Pallas kernels for 0%

profile of v13, /device:TPU:32, one launch (start us, length us, event | category | flops | bytes accessed | tf_op | source)
XLA Modules:
  0.0 82.0 jit_solution(8057009102389393847)
XLA Ops:
  0.0 0.8 fusion.24
  0.8 0.8 eq.138
  1.6 0.2 broadcast_compare_fusion
  1.9 0.3 convolution_bitcast_fusion
  2.3 1.6 %copy.10 = f32[128,1,2,8,128]{4,3,2,1,0:T(8,128)} copy(f32[128,1,2,8,128]{4,0,3,2,1:T(8,128)S(1)} %convolution_bitcast_fusion) | data formatting | bytes 2097152 | tf_op jit(solution)/shard_map/reshape | solution.py:73
  3.9 15.0 %all-to-all-start = ((f32[128,1,2,8,128]{4,3,2,1,0:T(8,128)}), f32[128,1,2,8,128]{4,3,2,1,0:T(8,128)S(1)}, u32[]{:S(2)}, u32[]{:S(2)}) async-start(f32[128,1,2,8,128]{4,3,2,1,0:T(8,128)} %copy.10), calls=%async_computation | async-start | bytes 2097152 | tf_op jit(solution)/shard_map/all_to_all | solution.py:74
  18.9 0.1 collective-permute-start
  19.7 1.2 %collective-permute-done = f32[32,16,256]{2,1,0:T(8,128)S(1)} collective-permute-done((f32[32,16,256]{2,1,0:T(8,128)S(1)}, f32[32,16,256]{2,1,0:T(8,128)S(1)}, u32[]{:S(2)}, u32[]{:S(2)}) %collective-permute-start) | collective-permute-done | bytes 524320 | tf_op jit(solution)/shard_map/ppermute | solution.py:38
  20.9 0.1 broadcast_select_fusion.1
  21.0 0.3 reduce-precision_convert_fusion.1
  21.3 17.8 %fusion.2 = f32[512,64,48]{0,2,1:T(8,128)S(1)} fusion(s32[64,512]{1,0:T(8,128)S(1)} %bitcast.75, bf16[64,256,16]{1,2,0:T(8,128)(2,1)S(1)} %get-tuple-element.9, bf16[64,256,16]{1,2,0:T(8,128)(2,1)S(1)} %get-tuple-element.8, bf16[64,256,16]{1,2,0:T(8,128)(2,1)S(1)} %get-tuple-element.7), kind=kOutput, calls=%fused_computation.5 | convolution fusion | flops 818413568 | bytes 7995392 | tf_op jit(solution)/shard_map/mvk,mkd->vmd/dot_general | solution.py:23
  39.1 2.2 %multiply_reduce_fusion = (f32[512]{0:T(512)S(1)}, f32[512,64,16]{0,2,1:T(8,128)}) fusion(f32[512,64,48]{0,2,1:T(8,128)S(1)} %fusion.2), kind=kLoop, calls=%fused_computation.8 | loop fusion | flops 2096640 | bytes 8390656 | tf_op jit(solution)/shard_map/reduce_sum | solution.py:85
  41.3 8.9 %all-to-all-done = f32[128,1,2,8,128]{4,3,2,1,0:T(8,128)S(1)} async-done(((f32[128,1,2,8,128]{4,3,2,1,0:T(8,128)}), f32[128,1,2,8,128]{4,3,2,1,0:T(8,128)S(1)}, u32[]{:S(2)}, u32[]{:S(2)}) %all-to-all-start) | async-done | bytes 1048608 | tf_op jit(solution)/shard_map/all_to_all | solution.py:74
  50.2 0.5 fusion.14
  50.7 0.1 add.64
  51.0 1.5 %copy-done.1 = f32[512,64,16]{0,2,1:T(8,128)S(1)} copy-done((f32[512,64,16]{0,2,1:T(8,128)S(1)}, f32[512,64,16]{0,2,1:T(8,128)}, u32[]{:S(2)}) %copy-start.1) | copy-done | bytes 2097176
  52.5 1.2 %fusion.9 = f32[256,512]{1,0:T(8,128)S(1)} fusion(f32[512,1024]{0,1:T(8,128)S(1)} %bitcast.70, f32[32,8,8,128]{3,2,1,0:T(8,128)S(1)} %bitcast.71, f32[512]{0:T(512)S(1)} %get-tuple-element.5, f32[256]{0:T(256)S(1)} %add.64, pred[512]{0:T(512)(128)(4,1)S(1)} %iota_compare_fusion.8), kind=kOutput, calls=%fused_computation.21 | convolution fusion | flops 805830656 | bytes 3673600 | tf_op jit(solution)/shard_map/sf,vf->sv/dot_general | solution.py:86
  53.7 1.1 %stack_reshape.3 = f32[128,1,2,512]{3,2,0,1:T(2,128)} reshape(f32[256,512]{1,0:T(8,128)S(1)} %fusion.9) | data formatting | bytes 1048576 | tf_op jit(solution)/shard_map/stack;reshape | solution.py:93
  54.8 6.6 %all-to-all-start.1 = ((f32[128,1,2,512]{3,2,1,0:T(2,128)}), f32[128,1,2,512]{3,2,1,0:T(2,128)S(1)}, u32[]{:S(2)}, u32[]{:S(2)}) async-start(f32[128,1,2,512]{3,2,1,0:T(2,128)} %bitcast.24), calls=%async_computation.1 | async-start | bytes 1048576 | tf_op jit(solution)/shard_map/all_to_all | solution.py:94
  61.6 1.5 %gather_fusion.1 = s32[128]{0:T(128)S(1)} fusion(s32[4,128]{1,0:T(4,128)S(1)} %sub.45, s32[128]{0:T(128)S(1)} %reshape.319), kind=kCustom, calls=%fused_computation.1 | custom fusion | bytes 2048 | tf_op jit(solution)/shard_map/jit(take_along_axis)/gather | solution.py:56
  63.2 0.1 add.73
  63.3 16.9 %all-to-all-done.1 = f32[128,1,2,512]{3,2,1,0:T(2,128)S(1)} async-done(((f32[128,1,2,512]{3,2,1,0:T(2,128)}), f32[128,1,2,512]{3,2,1,0:T(2,128)S(1)}, u32[]{:S(2)}, u32[]{:S(2)}) %all-to-all-start.1) | async-done | bytes 524320 | tf_op jit(solution)/shard_map/all_to_all | solution.py:94
  80.2 0.4 reshape.308
  80.5 1.5 %gather_fusion = f32[128,512]{1,0:T(8,128)} fusion(f32[256,512]{1,0:T(8,128)S(1)} %reshape.308, s32[1024]{0:T(1024)S(1)} %pad_clamp_fusion), kind=kCustom, calls=%fused_computation | custom fusion | bytes 524800 | tf_op jit(solution)/shard_map/gather | solution.py:96
  (27 shorter events, 0.4 us)
Async XLA Ops:
  0.0 19.7 %copy-start = (f32[128,1024]{1,0:T(8,128)S(1)}, f32[128,1024]{1,0:T(8,128)}, u32[]{:S(2)}) copy-start(f32[128,1024]{1,0:T(8,128)} %param.8) | copy-start | bytes 1572868
  2.3 16.6 %copy-start.2 = (f32[32,16,256]{2,1,0:T(8,128)S(1)}, f32[32,16,256]{2,1,0:T(8,128)}, u32[]{:S(2)}) copy-start(f32[32,16,256]{2,1,0:T(8,128)} %param.9) | copy-start | bytes 1572868
  3.9 46.4 %all-to-all-start = ((f32[128,1,2,8,128]{4,3,2,1,0:T(8,128)}), f32[128,1,2,8,128]{4,3,2,1,0:T(8,128)S(1)}, u32[]{:S(2)}, u32[]{:S(2)}) async-start(f32[128,1,2,8,128]{4,3,2,1,0:T(8,128)} %copy.10), calls=%async_computation | async-start | bytes 2097152 | tf_op jit(solution)/shard_map/all_to_all | solution.py:74
  18.9 2.0 %collective-permute-start = (f32[32,16,256]{2,1,0:T(8,128)S(1)}, f32[32,16,256]{2,1,0:T(8,128)S(1)}, u32[]{:S(2)}, u32[]{:S(2)}) collective-permute-start(f32[32,16,256]{2,1,0:T(8,128)S(1)} %copy-done.2), channel_id=1, source_target_pairs={{0,128},{128,0},{1,129},{129,1},{2,130},{130,2},{3,131},{131,3},{4... | collective-permute-start | bytes 1572872 | tf_op jit(solution)/shard_map/ppermute | solution.py:38
  19.7 1.6 %copy-start.4 = (s32[1,64,512]{2,1,0:T(8,128)S(1)}, s32[1,64,512]{2,1,0:T(8,128)}, u32[]{:S(2)}) copy-start(s32[1,64,512]{2,1,0:T(8,128)} %param.10) | copy-start | bytes 393220
  50.9 1.6 %copy-start.1 = (f32[512,64,16]{0,2,1:T(8,128)S(1)}, f32[512,64,16]{0,2,1:T(8,128)}, u32[]{:S(2)}) copy-start(f32[512,64,16]{0,2,1:T(8,128)} %get-tuple-element.6) | copy-start | bytes 6291460
  52.5 9.0 %copy-start.3 = (s32[4,32]{1,0:T(4,128)S(1)}, s32[4,32]{1,0:T(4,128)}, u32[]{:S(2)}) copy-start(s32[4,32]{1,0:T(4,128)} %param.7) | copy-start | bytes 1540
  54.8 25.3 %all-to-all-start.1 = ((f32[128,1,2,512]{3,2,1,0:T(2,128)}), f32[128,1,2,512]{3,2,1,0:T(2,128)S(1)}, u32[]{:S(2)}, u32[]{:S(2)}) async-start(f32[128,1,2,512]{3,2,1,0:T(2,128)} %bitcast.24), calls=%async_computation.1 | async-start | bytes 1048576 | tf_op jit(solution)/shard_map/all_to_all | solution.py:94

commit v14 on v12

--- a/solution.py
+++ b/solution.py
@@ -88,7 +88,16 @@
     scored = jnp.stack(scored, axis=1)
     returned = lax.all_to_all(scored, "list", split_axis=0, concat_axis=0, tiled=True)
     returned = returned.reshape(cell_count * slot_count, capacity)
-    result = returned[flat_cells * slot_count + slot_rank]
+    picks = flat_cells * slot_count + slot_rank
+    pick_hot = (
+        picks[:, None] == jnp.arange(cell_count * slot_count, dtype=jnp.int32)[None, :]
+    ).astype(jnp.bfloat16)
+    picked = jnp.einsum(
+        "pr,rf->pf", pick_hot, exact_parts(returned), preferred_element_type=jnp.float32
+    )
+    result = (
+        picked[:, :capacity] + picked[:, capacity : 2 * capacity]
+    ) + picked[:, 2 * capacity :]
     return result.reshape(query_rows, probe_count, capacity)
 
 

time: 82.2 us -> 81.9 us (level)
  local copies, waits for them, and re-layouts: 7.98 us -> 6.52 us
  other arithmetic: 4.83 us -> 5.7 us
    gather x1 -> x0, local copies, waits for them, and re-layouts: 1.45 us -> none  [body(): result = returned[flat_cells * slot_count + slot_rank]]
where the time goes in v14:
time: 81.9 us; the launch traced here: 81.5 us
  waiting for transfers between devices  27 us (33%)
  starting transfers between devices  21.7 us (26%)
  matrix products  19.7 us (24%)
  local copies, waits for them, and re-layouts  6.52 us (8%)
  other arithmetic  5.7 us (7%)
  between operations  0.86 us (1%)
    dot_general x1, matrix products, rebuilt_slots(): jnp.einsum('mvk,mkd->vmd', one_hot, parts, preferred_element_type=jnp.flo...  17.8 us
    all_to_all x1, waiting for transfers between devices, body(): lax.all_to_all(scored, 'list', split_axis=0, concat_axis=0, tiled=True)  16.9 us
    all_to_all x1, starting transfers between devices, body(): lax.all_to_all(outgoing, 'list', split_axis=0, concat_axis=0, tiled=True)  15 us
    all_to_all x1, waiting for transfers between devices, body(): lax.all_to_all(outgoing, 'list', split_axis=0, concat_axis=0, tiled=True)  8.9 us
    all_to_all x1, starting transfers between devices, body(): lax.all_to_all(scored, 'list', split_axis=0, concat_axis=0, tiled=True)  6.63 us
    reduce_sum x1, other arithmetic, body(): slot_norm = jnp.sum(rebuilt * rebuilt, axis=1)  2.22 us
    gather x3, local copies, waits for them, and re-layouts, body(): rank_of = jnp.take_along_axis(earlier_rows, probes, axis=1)  1.67 us
  transfers between devices with their start and end apart: 3, of which 3 were waited for; matrix products, arithmetic and copies ran while one was open for 27% of the time, Pallas kernels for 0%

profile of v14, /device:TPU:32, one launch (start us, length us, event | category | flops | bytes accessed | tf_op | source)
XLA Modules:
  0.0 81.5 jit_solution(15919921463268469883)
XLA Ops:
  0.0 0.8 %fusion.23 = pred[4,128]{1,0:T(4,128)(4,1)S(1)} fusion(s32[4,32]{1,0:T(4,128)} %param.7), kind=kLoop, calls=%fused_computation.47 | loop fusion | flops 32256 | bytes 1024 | tf_op jit(solution)/shard_map/reduce_or | solution.py:48
  0.9 0.7 fusion.32
  1.7 0.3 convolution_bitcast_fusion
  2.1 1.6 %copy.15 = f32[128,1,2,8,128]{4,3,2,1,0:T(8,128)} copy(f32[128,1,2,8,128]{4,0,3,2,1:T(8,128)S(1)} %convolution_bitcast_fusion) | data formatting | bytes 2097152 | tf_op jit(solution)/shard_map/reshape | solution.py:68
  3.7 15.0 %all-to-all-start = ((f32[128,1,2,8,128]{4,3,2,1,0:T(8,128)}), f32[128,1,2,8,128]{4,3,2,1,0:T(8,128)S(1)}, u32[]{:S(2)}, u32[]{:S(2)}) async-start(f32[128,1,2,8,128]{4,3,2,1,0:T(8,128)} %copy.15), calls=%async_computation | async-start | bytes 2097152 | tf_op jit(solution)/shard_map/all_to_all | solution.py:69
  18.7 0.1 collective-permute-start
  19.5 1.2 %collective-permute-done = f32[32,16,256]{2,1,0:T(8,128)S(1)} collective-permute-done((f32[32,16,256]{2,1,0:T(8,128)S(1)}, f32[32,16,256]{2,1,0:T(8,128)S(1)}, u32[]{:S(2)}, u32[]{:S(2)}) %collective-permute-start) | collective-permute-done | bytes 524320 | tf_op jit(solution)/shard_map/ppermute | solution.py:38
  20.7 0.1 broadcast_select_fusion.1
  20.8 0.3 reduce-precision_convert_fusion.1
  21.1 17.8 %fusion.2 = f32[512,64,48]{0,2,1:T(8,128)S(1)} fusion(s32[64,512]{1,0:T(8,128)S(1)} %bitcast.73, bf16[64,256,16]{1,2,0:T(8,128)(2,1)S(1)} %get-tuple-element.9, bf16[64,256,16]{1,2,0:T(8,128)(2,1)S(1)} %get-tuple-element.8, bf16[64,256,16]{1,2,0:T(8,128)(2,1)S(1)} %get-tuple-element.7), kind=kOutput, calls=%fused_computation.4 | convolution fusion | flops 818413568 | bytes 7995392 | tf_op jit(solution)/shard_map/mvk,mkd->vmd/dot_general | solution.py:23
  38.9 2.2 %multiply_reduce_fusion = (f32[512]{0:T(512)S(1)}, f32[512,64,16]{0,2,1:T(8,128)}) fusion(f32[512,64,48]{0,2,1:T(8,128)S(1)} %fusion.2), kind=kLoop, calls=%fused_computation.7 | loop fusion | flops 2096640 | bytes 8390656 | tf_op jit(solution)/shard_map/reduce_sum | solution.py:80
  41.2 8.9 %all-to-all-done = f32[128,1,2,8,128]{4,3,2,1,0:T(8,128)S(1)} async-done(((f32[128,1,2,8,128]{4,3,2,1,0:T(8,128)}), f32[128,1,2,8,128]{4,3,2,1,0:T(8,128)S(1)}, u32[]{:S(2)}, u32[]{:S(2)}) %all-to-all-start) | async-done | bytes 1048608 | tf_op jit(solution)/shard_map/all_to_all | solution.py:69
  50.1 0.5 fusion.14
  50.6 0.1 add.53
  50.8 1.5 %copy-done.1 = f32[512,64,16]{0,2,1:T(8,128)S(1)} copy-done((f32[512,64,16]{0,2,1:T(8,128)S(1)}, f32[512,64,16]{0,2,1:T(8,128)}, u32[]{:S(2)}) %copy-start.1) | copy-done | bytes 2097176
  52.3 1.2 %fusion.9 = f32[256,512]{1,0:T(8,128)S(1)} fusion(f32[512,1024]{0,1:T(8,128)S(1)} %bitcast.68, f32[32,8,8,128]{3,2,1,0:T(8,128)S(1)} %bitcast.69, f32[512]{0:T(512)S(1)} %get-tuple-element.5, f32[256]{0:T(256)S(1)} %add.53, pred[512]{0:T(512)(128)(4,1)S(1)} %iota_compare_fusion.8), kind=kOutput, calls=%fused_computation.20 | convolution fusion | flops 805830656 | bytes 3673600 | tf_op jit(solution)/shard_map/sf,vf->sv/dot_general | solution.py:81
  53.5 1.1 %stack_reshape.3 = f32[128,1,2,512]{3,2,0,1:T(2,128)} reshape(f32[256,512]{1,0:T(8,128)S(1)} %fusion.9) | data formatting | bytes 1048576 | tf_op jit(solution)/shard_map/stack;reshape | solution.py:88
  54.6 6.6 %all-to-all-start.1 = ((f32[128,1,2,512]{3,2,1,0:T(2,128)}), f32[128,1,2,512]{3,2,1,0:T(2,128)S(1)}, u32[]{:S(2)}, u32[]{:S(2)}) async-start(f32[128,1,2,512]{3,2,1,0:T(2,128)} %bitcast.25), calls=%async_computation.1 | async-start | bytes 1048576 | tf_op jit(solution)/shard_map/all_to_all | solution.py:89
  61.4 1.5 %gather_fusion = s32[128]{0:T(128)S(1)} fusion(s32[4,128]{1,0:T(4,128)S(1)} %convert_subtract_fusion, s32[128]{0:T(128)S(1)} %reshape.274), kind=kCustom, calls=%fused_computation | custom fusion | bytes 2048 | tf_op jit(solution)/shard_map/jit(take_along_axis)/gather | solution.py:51
  63.1 16.9 %all-to-all-done.1 = f32[128,1,2,512]{3,2,1,0:T(2,128)S(1)} async-done(((f32[128,1,2,512]{3,2,1,0:T(2,128)}), f32[128,1,2,512]{3,2,1,0:T(2,128)S(1)}, u32[]{:S(2)}, u32[]{:S(2)}) %all-to-all-start.1) | async-done | bytes 524320 | tf_op jit(solution)/shard_map/all_to_all | solution.py:89
  80.0 0.4 reshape.272
  80.3 0.1 reduce-precision_convert_fusion.3
  80.5 0.3 fusion.15
  80.8 0.8 slice_add_fusion.2
  (26 shorter events, 0.5 us)
Async XLA Ops:
  0.0 19.5 %copy-start = (f32[128,1024]{1,0:T(8,128)S(1)}, f32[128,1024]{1,0:T(8,128)}, u32[]{:S(2)}) copy-start(f32[128,1024]{1,0:T(8,128)} %param.8) | copy-start | bytes 1572868
  2.1 16.6 %copy-start.2 = (f32[32,16,256]{2,1,0:T(8,128)S(1)}, f32[32,16,256]{2,1,0:T(8,128)}, u32[]{:S(2)}) copy-start(f32[32,16,256]{2,1,0:T(8,128)} %param.9) | copy-start | bytes 1572868
  3.7 46.4 %all-to-all-start = ((f32[128,1,2,8,128]{4,3,2,1,0:T(8,128)}), f32[128,1,2,8,128]{4,3,2,1,0:T(8,128)S(1)}, u32[]{:S(2)}, u32[]{:S(2)}) async-start(f32[128,1,2,8,128]{4,3,2,1,0:T(8,128)} %copy.15), calls=%async_computation | async-start | bytes 2097152 | tf_op jit(solution)/shard_map/all_to_all | solution.py:69
  18.7 2.0 %collective-permute-start = (f32[32,16,256]{2,1,0:T(8,128)S(1)}, f32[32,16,256]{2,1,0:T(8,128)S(1)}, u32[]{:S(2)}, u32[]{:S(2)}) collective-permute-start(f32[32,16,256]{2,1,0:T(8,128)S(1)} %copy-done.2), channel_id=1, source_target_pairs={{0,128},{128,0},{1,129},{129,1},{2,130},{130,2},{3,131},{131,3},{4... | collective-permute-start | bytes 1572872 | tf_op jit(solution)/shard_map/ppermute | solution.py:38
  19.5 1.6 %copy-start.4 = (s32[1,64,512]{2,1,0:T(8,128)S(1)}, s32[1,64,512]{2,1,0:T(8,128)}, u32[]{:S(2)}) copy-start(s32[1,64,512]{2,1,0:T(8,128)} %param.10) | copy-start | bytes 393220
  50.7 1.6 %copy-start.1 = (f32[512,64,16]{0,2,1:T(8,128)S(1)}, f32[512,64,16]{0,2,1:T(8,128)}, u32[]{:S(2)}) copy-start(f32[512,64,16]{0,2,1:T(8,128)} %get-tuple-element.6) | copy-start | bytes 6291460
  52.3 9.0 %copy-start.3 = (s32[4,32]{1,0:T(4,128)S(1)}, s32[4,32]{1,0:T(4,128)}, u32[]{:S(2)}) copy-start(s32[4,32]{1,0:T(4,128)} %param.7) | copy-start | bytes 1540
  54.6 25.3 %all-to-all-start.1 = ((f32[128,1,2,512]{3,2,1,0:T(2,128)}), f32[128,1,2,512]{3,2,1,0:T(2,128)S(1)}, u32[]{:S(2)}, u32[]{:S(2)}) async-start(f32[128,1,2,512]{3,2,1,0:T(2,128)} %bitcast.25), calls=%async_computation.1 | async-start | bytes 1048576 | tf_op jit(solution)/shard_map/all_to_all | solution.py:89

commit v15 on v14

--- a/solution.py
+++ b/solution.py
@@ -84,7 +84,7 @@
         total = (own_norm[:, None] + slot_norm[None, :]) - 2.0 * cross
         valid = positions < cell_sizes[local]
         total = jnp.where(valid[None, :], total, jnp.zeros((), jnp.float32))
-        scored.append(total.reshape(list_size, slot_count, capacity))
+        scored.append(total.reshape(list_size, slot_count, capacity // 128, 128))
     scored = jnp.stack(scored, axis=1)
     returned = lax.all_to_all(scored, "list", split_axis=0, concat_axis=0, tiled=True)
     returned = returned.reshape(cell_count * slot_count, capacity)

time: 81.9 us -> 81.4 us (level)
  no operation moved by 1% of the time
where the time goes in v15:
time: 81.4 us; the launch traced here: 81 us
  waiting for transfers between devices  27 us (33%)
  starting transfers between devices  21.7 us (27%)
  matrix products  19.7 us (24%)
  local copies, waits for them, and re-layouts  6.02 us (7%)
  other arithmetic  5.7 us (7%)
  between operations  0.86 us (1%)
    dot_general x1, matrix products, rebuilt_slots(): jnp.einsum('mvk,mkd->vmd', one_hot, parts, preferred_element_type=jnp.flo...  17.8 us
    all_to_all x1, waiting for transfers between devices, body(): lax.all_to_all(scored, 'list', split_axis=0, concat_axis=0, tiled=True)  16.9 us
    all_to_all x1, starting transfers between devices, body(): lax.all_to_all(outgoing, 'list', split_axis=0, concat_axis=0, tiled=True)  15 us
    all_to_all x1, waiting for transfers between devices, body(): lax.all_to_all(outgoing, 'list', split_axis=0, concat_axis=0, tiled=True)  8.9 us
    all_to_all x1, starting transfers between devices, body(): lax.all_to_all(scored, 'list', split_axis=0, concat_axis=0, tiled=True)  6.63 us
    reduce_sum x1, other arithmetic, body(): slot_norm = jnp.sum(rebuilt * rebuilt, axis=1)  2.22 us
    gather x3, local copies, waits for them, and re-layouts, body(): rank_of = jnp.take_along_axis(earlier_rows, probes, axis=1)  1.67 us
  transfers between devices with their start and end apart: 3, of which 3 were waited for; matrix products, arithmetic and copies ran while one was open for 27% of the time, Pallas kernels for 0%

profile of v15, /device:TPU:32, one launch (start us, length us, event | category | flops | bytes accessed | tf_op | source)
XLA Modules:
  0.0 81.0 jit_solution(3408516778342246905)
XLA Ops:
  0.0 0.8 %fusion.23 = pred[4,128]{1,0:T(4,128)(4,1)S(1)} fusion(s32[4,32]{1,0:T(4,128)} %param.7), kind=kLoop, calls=%fused_computation.47 | loop fusion | flops 32256 | bytes 1024 | tf_op jit(solution)/shard_map/reduce_or | solution.py:48
  0.9 0.7 fusion.32
  1.7 0.3 convolution_bitcast_fusion
  2.1 1.6 %copy.15 = f32[128,1,2,8,128]{4,3,2,1,0:T(8,128)} copy(f32[128,1,2,8,128]{4,0,3,2,1:T(8,128)S(1)} %convolution_bitcast_fusion) | data formatting | bytes 2097152 | tf_op jit(solution)/shard_map/reshape | solution.py:68
  3.7 15.0 %all-to-all-start = ((f32[128,1,2,8,128]{4,3,2,1,0:T(8,128)}), f32[128,1,2,8,128]{4,3,2,1,0:T(8,128)S(1)}, u32[]{:S(2)}, u32[]{:S(2)}) async-start(f32[128,1,2,8,128]{4,3,2,1,0:T(8,128)} %copy.15), calls=%async_computation | async-start | bytes 2097152 | tf_op jit(solution)/shard_map/all_to_all | solution.py:69
  18.7 0.1 collective-permute-start
  19.5 1.2 %collective-permute-done = f32[32,16,256]{2,1,0:T(8,128)S(1)} collective-permute-done((f32[32,16,256]{2,1,0:T(8,128)S(1)}, f32[32,16,256]{2,1,0:T(8,128)S(1)}, u32[]{:S(2)}, u32[]{:S(2)}) %collective-permute-start) | collective-permute-done | bytes 524320 | tf_op jit(solution)/shard_map/ppermute | solution.py:38
  20.7 0.1 broadcast_select_fusion.1
  20.8 0.3 reduce-precision_convert_fusion.1
  21.1 17.8 %fusion.2 = f32[512,64,48]{0,2,1:T(8,128)S(1)} fusion(s32[64,512]{1,0:T(8,128)S(1)} %bitcast.83, bf16[64,256,16]{1,2,0:T(8,128)(2,1)S(1)} %get-tuple-element.9, bf16[64,256,16]{1,2,0:T(8,128)(2,1)S(1)} %get-tuple-element.8, bf16[64,256,16]{1,2,0:T(8,128)(2,1)S(1)} %get-tuple-element.7), kind=kOutput, calls=%fused_computation.4 | convolution fusion | flops 818413568 | bytes 7995392 | tf_op jit(solution)/shard_map/mvk,mkd->vmd/dot_general | solution.py:23
  38.9 2.2 %multiply_reduce_fusion = (f32[512]{0:T(512)S(1)}, f32[512,64,16]{0,2,1:T(8,128)}) fusion(f32[512,64,48]{0,2,1:T(8,128)S(1)} %fusion.2), kind=kLoop, calls=%fused_computation.7 | loop fusion | flops 2096640 | bytes 8390656 | tf_op jit(solution)/shard_map/reduce_sum | solution.py:80
  41.2 8.9 %all-to-all-done = f32[128,1,2,8,128]{4,3,2,1,0:T(8,128)S(1)} async-done(((f32[128,1,2,8,128]{4,3,2,1,0:T(8,128)}), f32[128,1,2,8,128]{4,3,2,1,0:T(8,128)S(1)}, u32[]{:S(2)}, u32[]{:S(2)}) %all-to-all-start) | async-done | bytes 1048608 | tf_op jit(solution)/shard_map/all_to_all | solution.py:69
  50.1 0.5 fusion.14
  50.6 0.1 add.53
  50.8 1.5 %copy-done.1 = f32[512,64,16]{0,2,1:T(8,128)S(1)} copy-done((f32[512,64,16]{0,2,1:T(8,128)S(1)}, f32[512,64,16]{0,2,1:T(8,128)}, u32[]{:S(2)}) %copy-start.1) | copy-done | bytes 2097176
  52.3 1.2 %fusion.9 = f32[256,512]{1,0:T(8,128)S(1)} fusion(f32[512,1024]{0,1:T(8,128)S(1)} %bitcast.77, f32[32,8,8,128]{3,2,1,0:T(8,128)S(1)} %bitcast.78, f32[512]{0:T(512)S(1)} %get-tuple-element.5, f32[256]{0:T(256)S(1)} %add.53, pred[512]{0:T(512)(128)(4,1)S(1)} %iota_compare_fusion.8), kind=kOutput, calls=%fused_computation.20 | convolution fusion | flops 805830656 | bytes 3673600 | tf_op jit(solution)/shard_map/sf,vf->sv/dot_general | solution.py:81
  53.5 1.0 %stack_reshape.3 = f32[128,1,2,4,128]{4,3,2,0,1:T(4,128)} reshape(f32[256,512]{1,0:T(8,128)S(1)} %fusion.9) | data formatting | bytes 1048576 | tf_op jit(solution)/shard_map/stack;reshape | solution.py:88
  54.5 6.6 %all-to-all-start.1 = ((f32[128,1,2,4,128]{4,3,2,1,0:T(4,128)}), f32[128,1,2,4,128]{4,3,2,1,0:T(4,128)S(1)}, u32[]{:S(2)}, u32[]{:S(2)}) async-start(f32[128,1,2,4,128]{4,3,2,1,0:T(4,128)} %bitcast.25), calls=%async_computation.1 | async-start | bytes 1048576 | tf_op jit(solution)/shard_map/all_to_all | solution.py:89
  61.2 1.5 %gather_fusion = s32[128]{0:T(128)S(1)} fusion(s32[4,128]{1,0:T(4,128)S(1)} %convert_subtract_fusion, s32[128]{0:T(128)S(1)} %reshape.274), kind=kCustom, calls=%fused_computation | custom fusion | bytes 2048 | tf_op jit(solution)/shard_map/jit(take_along_axis)/gather | solution.py:51
  62.8 0.1 add.51
  62.9 16.9 %all-to-all-done.1 = f32[128,1,2,4,128]{4,3,2,1,0:T(4,128)S(1)} async-done(((f32[128,1,2,4,128]{4,3,2,1,0:T(4,128)}), f32[128,1,2,4,128]{4,3,2,1,0:T(4,128)S(1)}, u32[]{:S(2)}, u32[]{:S(2)}) %all-to-all-start.1) | async-done | bytes 524320 | tf_op jit(solution)/shard_map/all_to_all | solution.py:89
  79.8 0.1 reduce-precision_convert_fusion.3
  80.0 0.3 fusion.15
  80.3 0.8 slice_add_fusion.2
  (25 shorter events, 0.4 us)
Async XLA Ops:
  0.0 19.5 %copy-start = (f32[128,1024]{1,0:T(8,128)S(1)}, f32[128,1024]{1,0:T(8,128)}, u32[]{:S(2)}) copy-start(f32[128,1024]{1,0:T(8,128)} %param.8) | copy-start | bytes 1572868
  2.1 16.6 %copy-start.2 = (f32[32,16,256]{2,1,0:T(8,128)S(1)}, f32[32,16,256]{2,1,0:T(8,128)}, u32[]{:S(2)}) copy-start(f32[32,16,256]{2,1,0:T(8,128)} %param.9) | copy-start | bytes 1572868
  3.7 46.4 %all-to-all-start = ((f32[128,1,2,8,128]{4,3,2,1,0:T(8,128)}), f32[128,1,2,8,128]{4,3,2,1,0:T(8,128)S(1)}, u32[]{:S(2)}, u32[]{:S(2)}) async-start(f32[128,1,2,8,128]{4,3,2,1,0:T(8,128)} %copy.15), calls=%async_computation | async-start | bytes 2097152 | tf_op jit(solution)/shard_map/all_to_all | solution.py:69
  18.7 2.0 %collective-permute-start = (f32[32,16,256]{2,1,0:T(8,128)S(1)}, f32[32,16,256]{2,1,0:T(8,128)S(1)}, u32[]{:S(2)}, u32[]{:S(2)}) collective-permute-start(f32[32,16,256]{2,1,0:T(8,128)S(1)} %copy-done.2), channel_id=1, source_target_pairs={{0,128},{128,0},{1,129},{129,1},{2,130},{130,2},{3,131},{131,3},{4... | collective-permute-start | bytes 1572872 | tf_op jit(solution)/shard_map/ppermute | solution.py:38
  19.5 1.6 %copy-start.4 = (s32[1,64,512]{2,1,0:T(8,128)S(1)}, s32[1,64,512]{2,1,0:T(8,128)}, u32[]{:S(2)}) copy-start(s32[1,64,512]{2,1,0:T(8,128)} %param.10) | copy-start | bytes 393220
  50.7 1.6 %copy-start.1 = (f32[512,64,16]{0,2,1:T(8,128)S(1)}, f32[512,64,16]{0,2,1:T(8,128)}, u32[]{:S(2)}) copy-start(f32[512,64,16]{0,2,1:T(8,128)} %get-tuple-element.6) | copy-start | bytes 6291460
  52.3 8.8 %copy-start.3 = (s32[4,32]{1,0:T(4,128)S(1)}, s32[4,32]{1,0:T(4,128)}, u32[]{:S(2)}) copy-start(s32[4,32]{1,0:T(4,128)} %param.7) | copy-start | bytes 1540
  54.5 25.3 %all-to-all-start.1 = ((f32[128,1,2,4,128]{4,3,2,1,0:T(4,128)}), f32[128,1,2,4,128]{4,3,2,1,0:T(4,128)S(1)}, u32[]{:S(2)}, u32[]{:S(2)}) async-start(f32[128,1,2,4,128]{4,3,2,1,0:T(4,128)} %bitcast.25), calls=%async_computation.1 | async-start | bytes 1048576 | tf_op jit(solution)/shard_map/all_to_all | solution.py:89

commit v16 on v15

--- a/solution.py
+++ b/solution.py
@@ -84,7 +84,7 @@
         total = (own_norm[:, None] + slot_norm[None, :]) - 2.0 * cross
         valid = positions < cell_sizes[local]
         total = jnp.where(valid[None, :], total, jnp.zeros((), jnp.float32))
-        scored.append(total.reshape(list_size, slot_count, capacity // 128, 128))
+        scored.append(total.reshape(list_size, 1, slot_count * capacity // 128, 128))
     scored = jnp.stack(scored, axis=1)
     returned = lax.all_to_all(scored, "list", split_axis=0, concat_axis=0, tiled=True)
     returned = returned.reshape(cell_count * slot_count, capacity)

time: 81.4 us -> 81.4 us (level)
  no operation moved by 1% of the time
where the time goes in v16:
time: 81.4 us; the launch traced here: 81 us
  waiting for transfers between devices  27 us (33%)
  starting transfers between devices  21.7 us (27%)
  matrix products  19.7 us (24%)
  local copies, waits for them, and re-layouts  5.96 us (7%)
  other arithmetic  5.7 us (7%)
  between operations  0.86 us (1%)
    dot_general x1, matrix products, rebuilt_slots(): jnp.einsum('mvk,mkd->vmd', one_hot, parts, preferred_element_type=jnp.flo...  17.8 us
    all_to_all x1, waiting for transfers between devices, body(): lax.all_to_all(scored, 'list', split_axis=0, concat_axis=0, tiled=True)  16.9 us
    all_to_all x1, starting transfers between devices, body(): lax.all_to_all(outgoing, 'list', split_axis=0, concat_axis=0, tiled=True)  15 us
    all_to_all x1, waiting for transfers between devices, body(): lax.all_to_all(outgoing, 'list', split_axis=0, concat_axis=0, tiled=True)  8.9 us
    all_to_all x1, starting transfers between devices, body(): lax.all_to_all(scored, 'list', split_axis=0, concat_axis=0, tiled=True)  6.63 us
    reduce_sum x1, other arithmetic, body(): slot_norm = jnp.sum(rebuilt * rebuilt, axis=1)  2.22 us
    gather x3, local copies, waits for them, and re-layouts, body(): rank_of = jnp.take_along_axis(earlier_rows, probes, axis=1)  1.67 us
  transfers between devices with their start and end apart: 3, of which 3 were waited for; matrix products, arithmetic and copies ran while one was open for 27% of the time, Pallas kernels for 0%

profile of v16, /device:TPU:32, one launch (start us, length us, event | category | flops | bytes accessed | tf_op | source)
XLA Modules:
  0.0 81.0 jit_solution(9599490578945952739)
XLA Ops:
  0.0 0.8 %fusion.23 = pred[4,128]{1,0:T(4,128)(4,1)S(1)} fusion(s32[4,32]{1,0:T(4,128)} %param.7), kind=kLoop, calls=%fused_computation.47 | loop fusion | flops 32256 | bytes 1024 | tf_op jit(solution)/shard_map/reduce_or | solution.py:48
  0.9 0.7 fusion.32
  1.7 0.3 convolution_bitcast_fusion
  2.1 1.6 %copy.15 = f32[128,1,2,8,128]{4,3,2,1,0:T(8,128)} copy(f32[128,1,2,8,128]{4,0,3,2,1:T(8,128)S(1)} %convolution_bitcast_fusion) | data formatting | bytes 2097152 | tf_op jit(solution)/shard_map/reshape | solution.py:68
  3.7 15.0 %all-to-all-start = ((f32[128,1,2,8,128]{4,3,2,1,0:T(8,128)}), f32[128,1,2,8,128]{4,3,2,1,0:T(8,128)S(1)}, u32[]{:S(2)}, u32[]{:S(2)}) async-start(f32[128,1,2,8,128]{4,3,2,1,0:T(8,128)} %copy.15), calls=%async_computation | async-start | bytes 2097152 | tf_op jit(solution)/shard_map/all_to_all | solution.py:69
  18.7 0.1 collective-permute-start
  19.5 1.2 %collective-permute-done = f32[32,16,256]{2,1,0:T(8,128)S(1)} collective-permute-done((f32[32,16,256]{2,1,0:T(8,128)S(1)}, f32[32,16,256]{2,1,0:T(8,128)S(1)}, u32[]{:S(2)}, u32[]{:S(2)}) %collective-permute-start) | collective-permute-done | bytes 524320 | tf_op jit(solution)/shard_map/ppermute | solution.py:38
  20.7 0.1 broadcast_select_fusion.1
  20.8 0.3 reduce-precision_convert_fusion.1
  21.1 17.8 %fusion.2 = f32[512,64,48]{0,2,1:T(8,128)S(1)} fusion(s32[64,512]{1,0:T(8,128)S(1)} %bitcast.75, bf16[64,256,16]{1,2,0:T(8,128)(2,1)S(1)} %get-tuple-element.9, bf16[64,256,16]{1,2,0:T(8,128)(2,1)S(1)} %get-tuple-element.8, bf16[64,256,16]{1,2,0:T(8,128)(2,1)S(1)} %get-tuple-element.7), kind=kOutput, calls=%fused_computation.4 | convolution fusion | flops 818413568 | bytes 7995392 | tf_op jit(solution)/shard_map/mvk,mkd->vmd/dot_general | solution.py:23
  38.9 2.2 %multiply_reduce_fusion = (f32[512]{0:T(512)S(1)}, f32[512,64,16]{0,2,1:T(8,128)}) fusion(f32[512,64,48]{0,2,1:T(8,128)S(1)} %fusion.2), kind=kLoop, calls=%fused_computation.7 | loop fusion | flops 2096640 | bytes 8390656 | tf_op jit(solution)/shard_map/reduce_sum | solution.py:80
  41.2 8.9 %all-to-all-done = f32[128,1,2,8,128]{4,3,2,1,0:T(8,128)S(1)} async-done(((f32[128,1,2,8,128]{4,3,2,1,0:T(8,128)}), f32[128,1,2,8,128]{4,3,2,1,0:T(8,128)S(1)}, u32[]{:S(2)}, u32[]{:S(2)}) %all-to-all-start) | async-done | bytes 1048608 | tf_op jit(solution)/shard_map/all_to_all | solution.py:69
  50.1 0.5 fusion.14
  50.6 0.1 add.53
  50.8 1.5 %copy-done.1 = f32[512,64,16]{0,2,1:T(8,128)S(1)} copy-done((f32[512,64,16]{0,2,1:T(8,128)S(1)}, f32[512,64,16]{0,2,1:T(8,128)}, u32[]{:S(2)}) %copy-start.1) | copy-done | bytes 2097176
  52.3 1.2 %fusion.9 = f32[256,512]{1,0:T(8,128)S(1)} fusion(f32[512,1024]{0,1:T(8,128)S(1)} %bitcast.70, f32[32,8,8,128]{3,2,1,0:T(8,128)S(1)} %bitcast.71, f32[512]{0:T(512)S(1)} %get-tuple-element.5, f32[256]{0:T(256)S(1)} %add.53, pred[512]{0:T(512)(128)(4,1)S(1)} %iota_compare_fusion.8), kind=kOutput, calls=%fused_computation.20 | convolution fusion | flops 805830656 | bytes 3673600 | tf_op jit(solution)/shard_map/sf,vf->sv/dot_general | solution.py:81
  53.5 0.8 %stack_reshape.3 = f32[128,1,1,8,128]{4,3,0,2,1:T(8,128)} reshape(f32[256,512]{1,0:T(8,128)S(1)} %fusion.9) | data formatting | bytes 1048576 | tf_op jit(solution)/shard_map/stack;reshape | solution.py:88
  54.4 6.6 %all-to-all-start.1 = ((f32[128,1,1,8,128]{4,3,2,1,0:T(8,128)}), f32[128,1,1,8,128]{4,3,2,1,0:T(8,128)S(1)}, u32[]{:S(2)}, u32[]{:S(2)}) async-start(f32[128,1,1,8,128]{4,3,2,1,0:T(8,128)} %bitcast.25), calls=%async_computation.1 | async-start | bytes 1048576 | tf_op jit(solution)/shard_map/all_to_all | solution.py:89
  61.1 1.5 %gather_fusion = s32[128]{0:T(128)S(1)} fusion(s32[4,128]{1,0:T(4,128)S(1)} %convert_subtract_fusion, s32[128]{0:T(128)S(1)} %reshape.274), kind=kCustom, calls=%fused_computation | custom fusion | bytes 2048 | tf_op jit(solution)/shard_map/jit(take_along_axis)/gather | solution.py:51
  62.7 0.1 add.51
  62.8 16.9 %all-to-all-done.1 = f32[128,1,1,8,128]{4,3,2,1,0:T(8,128)S(1)} async-done(((f32[128,1,1,8,128]{4,3,2,1,0:T(8,128)}), f32[128,1,1,8,128]{4,3,2,1,0:T(8,128)S(1)}, u32[]{:S(2)}, u32[]{:S(2)}) %all-to-all-start.1) | async-done | bytes 524320 | tf_op jit(solution)/shard_map/all_to_all | solution.py:89
  79.8 0.1 reduce-precision_convert_fusion.3
  79.9 0.3 fusion.15
  80.2 0.8 slice_add_fusion.2
  (26 shorter events, 0.5 us)
Async XLA Ops:
  0.0 19.5 %copy-start = (f32[128,1024]{1,0:T(8,128)S(1)}, f32[128,1024]{1,0:T(8,128)}, u32[]{:S(2)}) copy-start(f32[128,1024]{1,0:T(8,128)} %param.8) | copy-start | bytes 1572868
  2.1 16.6 %copy-start.2 = (f32[32,16,256]{2,1,0:T(8,128)S(1)}, f32[32,16,256]{2,1,0:T(8,128)}, u32[]{:S(2)}) copy-start(f32[32,16,256]{2,1,0:T(8,128)} %param.9) | copy-start | bytes 1572868
  3.7 46.4 %all-to-all-start = ((f32[128,1,2,8,128]{4,3,2,1,0:T(8,128)}), f32[128,1,2,8,128]{4,3,2,1,0:T(8,128)S(1)}, u32[]{:S(2)}, u32[]{:S(2)}) async-start(f32[128,1,2,8,128]{4,3,2,1,0:T(8,128)} %copy.15), calls=%async_computation | async-start | bytes 2097152 | tf_op jit(solution)/shard_map/all_to_all | solution.py:69
  18.7 2.0 %collective-permute-start = (f32[32,16,256]{2,1,0:T(8,128)S(1)}, f32[32,16,256]{2,1,0:T(8,128)S(1)}, u32[]{:S(2)}, u32[]{:S(2)}) collective-permute-start(f32[32,16,256]{2,1,0:T(8,128)S(1)} %copy-done.2), channel_id=1, source_target_pairs={{0,128},{128,0},{1,129},{129,1},{2,130},{130,2},{3,131},{131,3},{4... | collective-permute-start | bytes 1572872 | tf_op jit(solution)/shard_map/ppermute | solution.py:38
  19.5 1.6 %copy-start.4 = (s32[1,64,512]{2,1,0:T(8,128)S(1)}, s32[1,64,512]{2,1,0:T(8,128)}, u32[]{:S(2)}) copy-start(s32[1,64,512]{2,1,0:T(8,128)} %param.10) | copy-start | bytes 393220
  50.7 1.6 %copy-start.1 = (f32[512,64,16]{0,2,1:T(8,128)S(1)}, f32[512,64,16]{0,2,1:T(8,128)}, u32[]{:S(2)}) copy-start(f32[512,64,16]{0,2,1:T(8,128)} %get-tuple-element.6) | copy-start | bytes 6291460
  52.3 8.7 %copy-start.3 = (s32[4,32]{1,0:T(4,128)S(1)}, s32[4,32]{1,0:T(4,128)}, u32[]{:S(2)}) copy-start(s32[4,32]{1,0:T(4,128)} %param.7) | copy-start | bytes 1540
  54.4 25.3 %all-to-all-start.1 = ((f32[128,1,1,8,128]{4,3,2,1,0:T(8,128)}), f32[128,1,1,8,128]{4,3,2,1,0:T(8,128)S(1)}, u32[]{:S(2)}, u32[]{:S(2)}) async-start(f32[128,1,1,8,128]{4,3,2,1,0:T(8,128)} %bitcast.25), calls=%async_computation.1 | async-start | bytes 1048576 | tf_op jit(solution)/shard_map/all_to_all | solution.py:89
